TPU v7x, 768 devices: a whole 4x8x12 slice. The times are simulated.
768 devices in a mesh: group: 16 (over y, core), frame: 48 (over x, z).
Axes of the slice: x: 4, y: 8, z: 12, core: 2. Of those that a mesh axis runs over, the one named last changes fastest.
Arguments:
- video: bfloat16 [48, 48, 128, 384], P('group', 'frame'), may hold values from -6 to 6
- kernel3: bfloat16 [3, 3, 3, 384, 384], replicated, may hold values from -0.0625 to 0.0625
- kernel2: bfloat16 [3, 3, 384, 384], replicated, may hold values from -0.109375 to 0.109375
Outputs:
- features: bfloat16 [48, 48, 128, 384], P('group', 'frame')
- critic: bfloat16 [48, 48, 128, 384], P('frame', None, 'group')
All inputs are finite; a program needn't handle non-finite values.
Results may differ from a plain program's by a relative error of at most 0.005.
Values may be sent and summed in bfloat16 or wider, within the bound.
No kernel may reach another device: no remote copies, remote signals or barrier semaphores. Data moves between devices by JAX's collectives and lax.ppermute only.
A program may use at most 64 MiB of HBM per device.

v0:
```python
import jax
import jax.numpy as jnp
from jax import lax
from jax.sharding import PartitionSpec as P


def shifted(value, axis, steps):
    count = lax.axis_size(axis)
    first, last = (max(0, -steps), min(count, count - steps))
    return lax.ppermute(value, axis, [(source, source + steps) for source in range(first, last)])


def extended_2(shard, sides, width):
    for axis, dim in sides:
        size, length = (lax.axis_size(axis), shard.shape[dim])
        up = [(i, (i + 1) % size) for i in range(size - 1)]
        down = [(j, i) for i, j in up]
        last = lax.slice_in_dim(shard, length - width, length, axis=dim)
        first = lax.slice_in_dim(shard, 0, width, axis=dim)
        before = lax.ppermute(last, axis, up)
        after = lax.ppermute(first, axis, down)
        shard = jnp.concatenate([before, shard, after], axis=dim)
    return shard


def planar(frames, kernel2, rows_pad, cols_pad):
    result = lax.conv_general_dilated(
        frames,
        kernel2,
        (1, 1),
        (rows_pad, cols_pad),
        dimension_numbers=("NHWC", "HWIO", "NHWC"),
        preferred_element_type=jnp.float32,
    )
    return result.astype(jnp.bfloat16)


def shards(video, kernel3, kernel2):
    length = video.shape[0]
    cached = shifted(video[length - 2 :], "group", 1)
    extended = jnp.concatenate([cached, video], 0)
    padded = extended_2(extended, (("frame", 1),), 1)
    conv = lax.conv_general_dilated(
        padded[None],
        kernel3,
        (1, 1, 1),
        ((0, 0), (0, 0), (1, 1)),
        dimension_numbers=("NDHWC", "DHWIO", "NDHWC"),
        preferred_element_type=jnp.float32,
    )[0]
    features = jax.nn.silu(conv).astype(jnp.bfloat16)
    regrouped = lax.all_to_all(
        lax.all_to_all(features, "group", split_axis=2, concat_axis=0, tiled=True),
        "frame",
        split_axis=0,
        concat_axis=1,
        tiled=True,
    )
    bordered = extended_2(regrouped, (("group", 2),), 1)
    critic = planar(bordered, kernel2, (1, 1), (0, 0))
    return (features, critic)


def solution(mesh):
    return jax.shard_map(
        shards,
        mesh=mesh,
        in_specs=(P("group", "frame", None, None), P(), P()),
        out_specs=(P("group", "frame", None, None), P("frame", None, "group", None)),
        check_vma=False,
    )
```

profile of v0, /device:TPU:1, one launch (start us, length us, event | category | flops | bytes accessed | tf_op | source)
XLA Modules:
  0.0 129.7 jit_solution(18402993253196905377)
XLA Ops:
  0.6 0.0 copy-start
  0.6 1.1 slice.9
  1.7 4.6 %collective-permute-start = (bf16[2,1,128,384]{3,2,1,0:T(8,128)(2,1)S(1)}, bf16[2,1,128,384]{3,2,1,0:T(8,128)(2,1)S(1)}, u32[]{:S(2)}, u32[]{:S(2)}) collective-permute-start(bf16[2,1,128,384]{3,2,1,0:T(8,128)(2,1)S(1)} %slice.9), channel_id=1, source_target_pairs={{0,48},{48,96},{96,144},{144,192},{192,240},{240,288},{288,336},{3... | collective-permute-start | bytes 589832 | tf_op jit(solution)/shard_map/ppermute | solution.py:10
  6.4 8.1 %collective-permute-done = bf16[2,1,128,384]{3,2,1,0:T(8,128)(2,1)S(1)} collective-permute-done((bf16[2,1,128,384]{3,2,1,0:T(8,128)(2,1)S(1)}, bf16[2,1,128,384]{3,2,1,0:T(8,128)(2,1)S(1)}, u32[]{:S(2)}, u32[]{:S(2)}) %collective-permute-start) | collective-permute-done | bytes 196640 | tf_op jit(solution)/shard_map/ppermute | solution.py:10
  14.5 1.0 constant_dynamic-update-slice_fusion
  15.5 1.3 %collective-permute-start.1 = (bf16[5,1,128,384]{3,2,1,0:T(8,128)(2,1)S(1)}, bf16[5,1,128,384]{3,2,1,0:T(8,128)(2,1)S(1)}, u32[]{:S(2)}, u32[]{:S(2)}) collective-permute-start(bf16[5,1,128,384]{3,2,1,0:T(8,128)(2,1)S(1)} %constant_dynamic-update-slice_fusion), channel_id=1, source_target_pairs={{0,1},{1,2},{2,3},{3,4},{4,5},{5,6},{6,7},{7,8},{8,9},{9,10},{10,1... | collective-permute-start | bytes 1474568 | tf_op jit(solution)/shard_map/ppermute | solution.py:20
  16.8 1.3 collective-permute-start.2
  18.1 9.4 %collective-permute-done.1 = bf16[5,1,128,384]{3,2,1,0:T(8,128)(2,1)S(1)} collective-permute-done((bf16[5,1,128,384]{3,2,1,0:T(8,128)(2,1)S(1)}, bf16[5,1,128,384]{3,2,1,0:T(8,128)(2,1)S(1)}, u32[]{:S(2)}, u32[]{:S(2)}) %collective-permute-start.1) | collective-permute-done | bytes 491552 | tf_op jit(solution)/shard_map/ppermute | solution.py:20
  27.5 3.9 %collective-permute-done.2 = bf16[5,1,128,384]{3,2,1,0:T(8,128)(2,1)S(1)} collective-permute-done((bf16[5,1,128,384]{3,2,1,0:T(8,128)(2,1)S(1)}, bf16[5,1,128,384]{3,2,1,0:T(8,128)(2,1)S(1)}, u32[]{:S(2)}, u32[]{:S(2)}) %collective-permute-start.2) | collective-permute-done | bytes 491552 | tf_op jit(solution)/shard_map/ppermute | solution.py:21
  31.4 0.2 maximum_bitcast_fusion
  31.6 1.7 %pad = bf16[5,3,1,136,384]{4,3,1,0,2:T(8,128)(2,1)} pad(bf16[5,3,1,128,384]{4,3,1,0,2:T(8,128)(2,1)S(1)} %maximum_bitcast_fusion, bf16[]{:T(256)} %constant.4), padding=0_0x0_0x0_0x1_7x0_0 | pad | bytes 3041282 | tf_op jit(solution)/shard_map/broadcast_in_dim | solution.py:44
  33.3 3.7 %reshape.49 = bf16[5,3,1,8,17,384]{5,4,3,1,0,2:T(8,128)(2,1)} reshape(bf16[5,3,1,136,384]{4,3,1,0,2:T(8,128)(2,1)} %pad) | data formatting | bytes 3133440 | tf_op jit(solution)/shard_map/conv_general_dilated | solution.py:43
  37.0 1.8 %copy.37 = bf16[5,3,1,8,17,384]{5,3,4,1,0,2:T(8,128)(2,1)S(1)} copy(bf16[5,3,1,8,17,384]{5,4,3,1,0,2:T(8,128)(2,1)} %reshape.49) | data formatting | bytes 3133440 | tf_op jit(solution)/shard_map/conv_general_dilated | solution.py:43
  38.9 9.0 %fusion.8 = f32[3,1,8,17,384]{4,2,3,1,0:T(8,128)S(1)} fusion(bf16[3,3,3,384,384]{4,3,2,1,0:T(8,128)(2,1)} %param.4, bf16[5,3,1,7,2,384]{5,3,4,1,0,2:T(8,128)(2,1)S(1)} %slice.14, bf16[5,3,1,8,17,384]{5,3,4,1,0,2:T(8,128)(2,1)S(1)} %copy.37, pred[8,17]{0,1:T(8,128)(4,1)S(1)} %copy-done.1), kind=kOutput, calls=%fused_computation.10 | convolution fusion | flops 3254160384 | bytes 10317448 | tf_op jit(solution)/shard_map/conv_general_dilated | solution.py:43
  47.8 0.6 copy.38
  48.5 2.0 %copy_bitcast_fusion.1 = bf16[128,3,1,384]{3,2,1,0:T(2,128)(2,1)} fusion(f32[3,1,1,136,384]{4,1,3,0,2:T(1,128)S(1)} %bitcast.33), kind=kLoop, calls=%fused_computation.27 | loop fusion | flops 737280 | bytes 884736
  50.5 0.5 broadcast.34
  51.1 4.2 %reduce = bf16[128,3,384]{2,1,0:T(4,128)(2,1)} reduce(bf16[128,3,1,384]{3,2,1,0:T(2,128)(2,1)} %copy_bitcast_fusion.1, bf16[]{:T(256)} %broadcast.34), dimensions={2}, to_apply=%copy_bitcast_fusion.1.reduce_sub_computation | reduce | bytes 589826
  55.3 2.0 %reshape.61 = bf16[16,2,4608]{2,1,0:T(2,128)(2,1)} reshape(bf16[128,3,384]{2,1,0:T(4,128)(2,1)} %reduce) | data formatting | bytes 589824
  57.3 17.4 %all_to_all.30 = bf16[16,2,4608]{2,1,0:T(2,128)(2,1)} all-to-all(bf16[16,2,4608]{2,1,0:T(2,128)(2,1)} %reshape.61), channel_id=1, replica_groups=mesh['group'=16,'frame'=48] {'group'}, dimensions={0} | all-to-all | bytes 589824 | tf_op jit(solution)/shard_map/all_to_all | solution.py:53
  74.7 2.9 %reshape.62 = bf16[128,3,1,384]{3,2,1,0:T(2,128)(2,1)} reshape(bf16[16,2,4608]{2,1,0:T(2,128)(2,1)} %all_to_all.30) | data formatting | bytes 589824
  77.6 1.1 copy.50
  78.8 35.0 %all_to_all.31 = bf16[48,1,8,384]{3,2,1,0:T(8,128)(2,1)S(1)} all-to-all(bf16[48,1,8,384]{3,2,1,0:T(8,128)(2,1)S(1)} %bitcast.38), channel_id=1, replica_groups=mesh['group'=16,'frame'=48] {'frame'}, dimensions={0} | all-to-all | bytes 589824 | tf_op jit(solution)/shard_map/all_to_all | solution.py:52
  113.8 0.5 copy.43
  114.3 0.2 fusion.20
  114.4 3.0 %collective-permute-start.3 = (bf16[1,48,1,384]{3,0,2,1:T(2,128)(2,1)S(1)}, bf16[1,48,1,384]{3,0,2,1:T(2,128)(2,1)S(1)}, u32[]{:S(2)}, u32[]{:S(2)}) collective-permute-start(bf16[1,48,1,384]{3,0,2,1:T(2,128)(2,1)S(1)} %get-tuple-element.12), channel_id=1, source_target_pairs={{0,48},{48,96},{96,144},{144,192},{192,240},{240,288},{288,336},{3... | collective-permute-start | bytes 110600 | tf_op jit(solution)/shard_map/ppermute | solution.py:20
  117.4 2.1 %collective-permute-start.4 = (bf16[1,48,1,384]{3,0,2,1:T(2,128)(2,1)S(1)}, bf16[1,48,1,384]{3,0,2,1:T(2,128)(2,1)S(1)}, u32[]{:S(2)}, u32[]{:S(2)}) collective-permute-start(bf16[1,48,1,384]{3,0,2,1:T(2,128)(2,1)S(1)} %get-tuple-element.13), channel_id=1, source_target_pairs={{48,0},{96,48},{144,96},{192,144},{240,192},{288,240},{336,288},{3... | collective-permute-start | bytes 110600 | tf_op jit(solution)/shard_map/ppermute | solution.py:21
  119.5 1.2 fusion.15
  120.8 0.8 copy.46
  121.5 1.6 %collective-permute-done.4 = bf16[1,48,1,384]{3,0,2,1:T(2,128)(2,1)S(1)} collective-permute-done((bf16[1,48,1,384]{3,0,2,1:T(2,128)(2,1)S(1)}, bf16[1,48,1,384]{3,0,2,1:T(2,128)(2,1)S(1)}, u32[]{:S(2)}, u32[]{:S(2)}) %collective-permute-start.4) | collective-permute-done | bytes 36896 | tf_op jit(solution)/shard_map/ppermute | solution.py:21
  123.1 5.8 %convolution_convert_fusion = bf16[1,48,8,384]{3,0,2,1:T(2,128)(2,1)S(1)} fusion(bf16[3,3,384,384]{3,2,1,0:T(8,128)(2,1)S(1)} %copy-done, bf16[1,48,1,384]{3,0,2,1:T(2,128)(2,1)S(1)} %collective-permute-done.4, bf16[1,48,8,384]{3,0,2,1:T(2,128)(2,1)S(1)} %copy.43, bf16[1,48,1,384]{3,0,2,1:T(2,128)(2,1)S(1)} %collective-permute-done.3), kind=kOutput, calls=%fused_computation.9 | convolution fusion | flops 1006313472 | bytes 3317760 | tf_op jit(solution)/shard_map/conv_general_dilated | solution.py:27
  128.9 0.8 copy.47
  (7 shorter events, 0.1 us)
Async XLA Ops:
  0.6 122.5 %copy-start = (bf16[3,3,384,384]{3,2,1,0:T(8,128)(2,1)S(1)}, bf16[3,3,384,384]{3,2,1,0:T(8,128)(2,1)}, u32[]{:S(2)}) copy-start(bf16[3,3,384,384]{3,2,1,0:T(8,128)(2,1)} %param.5) | copy-start | bytes 7962628
  1.7 12.7 %collective-permute-start = (bf16[2,1,128,384]{3,2,1,0:T(8,128)(2,1)S(1)}, bf16[2,1,128,384]{3,2,1,0:T(8,128)(2,1)S(1)}, u32[]{:S(2)}, u32[]{:S(2)}) collective-permute-start(bf16[2,1,128,384]{3,2,1,0:T(8,128)(2,1)S(1)} %slice.9), channel_id=1, source_target_pairs={{0,48},{48,96},{96,144},{144,192},{192,240},{240,288},{288,336},{3... | collective-permute-start | bytes 589832 | tf_op jit(solution)/shard_map/ppermute | solution.py:10
  15.5 12.0 %collective-permute-start.1 = (bf16[5,1,128,384]{3,2,1,0:T(8,128)(2,1)S(1)}, bf16[5,1,128,384]{3,2,1,0:T(8,128)(2,1)S(1)}, u32[]{:S(2)}, u32[]{:S(2)}) collective-permute-start(bf16[5,1,128,384]{3,2,1,0:T(8,128)(2,1)S(1)} %constant_dynamic-update-slice_fusion), channel_id=1, source_target_pairs={{0,1},{1,2},{2,3},{3,4},{4,5},{5,6},{6,7},{7,8},{8,9},{9,10},{10,1... | collective-permute-start | bytes 1474568 | tf_op jit(solution)/shard_map/ppermute | solution.py:20
  16.8 14.6 %collective-permute-start.2 = (bf16[5,1,128,384]{3,2,1,0:T(8,128)(2,1)S(1)}, bf16[5,1,128,384]{3,2,1,0:T(8,128)(2,1)S(1)}, u32[]{:S(2)}, u32[]{:S(2)}) collective-permute-start(bf16[5,1,128,384]{3,2,1,0:T(8,128)(2,1)S(1)} %constant_dynamic-update-slice_fusion), channel_id=1, source_target_pairs={{1,0},{2,1},{3,2},{4,3},{5,4},{6,5},{7,6},{8,7},{9,8},{10,9},{11,1... | collective-permute-start | bytes 1474568 | tf_op jit(solution)/shard_map/ppermute | solution.py:21
  37.0 1.9 %copy-start.1 = (pred[8,17]{0,1:T(8,128)(4,1)S(1)}, pred[8,17]{0,1:T(8,128)(4,1)}, u32[]{:S(2)}) copy-start(pred[8,17]{0,1:T(8,128)(4,1)} %constant.8) | copy-start | bytes 412
  114.4 7.1 %collective-permute-start.3 = (bf16[1,48,1,384]{3,0,2,1:T(2,128)(2,1)S(1)}, bf16[1,48,1,384]{3,0,2,1:T(2,128)(2,1)S(1)}, u32[]{:S(2)}, u32[]{:S(2)}) collective-permute-start(bf16[1,48,1,384]{3,0,2,1:T(2,128)(2,1)S(1)} %get-tuple-element.12), channel_id=1, source_target_pairs={{0,48},{48,96},{96,144},{144,192},{192,240},{240,288},{288,336},{3... | collective-permute-start | bytes 110600 | tf_op jit(solution)/shard_map/ppermute | solution.py:20
  117.4 5.7 %collective-permute-start.4 = (bf16[1,48,1,384]{3,0,2,1:T(2,128)(2,1)S(1)}, bf16[1,48,1,384]{3,0,2,1:T(2,128)(2,1)S(1)}, u32[]{:S(2)}, u32[]{:S(2)}) collective-permute-start(bf16[1,48,1,384]{3,0,2,1:T(2,128)(2,1)S(1)} %get-tuple-element.13), channel_id=1, source_target_pairs={{48,0},{96,48},{144,96},{192,144},{240,192},{288,240},{336,288},{3... | collective-permute-start | bytes 110600 | tf_op jit(solution)/shard_map/ppermute | solution.py:21
where the time goes:
time: 130 us
  blocking collectives  52.5 us (40%)
  waiting for transfers between devices  23 us (18%)
  local copies, waits for them, and re-layouts  18.7 us (14%)
  matrix products  14.8 us (11%)
  starting transfers between devices  12.3 us (9%)
  other arithmetic  7.71 us (6%)
    all_to_all x1, blocking collectives, shards(): lax.all_to_all(lax.all_to_all(features, 'group', split_axis=2, concat_axi...  35 us
    all_to_all x1, blocking collectives, shards(): lax.all_to_all(features, 'group', split_axis=2, concat_axis=0, tiled=True)  17.4 us
    ppermute x2, waiting for transfers between devices, extended_2(): before = lax.ppermute(last, axis, up)  9.37 us
    conv_general_dilated x1, matrix products, shards(): lax.conv_general_dilated(padded[None], kernel3, (1, 1, 1), ((0, 0), (0, 0...  8.95 us
    ppermute x1, waiting for transfers between devices, shifted(): lax.ppermute(value, axis, [(source, source + steps) for source in range(f...  8.13 us
    unnamed x10, local copies, waits for them, and re-layouts  6.92 us
    unnamed x2, other arithmetic  6.3 us
    conv_general_dilated x4, local copies, waits for them, and re-layouts, shards(): lax.conv_general_dilated(padded[None], kernel3, (1, 1, 1), ((0, 0), (0, 0...  6.22 us
  transfers between devices with their start and end apart: 5, of which 4 were waited for; matrix products, arithmetic and copies ran while one was open for 2% of the time, Pallas kernels for 0%

commit v1 on v0

v1 whole, which is shorter than its diff:
```python
import jax
import jax.numpy as jnp
from jax import lax
from jax.sharding import PartitionSpec as P


def shifted(value, axis, steps):
    count = lax.axis_size(axis)
    first, last = (max(0, -steps), min(count, count - steps))
    return lax.ppermute(value, axis, [(source, source + steps) for source in range(first, last)])


def diagonal(value, group_steps, frame_steps):
    groups, frames = lax.axis_size("group"), lax.axis_size("frame")
    pairs = []
    for g in range(groups):
        for f in range(frames):
            h, e = g + group_steps, f + frame_steps
            if 0 <= h < groups and 0 <= e < frames:
                pairs.append((g * frames + f, h * frames + e))
    return lax.ppermute(value, ("group", "frame"), pairs)


def conv3d(rows, kernel3):
    return lax.conv_general_dilated(
        rows[None],
        kernel3,
        (1, 1, 1),
        ((0, 0), (0, 0), (1, 1)),
        dimension_numbers=("NDHWC", "DHWIO", "NDHWC"),
        preferred_element_type=jnp.float32,
    )[0, :, 0]


def shards(video, kernel3, kernel2):
    length, _, width, channels = video.shape
    groups = lax.axis_size("group")
    cached = shifted(video[length - 2 :], "group", 1)
    above = shifted(video, "frame", 1)
    below = shifted(video, "frame", -1)
    cached_above = diagonal(video[length - 2 :], 1, 1)
    cached_below = diagonal(video[length - 2 :], 1, -1)
    rows = jnp.concatenate(
        [
            jnp.concatenate([cached_above, above], 0),
            jnp.concatenate([cached, video], 0),
            jnp.concatenate([cached_below, below], 0),
        ],
        1,
    )
    conv = conv3d(rows, kernel3)
    features = jax.nn.silu(conv).astype(jnp.bfloat16)
    block = width // groups
    padded = jnp.pad(features, ((0, 0), (1, 1), (0, 0)))
    pieces = jnp.stack([padded[:, j * block : j * block + block + 2] for j in range(groups)], 0)
    pieces = lax.all_to_all(pieces, "group", 0, 0, tiled=False)
    pieces = pieces.reshape(groups * length, block + 2, channels)
    rows_all = lax.all_to_all(pieces, "frame", 0, 0, tiled=True)
    critic = lax.conv_general_dilated(
        rows_all[None],
        kernel2,
        (1, 1),
        ((1, 1), (0, 0)),
        dimension_numbers=("NHWC", "HWIO", "NHWC"),
        preferred_element_type=jnp.float32,
    ).astype(jnp.bfloat16)
    return features[:, None], critic


def solution(mesh):
    return jax.shard_map(
        shards,
        mesh=mesh,
        in_specs=(P("group", "frame", None, None), P(), P()),
        out_specs=(P("group", "frame", None, None), P("frame", None, "group", None)),
        check_vma=False,
    )
```

time: 130 us -> 123 us (0.946)
  blocking collectives: 52.5 us -> 23.1 us
  starting transfers between devices: 12.3 us -> 38.9 us
  local copies, waits for them, and re-layouts: 18.7 us -> 12.2 us
  waiting for transfers between devices: 23 us -> 29.2 us
  other arithmetic: 7.71 us -> 2.58 us
    all_to_all x2 -> x1, blocking collectives: 52.5 us -> 23.1 us  [shards(): pieces = lax.all_to_all(pieces, 'group', 0, 0, tiled=False)]
    all_to_all x0 -> x1, waiting for transfers between devices: none -> 24.7 us  [shards(): rows_all = lax.all_to_all(pieces, 'frame', 0, 0, tiled=True)]
    all_to_all x0 -> x1, starting transfers between devices: none -> 22 us  [shards(): rows_all = lax.all_to_all(pieces, 'frame', 0, 0, tiled=True)]
    ppermute x4 -> x2, waiting for transfers between devices: 14.8 us -> 4.49 us  [diagonal(): return lax.ppermute(value, ('group', 'frame'), pairs)]
    ppermute x1 -> x3, waiting for transfers between devices: 8.13 us -> 0.01 us  [shifted(): lax.ppermute(value, axis, [(source, source + steps) for source in range(f...]
    unnamed x2 -> x0, other arithmetic: 6.3 us -> none
    ppermute x1 -> x3, starting transfers between devices: 4.59 us -> 10.4 us  [shifted(): lax.ppermute(value, axis, [(source, source + steps) for source in range(f...]
    unnamed x10 -> x21, local copies, waits for them, and re-layouts: 6.92 us -> 1.82 us
  transfers between devices with their start and end apart: 5 -> 6, of which waited for: 4 -> 2; matrix products, arithmetic and copies ran while one was open for 2% -> 2% of each run, Pallas kernels for 0% -> 0%
where the time goes in v1:
time: 123 us; the launch traced here: 122 us
  starting transfers between devices  38.9 us (32%)
  waiting for transfers between devices  29.2 us (24%)
  blocking collectives  23.1 us (19%)
  matrix products  15.6 us (13%)
  local copies, waits for them, and re-layouts  12.2 us (10%)
  other arithmetic  2.58 us (2%)
    all_to_all x1, waiting for transfers between devices, shards(): rows_all = lax.all_to_all(pieces, 'frame', 0, 0, tiled=True)  24.7 us
    all_to_all x1, blocking collectives, shards(): pieces = lax.all_to_all(pieces, 'group', 0, 0, tiled=False)  23.1 us
    all_to_all x1, starting transfers between devices, shards(): rows_all = lax.all_to_all(pieces, 'frame', 0, 0, tiled=True)  22 us
    ppermute x3, starting transfers between devices, shifted(): lax.ppermute(value, axis, [(source, source + steps) for source in range(f...  10.4 us
    conv_general_dilated x1, matrix products, conv3d(): lax.conv_general_dilated(rows[None], kernel3, (1, 1, 1), ((0, 0), (0, 0),...  9.01 us
    conv_general_dilated x5, local copies, waits for them, and re-layouts, conv3d(): lax.conv_general_dilated(rows[None], kernel3, (1, 1, 1), ((0, 0), (0, 0),...  6.63 us
    conv_general_dilated x1, matrix products, shards(): lax.conv_general_dilated(rows_all[None], kernel2, (1, 1), ((1, 1), (0, 0)...  6.59 us
    ppermute x2, starting transfers between devices, diagonal(): return lax.ppermute(value, ('group', 'frame'), pairs)  6.41 us
  transfers between devices with their start and end apart: 6, of which 2 were waited for; matrix products, arithmetic and copies ran while one was open for 2% of the time, Pallas kernels for 0%

profile of v1, /device:TPU:1, one launch (start us, length us, event | category | flops | bytes accessed | tf_op | source)
XLA Modules:
  0.0 122.4 jit_solution(12492586762718093031)
XLA Ops:
  0.6 0.0 copy-start
  0.6 5.1 %collective-permute-start.1 = (bf16[3,1,128,384]{3,2,1,0:T(8,128)(2,1)}, bf16[3,1,128,384]{3,2,1,0:T(8,128)(2,1)S(1)}, u32[]{:S(2)}, u32[]{:S(2)}) collective-permute-start(bf16[3,1,128,384]{3,2,1,0:T(8,128)(2,1)} %param.3), channel_id=1, source_target_pairs={{0,1},{1,2},{2,3},{3,4},{4,5},{5,6},{6,7},{7,8},{8,9},{9,10},{10,1... | collective-permute-start | bytes 884744 | tf_op jit(solution)/shard_map/ppermute | solution.py:10
  5.8 1.3 %collective-permute-start.4 = (bf16[3,1,128,384]{3,2,1,0:T(8,128)(2,1)}, bf16[3,1,128,384]{3,2,1,0:T(8,128)(2,1)S(1)}, u32[]{:S(2)}, u32[]{:S(2)}) collective-permute-start(bf16[3,1,128,384]{3,2,1,0:T(8,128)(2,1)} %param.3), channel_id=1, source_target_pairs={{1,0},{2,1},{3,2},{4,3},{5,4},{6,5},{7,6},{8,7},{9,8},{10,9},{11,1... | collective-permute-start | bytes 884744 | tf_op jit(solution)/shard_map/ppermute | solution.py:10
  7.1 1.0 slice.67
  8.0 1.3 %collective-permute-start.3 = (bf16[2,1,128,384]{3,2,1,0:T(8,128)(2,1)S(1)}, bf16[2,1,128,384]{3,2,1,0:T(8,128)(2,1)S(1)}, u32[]{:S(2)}, u32[]{:S(2)}) collective-permute-start(bf16[2,1,128,384]{3,2,1,0:T(8,128)(2,1)S(1)} %slice.67), channel_id=1, source_target_pairs={{1,48},{2,49},{3,50},{4,51},{5,52},{6,53},{7,54},{8,55},{9,56},{10... | collective-permute-start | bytes 589832 | tf_op jit(solution)/shard_map/ppermute | solution.py:21
  9.3 4.0 %collective-permute-start.2 = (bf16[2,1,128,384]{3,2,1,0:T(8,128)(2,1)S(1)}, bf16[2,1,128,384]{3,2,1,0:T(8,128)(2,1)S(1)}, u32[]{:S(2)}, u32[]{:S(2)}) collective-permute-start(bf16[2,1,128,384]{3,2,1,0:T(8,128)(2,1)S(1)} %slice.67), channel_id=1, source_target_pairs={{0,48},{48,96},{96,144},{144,192},{192,240},{240,288},{288,336},{3... | collective-permute-start | bytes 589832 | tf_op jit(solution)/shard_map/ppermute | solution.py:10
  13.4 5.1 %collective-permute-start = (bf16[2,1,128,384]{3,2,1,0:T(8,128)(2,1)S(1)}, bf16[2,1,128,384]{3,2,1,0:T(8,128)(2,1)S(1)}, u32[]{:S(2)}, u32[]{:S(2)}) collective-permute-start(bf16[2,1,128,384]{3,2,1,0:T(8,128)(2,1)S(1)} %slice.67), channel_id=1, source_target_pairs={{0,49},{1,50},{2,51},{3,52},{4,53},{5,54},{6,55},{7,56},{8,57},{9,... | collective-permute-start | bytes 589832 | tf_op jit(solution)/shard_map/ppermute | solution.py:21
  18.5 4.5 %collective-permute-done.3 = bf16[2,1,128,384]{3,2,1,0:T(8,128)(2,1)S(1)} collective-permute-done((bf16[2,1,128,384]{3,2,1,0:T(8,128)(2,1)S(1)}, bf16[2,1,128,384]{3,2,1,0:T(8,128)(2,1)S(1)}, u32[]{:S(2)}, u32[]{:S(2)}) %collective-permute-start.3) | collective-permute-done | bytes 196640 | tf_op jit(solution)/shard_map/ppermute | solution.py:21
  23.0 0.0 collective-permute-done.2
  23.0 0.0 collective-permute-done
  23.0 0.0 collective-permute-done.1
  23.0 0.0 collective-permute-done.4
  23.0 1.2 maximum_bitcast_fusion
  24.2 1.7 %pad.5 = bf16[5,3,1,136,384]{4,3,1,0,2:T(8,128)(2,1)} pad(bf16[5,3,1,128,384]{4,3,1,0,2:T(8,128)(2,1)S(1)} %maximum_bitcast_fusion, bf16[]{:T(256)} %constant.5.clone.1), padding=0_0x0_0x0_0x1_7x0_0 | pad | bytes 3041282 | tf_op jit(solution)/shard_map/broadcast_in_dim | solution.py:26
  25.9 3.7 %reshape.41 = bf16[5,3,1,8,17,384]{5,4,3,1,0,2:T(8,128)(2,1)} reshape(bf16[5,3,1,136,384]{4,3,1,0,2:T(8,128)(2,1)} %pad.5) | data formatting | bytes 3133440 | tf_op jit(solution)/shard_map/conv_general_dilated | solution.py:25
  29.6 0.0 copy-start.1
  29.6 1.8 %copy.22 = bf16[5,3,1,8,17,384]{5,3,4,1,0,2:T(8,128)(2,1)S(1)} copy(bf16[5,3,1,8,17,384]{5,4,3,1,0,2:T(8,128)(2,1)} %reshape.41) | data formatting | bytes 3133440 | tf_op jit(solution)/shard_map/conv_general_dilated | solution.py:25
  31.5 0.0 copy-done.1
  31.5 9.0 %fusion.8 = f32[3,1,8,17,384]{4,2,3,1,0:T(8,128)S(1)} fusion(bf16[3,3,3,384,384]{4,3,2,1,0:T(8,128)(2,1)} %param.4, bf16[5,3,1,7,2,384]{5,3,4,1,0,2:T(8,128)(2,1)S(1)} %slice.86, bf16[5,3,1,8,17,384]{5,3,4,1,0,2:T(8,128)(2,1)S(1)} %copy.22, pred[8,17]{0,1:T(8,128)(4,1)S(1)} %copy-done.1), kind=kOutput, calls=%fused_computation.10 | convolution fusion | flops 3254160384 | bytes 10317448 | tf_op jit(solution)/shard_map/conv_general_dilated | solution.py:25
  40.5 0.6 copy.23
  41.1 0.4 slice.87
  41.6 0.2 fusion.19
  42.1 0.2 copy.24
  42.3 23.1 %all_to_all.10 = bf16[16,3,10,384]{3,1,2,0:T(4,128)(2,1)S(1)} all-to-all(bf16[16,3,10,384]{3,1,2,0:T(4,128)(2,1)S(1)} %copy.24), channel_id=1, replica_groups=mesh['group'=16,'frame'=48] {'group'}, dimensions={0} | all-to-all | bytes 737280 | tf_op jit(solution)/shard_map/all_to_all | solution.py:56
  65.4 0.9 copy.31
  66.3 22.0 %all-to-all-start.1 = ((bf16[48,10,384]{2,1,0:T(8,128)(2,1)}), bf16[48,10,384]{2,1,0:T(8,128)(2,1)}, u32[]{:S(2)}, u32[]{:S(2)}) async-start(bf16[48,10,384]{2,1,0:T(8,128)(2,1)} %bitcast.106), calls=%async_computation.1 | async-start | bytes 1179648 | tf_op jit(solution)/shard_map/all_to_all | solution.py:58
  88.3 1.2 %fusion.18 = bf16[3,1,128,384]{3,1,2,0:T(2,128)(2,1)S(1)} fusion(f32[3,1,1,136,384]{4,1,3,0,2:T(1,128)S(1)} %bitcast.105), kind=kLoop, calls=%fused_computation.22 | loop fusion | flops 737280 | bytes 884736 | tf_op jit(solution)/shard_map/convert_element_type | solution.py:52
  89.6 0.8 copy.29
  90.3 24.7 %all-to-all-done.1 = bf16[48,10,384]{2,1,0:T(8,128)(2,1)} async-done(((bf16[48,10,384]{2,1,0:T(8,128)(2,1)}), bf16[48,10,384]{2,1,0:T(8,128)(2,1)}, u32[]{:S(2)}, u32[]{:S(2)}) %all-to-all-start.1) | async-done | bytes 368672 | tf_op jit(solution)/shard_map/all_to_all | solution.py:58
  115.0 0.0 copy-done
  115.0 6.6 %convolution_convert_fusion = bf16[1,48,8,384]{3,0,2,1:T(2,128)(2,1)S(1)} fusion(bf16[3,3,384,384]{3,2,1,0:T(8,128)(2,1)S(1)} %copy-done, bf16[1,48,10,384]{3,2,1,0:T(8,128)(2,1)} %bitcast.21), kind=kOutput, calls=%fused_computation.9 | convolution fusion | flops 1005207552 | bytes 3317760 | tf_op jit(solution)/shard_map/conv_general_dilated | solution.py:59
  121.6 0.8 copy.30
  (17 shorter events, 0.4 us)
Async XLA Ops:
  0.6 114.4 %copy-start = (bf16[3,3,384,384]{3,2,1,0:T(8,128)(2,1)S(1)}, bf16[3,3,384,384]{3,2,1,0:T(8,128)(2,1)}, u32[]{:S(2)}) copy-start(bf16[3,3,384,384]{3,2,1,0:T(8,128)(2,1)} %param.5) | copy-start | bytes 7962628
  0.6 22.4 %collective-permute-start.1 = (bf16[3,1,128,384]{3,2,1,0:T(8,128)(2,1)}, bf16[3,1,128,384]{3,2,1,0:T(8,128)(2,1)S(1)}, u32[]{:S(2)}, u32[]{:S(2)}) collective-permute-start(bf16[3,1,128,384]{3,2,1,0:T(8,128)(2,1)} %param.3), channel_id=1, source_target_pairs={{0,1},{1,2},{2,3},{3,4},{4,5},{5,6},{6,7},{7,8},{8,9},{9,10},{10,1... | collective-permute-start | bytes 884744 | tf_op jit(solution)/shard_map/ppermute | solution.py:10
  5.8 17.2 %collective-permute-start.4 = (bf16[3,1,128,384]{3,2,1,0:T(8,128)(2,1)}, bf16[3,1,128,384]{3,2,1,0:T(8,128)(2,1)S(1)}, u32[]{:S(2)}, u32[]{:S(2)}) collective-permute-start(bf16[3,1,128,384]{3,2,1,0:T(8,128)(2,1)} %param.3), channel_id=1, source_target_pairs={{1,0},{2,1},{3,2},{4,3},{5,4},{6,5},{7,6},{8,7},{9,8},{10,9},{11,1... | collective-permute-start | bytes 884744 | tf_op jit(solution)/shard_map/ppermute | solution.py:10
  8.0 15.0 %collective-permute-start.3 = (bf16[2,1,128,384]{3,2,1,0:T(8,128)(2,1)S(1)}, bf16[2,1,128,384]{3,2,1,0:T(8,128)(2,1)S(1)}, u32[]{:S(2)}, u32[]{:S(2)}) collective-permute-start(bf16[2,1,128,384]{3,2,1,0:T(8,128)(2,1)S(1)} %slice.67), channel_id=1, source_target_pairs={{1,48},{2,49},{3,50},{4,51},{5,52},{6,53},{7,54},{8,55},{9,56},{10... | collective-permute-start | bytes 589832 | tf_op jit(solution)/shard_map/ppermute | solution.py:21
  9.3 13.7 %collective-permute-start.2 = (bf16[2,1,128,384]{3,2,1,0:T(8,128)(2,1)S(1)}, bf16[2,1,128,384]{3,2,1,0:T(8,128)(2,1)S(1)}, u32[]{:S(2)}, u32[]{:S(2)}) collective-permute-start(bf16[2,1,128,384]{3,2,1,0:T(8,128)(2,1)S(1)} %slice.67), channel_id=1, source_target_pairs={{0,48},{48,96},{96,144},{144,192},{192,240},{240,288},{288,336},{3... | collective-permute-start | bytes 589832 | tf_op jit(solution)/shard_map/ppermute | solution.py:10
  13.4 9.6 %collective-permute-start = (bf16[2,1,128,384]{3,2,1,0:T(8,128)(2,1)S(1)}, bf16[2,1,128,384]{3,2,1,0:T(8,128)(2,1)S(1)}, u32[]{:S(2)}, u32[]{:S(2)}) collective-permute-start(bf16[2,1,128,384]{3,2,1,0:T(8,128)(2,1)S(1)} %slice.67), channel_id=1, source_target_pairs={{0,49},{1,50},{2,51},{3,52},{4,53},{5,54},{6,55},{7,56},{8,57},{9,... | collective-permute-start | bytes 589832 | tf_op jit(solution)/shard_map/ppermute | solution.py:21
  29.6 1.9 %copy-start.1 = (pred[8,17]{0,1:T(8,128)(4,1)S(1)}, pred[8,17]{0,1:T(8,128)(4,1)}, u32[]{:S(2)}) copy-start(pred[8,17]{0,1:T(8,128)(4,1)} %constant.13) | copy-start | bytes 412
  66.3 48.7 %all-to-all-start.1 = ((bf16[48,10,384]{2,1,0:T(8,128)(2,1)}), bf16[48,10,384]{2,1,0:T(8,128)(2,1)}, u32[]{:S(2)}, u32[]{:S(2)}) async-start(bf16[48,10,384]{2,1,0:T(8,128)(2,1)} %bitcast.106), calls=%async_computation.1 | async-start | bytes 1179648 | tf_op jit(solution)/shard_map/all_to_all | solution.py:58

commit v2 on v1

--- a/solution.py
+++ b/solution.py
@@ -1,6 +1,7 @@
 import jax
 import jax.numpy as jnp
 from jax import lax
+from jax.experimental import pallas as pl
 from jax.sharding import PartitionSpec as P
 
 
@@ -21,15 +22,38 @@
     return lax.ppermute(value, ("group", "frame"), pairs)
 
 
+def conv3d_kernel(rows_ref, kernel_ref, acc_ref):
+    step = pl.program_id(0)
+    frames, width, channels = acc_ref.shape[1:]
+
+    @pl.when(step == 0)
+    def _():
+        acc_ref[...] = jnp.zeros_like(acc_ref)
+
+    lhs = rows_ref[pl.ds(step // 3, frames), step % 3].reshape(frames * width, channels)
+    for c in range(3):
+        part = jnp.dot(lhs, kernel_ref[0, c], preferred_element_type=jnp.float32)
+        acc_ref[c] += part.reshape(frames, width, channels)
+
+
 def conv3d(rows, kernel3):
-    return lax.conv_general_dilated(
-        rows[None],
-        kernel3,
-        (1, 1, 1),
-        ((0, 0), (0, 0), (1, 1)),
-        dimension_numbers=("NDHWC", "DHWIO", "NDHWC"),
-        preferred_element_type=jnp.float32,
-    )[0, :, 0]
+    frames, _, width, channels = rows.shape
+    count = frames - 2
+    taps = kernel3.reshape(9, 3, channels, channels)
+    acc = pl.pallas_call(
+        conv3d_kernel,
+        grid=(9,),
+        in_specs=[
+            pl.BlockSpec(rows.shape, lambda s: (0, 0, 0, 0)),
+            pl.BlockSpec((1, 3, channels, channels), lambda s: (s, 0, 0, 0)),
+        ],
+        out_specs=pl.BlockSpec((3, count, width, channels), lambda s: (0, 0, 0, 0)),
+        out_shape=jax.ShapeDtypeStruct((3, count, width, channels), jnp.float32),
+    )(rows, taps)
+    zero = jnp.zeros((count, 1, channels), jnp.float32)
+    left = jnp.concatenate([zero, acc[0, :, :-1]], axis=1)
+    right = jnp.concatenate([acc[2, :, 1:], zero], axis=1)
+    return left + acc[1] + right
 
 
 def shards(video, kernel3, kernel2):

time: 123 us -> 118 us (0.959)
  blocking collectives: 23.1 us -> 71.5 us
  waiting for transfers between devices: 29.2 us -> 4.5 us
  starting transfers between devices: 38.9 us -> 16.9 us
  Pallas kernels: 0 us -> 11.3 us
  matrix products: 15.6 us -> 5.54 us
  local copies, waits for them, and re-layouts: 12.2 us -> 3.64 us
    all_to_all x0 -> x1, blocking collectives: none -> 48.4 us  [shards(): rows_all = lax.all_to_all(pieces, 'frame', 0, 0, tiled=True)]
    all_to_all x1 -> x0, waiting for transfers between devices: 24.7 us -> none  [shards(): rows_all = lax.all_to_all(pieces, 'frame', 0, 0, tiled=True)]
    all_to_all x1 -> x0, starting transfers between devices: 22 us -> none  [shards(): rows_all = lax.all_to_all(pieces, 'frame', 0, 0, tiled=True)]
    pallas_call x0 -> x1, Pallas kernels: none -> 11.3 us  [conv3d(): pl.pallas_call(conv3d_kernel, grid=(9,), in_specs=[pl.BlockSpec(rows.shap...]
    conv_general_dilated x1 -> x0, matrix products: 9.01 us -> none  [conv3d(): lax.conv_general_dilated(rows[None], kernel3, (1, 1, 1), ((0, 0), (0, 0),...]
    conv_general_dilated x5 -> x0, local copies, waits for them, and re-layouts: 6.63 us -> none  [conv3d(): lax.conv_general_dilated(rows[None], kernel3, (1, 1, 1), ((0, 0), (0, 0),...]
    concatenate x0 -> x1, other arithmetic: none -> 2.3 us  [shards(): jnp.concatenate([jnp.concatenate([cached_above, above], 0), jnp.concatena...]
    broadcast_in_dim x1 -> x0, local copies, waits for them, and re-layouts: 1.67 us -> none  [conv3d(): rows[None]]
  transfers between devices with their start and end apart: 6 -> 5, of which waited for: 2 -> 1; matrix products, arithmetic and copies ran while one was open for 2% -> 1% of each run, Pallas kernels for 0% -> 0%
where the time goes in v2:
time: 118 us
  blocking collectives  71.5 us (61%)
  starting transfers between devices  16.9 us (14%)
  Pallas kernels  11.3 us (10%)
  matrix products  5.54 us (5%)
  waiting for transfers between devices  4.5 us (4%)
  local copies, waits for them, and re-layouts  3.64 us (3%)
  other arithmetic  3.57 us (3%)
    all_to_all x1, blocking collectives, shards(): rows_all = lax.all_to_all(pieces, 'frame', 0, 0, tiled=True)  48.4 us
    all_to_all x1, blocking collectives, shards(): pieces = lax.all_to_all(pieces, 'group', 0, 0, tiled=False)  23.1 us
    pallas_call x1, Pallas kernels, conv3d(): pl.pallas_call(conv3d_kernel, grid=(9,), in_specs=[pl.BlockSpec(rows.shap...  11.3 us
    ppermute x3, starting transfers between devices, shifted(): lax.ppermute(value, axis, [(source, source + steps) for source in range(f...  10.4 us
    ppermute x2, starting transfers between devices, diagonal(): return lax.ppermute(value, ('group', 'frame'), pairs)  6.41 us
    conv_general_dilated x1, matrix products, shards(): lax.conv_general_dilated(rows_all[None], kernel2, (1, 1), ((1, 1), (0, 0)...  5.54 us
    ppermute x2, waiting for transfers between devices, diagonal(): return lax.ppermute(value, ('group', 'frame'), pairs)  4.49 us
  transfers between devices with their start and end apart: 5, of which 1 were waited for; matrix products, arithmetic and copies ran while one was open for 1% of the time, Pallas kernels for 0%

profile of v2, /device:TPU:1, one launch (start us, length us, event | category | flops | bytes accessed | tf_op | source)
XLA Modules:
  0.0 117.7 jit_solution(2107468074176853764)
XLA Ops:
  0.6 0.0 copy-start
  0.6 5.1 %collective-permute-start.1 = (bf16[3,1,128,384]{3,2,1,0:T(8,128)(2,1)}, bf16[3,1,128,384]{3,2,1,0:T(8,128)(2,1)S(1)}, u32[]{:S(2)}, u32[]{:S(2)}) collective-permute-start(bf16[3,1,128,384]{3,2,1,0:T(8,128)(2,1)} %param.3), channel_id=1, source_target_pairs={{0,1},{1,2},{2,3},{3,4},{4,5},{5,6},{6,7},{7,8},{8,9},{9,10},{10,1... | collective-permute-start | bytes 884744 | tf_op jit(solution)/shard_map/ppermute | solution.py:11
  5.8 1.3 %collective-permute-start.4 = (bf16[3,1,128,384]{3,2,1,0:T(8,128)(2,1)}, bf16[3,1,128,384]{3,2,1,0:T(8,128)(2,1)S(1)}, u32[]{:S(2)}, u32[]{:S(2)}) collective-permute-start(bf16[3,1,128,384]{3,2,1,0:T(8,128)(2,1)} %param.3), channel_id=1, source_target_pairs={{1,0},{2,1},{3,2},{4,3},{5,4},{6,5},{7,6},{8,7},{9,8},{10,9},{11,1... | collective-permute-start | bytes 884744 | tf_op jit(solution)/shard_map/ppermute | solution.py:11
  7.1 1.0 slice.76
  8.0 1.3 %collective-permute-start.3 = (bf16[2,1,128,384]{3,2,1,0:T(8,128)(2,1)S(1)}, bf16[2,1,128,384]{3,2,1,0:T(8,128)(2,1)S(1)}, u32[]{:S(2)}, u32[]{:S(2)}) collective-permute-start(bf16[2,1,128,384]{3,2,1,0:T(8,128)(2,1)S(1)} %slice.76), channel_id=1, source_target_pairs={{1,48},{2,49},{3,50},{4,51},{5,52},{6,53},{7,54},{8,55},{9,56},{10... | collective-permute-start | bytes 589832 | tf_op jit(solution)/shard_map/ppermute | solution.py:22
  9.3 4.0 %collective-permute-start.2 = (bf16[2,1,128,384]{3,2,1,0:T(8,128)(2,1)S(1)}, bf16[2,1,128,384]{3,2,1,0:T(8,128)(2,1)S(1)}, u32[]{:S(2)}, u32[]{:S(2)}) collective-permute-start(bf16[2,1,128,384]{3,2,1,0:T(8,128)(2,1)S(1)} %slice.76), channel_id=1, source_target_pairs={{0,48},{48,96},{96,144},{144,192},{192,240},{240,288},{288,336},{3... | collective-permute-start | bytes 589832 | tf_op jit(solution)/shard_map/ppermute | solution.py:11
  13.4 5.1 %collective-permute-start = (bf16[2,1,128,384]{3,2,1,0:T(8,128)(2,1)S(1)}, bf16[2,1,128,384]{3,2,1,0:T(8,128)(2,1)S(1)}, u32[]{:S(2)}, u32[]{:S(2)}) collective-permute-start(bf16[2,1,128,384]{3,2,1,0:T(8,128)(2,1)S(1)} %slice.76), channel_id=1, source_target_pairs={{0,49},{1,50},{2,51},{3,52},{4,53},{5,54},{6,55},{7,56},{8,57},{9,... | collective-permute-start | bytes 589832 | tf_op jit(solution)/shard_map/ppermute | solution.py:22
  18.5 4.5 %collective-permute-done.3 = bf16[2,1,128,384]{3,2,1,0:T(8,128)(2,1)S(1)} collective-permute-done((bf16[2,1,128,384]{3,2,1,0:T(8,128)(2,1)S(1)}, bf16[2,1,128,384]{3,2,1,0:T(8,128)(2,1)S(1)}, u32[]{:S(2)}, u32[]{:S(2)}) %collective-permute-start.3) | collective-permute-done | bytes 196640 | tf_op jit(solution)/shard_map/ppermute | solution.py:22
  23.0 0.0 collective-permute-done.2
  23.0 0.0 collective-permute-done
  23.0 0.0 collective-permute-done.1
  23.0 0.0 collective-permute-done.4
  23.0 2.3 %maximum_maximum_fusion.rows_ref = bf16[5,3,128,384]{3,2,1,0:T(8,128)(2,1)} fusion(bf16[3,1,128,384]{3,2,1,0:T(8,128)(2,1)S(1)} %collective-permute-done.4, bf16[2,1,128,384]{3,2,1,0:T(8,128)(2,1)S(1)} %collective-permute-done.3, bf16[3,1,128,384]{3,2,1,0:T(8,128)(2,1)} %param.3, bf16[2,1,128,384]{3,2,1,0:T(8,128)(2,1)S(1)} %collective-permute-done.2, ...), kind=kLoop, calls=%fused_computation | loop fusion | flops 3686400 | bytes 2949120 | tf_op jit(solution)/shard_map/concatenate | solution.py:67
  25.3 11.3 %shard_map.50 = f32[3,3,128,384]{3,2,1,0:T(8,128)} custom-call(bf16[5,3,128,384]{3,2,1,0:T(8,128)(2,1)} %maximum_maximum_fusion.rows_ref, bf16[9,3,384,384]{3,2,1,0:T(8,128)(2,1)} %bitcast.83), custom_call_target="tpu_custom_call" | custom-call | tf_op jit(solution)/shard_map/pallas_call | solution.py:43
  36.6 1.3 %slice_bitcast_fusion.2 = (f32[3,127,384]{2,1,0:T(8,128)S(1)}, f32[3,127,384]{2,1,0:T(8,128)S(1)}) fusion(f32[3,3,128,384]{3,2,1,0:T(8,128)} %shard_map.50), kind=kLoop, calls=%fused_computation.7 | loop fusion | bytes 2340864 | tf_op jit(solution)/shard_map/squeeze | solution.py:54
  37.9 1.3 %multiply_convert_fusion = bf16[3,128,384]{2,1,0:T(8,128)(2,1)S(1)} fusion(f32[3,3,128,384]{3,2,1,0:T(8,128)} %shard_map.50, f32[3,127,384]{2,1,0:T(8,128)S(1)} %get-tuple-element.11, f32[3,127,384]{2,1,0:T(8,128)S(1)} %get-tuple-element.10), kind=kLoop, calls=%fused_computation.8 | loop fusion | flops 1032192 | bytes 2055168 | tf_op jit(solution)/shard_map/convert_element_type | solution.py:76
  39.2 0.0 copy-start.1
  39.6 0.2 copy.16
  39.8 23.1 %all_to_all.10 = bf16[16,3,10,384]{3,1,2,0:T(4,128)(2,1)S(1)} all-to-all(bf16[16,3,10,384]{3,1,2,0:T(4,128)(2,1)S(1)} %copy.16), channel_id=1, replica_groups=mesh['group'=16,'frame'=48] {'group'}, dimensions={0} | all-to-all | bytes 737280 | tf_op jit(solution)/shard_map/all_to_all | solution.py:80
  62.9 0.0 copy-done.1
  62.9 0.1 copy.23
  63.0 48.4 %all_to_all.11 = bf16[48,10,384]{2,1,0:T(8,128)(2,1)S(1)} all-to-all(bf16[48,10,384]{2,1,0:T(8,128)(2,1)S(1)} %bitcast.85), channel_id=1, replica_groups=mesh['group'=16,'frame'=48] {'frame'}, dimensions={0} | all-to-all | bytes 737280 | tf_op jit(solution)/shard_map/all_to_all | solution.py:82
  111.3 0.0 copy-done
  111.4 5.5 %convolution_convert_fusion = bf16[1,48,8,384]{3,0,2,1:T(2,128)(2,1)S(1)} fusion(bf16[3,3,384,384]{3,2,1,0:T(8,128)(2,1)S(1)} %copy-done, bf16[1,48,10,384]{3,2,1,0:T(8,128)(2,1)S(1)} %bitcast.86), kind=kOutput, calls=%fused_computation.1 | convolution fusion | flops 1005207552 | bytes 3317760 | tf_op jit(solution)/shard_map/conv_general_dilated | solution.py:83
  116.9 0.8 copy.22
  (16 shorter events, 0.3 us)
Async XLA Ops:
  0.6 110.7 %copy-start = (bf16[3,3,384,384]{3,2,1,0:T(8,128)(2,1)S(1)}, bf16[3,3,384,384]{3,2,1,0:T(8,128)(2,1)}, u32[]{:S(2)}) copy-start(bf16[3,3,384,384]{3,2,1,0:T(8,128)(2,1)} %param.5) | copy-start | bytes 7962628
  0.6 22.4 %collective-permute-start.1 = (bf16[3,1,128,384]{3,2,1,0:T(8,128)(2,1)}, bf16[3,1,128,384]{3,2,1,0:T(8,128)(2,1)S(1)}, u32[]{:S(2)}, u32[]{:S(2)}) collective-permute-start(bf16[3,1,128,384]{3,2,1,0:T(8,128)(2,1)} %param.3), channel_id=1, source_target_pairs={{0,1},{1,2},{2,3},{3,4},{4,5},{5,6},{6,7},{7,8},{8,9},{9,10},{10,1... | collective-permute-start | bytes 884744 | tf_op jit(solution)/shard_map/ppermute | solution.py:11
  5.8 17.2 %collective-permute-start.4 = (bf16[3,1,128,384]{3,2,1,0:T(8,128)(2,1)}, bf16[3,1,128,384]{3,2,1,0:T(8,128)(2,1)S(1)}, u32[]{:S(2)}, u32[]{:S(2)}) collective-permute-start(bf16[3,1,128,384]{3,2,1,0:T(8,128)(2,1)} %param.3), channel_id=1, source_target_pairs={{1,0},{2,1},{3,2},{4,3},{5,4},{6,5},{7,6},{8,7},{9,8},{10,9},{11,1... | collective-permute-start | bytes 884744 | tf_op jit(solution)/shard_map/ppermute | solution.py:11
  8.0 15.0 %collective-permute-start.3 = (bf16[2,1,128,384]{3,2,1,0:T(8,128)(2,1)S(1)}, bf16[2,1,128,384]{3,2,1,0:T(8,128)(2,1)S(1)}, u32[]{:S(2)}, u32[]{:S(2)}) collective-permute-start(bf16[2,1,128,384]{3,2,1,0:T(8,128)(2,1)S(1)} %slice.76), channel_id=1, source_target_pairs={{1,48},{2,49},{3,50},{4,51},{5,52},{6,53},{7,54},{8,55},{9,56},{10... | collective-permute-start | bytes 589832 | tf_op jit(solution)/shard_map/ppermute | solution.py:22
  9.3 13.7 %collective-permute-start.2 = (bf16[2,1,128,384]{3,2,1,0:T(8,128)(2,1)S(1)}, bf16[2,1,128,384]{3,2,1,0:T(8,128)(2,1)S(1)}, u32[]{:S(2)}, u32[]{:S(2)}) collective-permute-start(bf16[2,1,128,384]{3,2,1,0:T(8,128)(2,1)S(1)} %slice.76), channel_id=1, source_target_pairs={{0,48},{48,96},{96,144},{144,192},{192,240},{240,288},{288,336},{3... | collective-permute-start | bytes 589832 | tf_op jit(solution)/shard_map/ppermute | solution.py:11
  13.4 9.6 %collective-permute-start = (bf16[2,1,128,384]{3,2,1,0:T(8,128)(2,1)S(1)}, bf16[2,1,128,384]{3,2,1,0:T(8,128)(2,1)S(1)}, u32[]{:S(2)}, u32[]{:S(2)}) collective-permute-start(bf16[2,1,128,384]{3,2,1,0:T(8,128)(2,1)S(1)} %slice.76), channel_id=1, source_target_pairs={{0,49},{1,50},{2,51},{3,52},{4,53},{5,54},{6,55},{7,56},{8,57},{9,... | collective-permute-start | bytes 589832 | tf_op jit(solution)/shard_map/ppermute | solution.py:22
  39.2 23.7 %copy-start.1 = (bf16[3,128,384]{2,1,0:T(8,128)(2,1)}, bf16[3,128,384]{2,1,0:T(8,128)(2,1)S(1)}, u32[]{:S(2)}) copy-start(bf16[3,128,384]{2,1,0:T(8,128)(2,1)S(1)} %multiply_convert_fusion) | copy-start | bytes 884740

commit v3 on v2

v3 whole, which is shorter than its diff:
```python
import jax
import jax.numpy as jnp
from jax import lax
from jax.experimental import pallas as pl
from jax.sharding import PartitionSpec as P


def shifted(value, axis, steps):
    count = lax.axis_size(axis)
    first, last = (max(0, -steps), min(count, count - steps))
    return lax.ppermute(value, axis, [(source, source + steps) for source in range(first, last)])


def diagonal(value, group_steps, frame_steps):
    groups, frames = lax.axis_size("group"), lax.axis_size("frame")
    pairs = []
    for g in range(groups):
        for f in range(frames):
            h, e = g + group_steps, f + frame_steps
            if 0 <= h < groups and 0 <= e < frames:
                pairs.append((g * frames + f, h * frames + e))
    return lax.ppermute(value, ("group", "frame"), pairs)


def conv3d_kernel(rows_ref, kernel_ref, *refs):
    acc_ref = refs[-1]
    step = pl.program_id(0)
    pairs = rows_ref.shape[1]
    frames, width, channels = acc_ref.shape[1:]

    if len(refs) == 1:

        @pl.when(step == 0)
        def _():
            acc_ref[...] = jnp.zeros_like(acc_ref)

    else:

        @pl.when(step == 0)
        def _():
            acc_ref[...] = refs[0][...]

    lhs = rows_ref[pl.ds(step // pairs, frames), step % pairs].reshape(frames * width, channels)
    for c in range(3):
        part = jnp.dot(lhs, kernel_ref[0, 0, c], preferred_element_type=jnp.float32)
        acc_ref[c] += part.reshape(frames, width, channels)


def conv3d_taps(rows, kernel3, row_taps, acc=None):
    frames, pairs, width, channels = rows.shape
    count = frames - 2
    if pairs == 1:
        index = lambda s: (s, row_taps[0], 0, 0, 0)
    else:
        index = lambda s: (s // 2, row_taps[0] + (row_taps[1] - row_taps[0]) * (s % 2), 0, 0, 0)
    acc_spec = pl.BlockSpec((3, count, width, channels), lambda s: (0, 0, 0, 0))
    operands = [rows, kernel3] + ([] if acc is None else [acc])
    return pl.pallas_call(
        conv3d_kernel,
        grid=(3 * pairs,),
        in_specs=[
            pl.BlockSpec(rows.shape, lambda s: (0, 0, 0, 0)),
            pl.BlockSpec((1, 1, 3, channels, channels), index),
        ]
        + ([] if acc is None else [acc_spec]),
        out_specs=acc_spec,
        out_shape=jax.ShapeDtypeStruct((3, count, width, channels), jnp.float32),
        input_output_aliases={} if acc is None else {2: 0},
    )(*operands)


def column_sum(acc):
    count, _, channels = acc.shape[1:]
    zero = jnp.zeros((count, 1, channels), jnp.float32)
    left = jnp.concatenate([zero, acc[0, :, :-1]], axis=1)
    right = jnp.concatenate([acc[2, :, 1:], zero], axis=1)
    return left + acc[1] + right


def critic_kernel(cols_ref, kernel_ref, out_ref):
    width = out_ref.shape[1]
    rows, channels = cols_ref.shape[1:]
    total = None
    for c in range(3):
        lhs = cols_ref[c : c + width].reshape(width * rows, channels)
        part = jnp.dot(lhs, kernel_ref[0, c], preferred_element_type=jnp.float32)
        total = part if total is None else total + part
    out_ref[0] = total.reshape(width, rows, channels)


def critic_conv(cols, kernel2):
    span, rows, channels = cols.shape
    width = span - 2
    acc = pl.pallas_call(
        critic_kernel,
        grid=(3,),
        in_specs=[
            pl.BlockSpec(cols.shape, lambda s: (0, 0, 0)),
            pl.BlockSpec((1, 3, channels, channels), lambda s: (s, 0, 0, 0)),
        ],
        out_specs=pl.BlockSpec((1, width, rows, channels), lambda s: (s, 0, 0, 0)),
        out_shape=jax.ShapeDtypeStruct((3, width, rows, channels), jnp.float32),
    )(cols, kernel2)
    zero = jnp.zeros((width, 1, channels), jnp.float32)
    above = jnp.concatenate([zero, acc[0, :, :-1]], axis=1)
    below = jnp.concatenate([acc[2, :, 1:], zero], axis=1)
    total = above + acc[1] + below
    return jnp.transpose(total, (1, 0, 2)).astype(jnp.bfloat16)


def shards(video, kernel3, kernel2):
    length, _, width, channels = video.shape
    groups = lax.axis_size("group")
    cached = shifted(video[length - 2 :], "group", 1)
    above = shifted(video, "frame", 1)
    below = shifted(video, "frame", -1)
    cached_above = diagonal(video[length - 2 :], 1, 1)
    cached_below = diagonal(video[length - 2 :], 1, -1)
    centre = jnp.concatenate([cached, video], 0)
    acc = conv3d_taps(centre, kernel3, (1,))
    edges = jnp.concatenate(
        [jnp.concatenate([cached_above, above], 0), jnp.concatenate([cached_below, below], 0)], 1
    )
    acc = conv3d_taps(edges, kernel3, (0, 2), acc)
    features = jax.nn.silu(column_sum(acc)).astype(jnp.bfloat16)
    block = width // groups
    padded = jnp.pad(features, ((0, 0), (1, 1), (0, 0)))
    pieces = jnp.stack([padded[:, j * block : j * block + block + 2] for j in range(groups)], 0)
    pieces = lax.all_to_all(pieces, "group", 0, 0, tiled=False)
    pieces = pieces.reshape(groups * length, block + 2, channels)
    cols = lax.all_to_all(pieces, "frame", 0, 1, tiled=False)
    critic = critic_conv(cols, kernel2)
    return features[:, None], critic[None]


def solution(mesh):
    return jax.shard_map(
        shards,
        mesh=mesh,
        in_specs=(P("group", "frame", None, None), P(), P()),
        out_specs=(P("group", "frame", None, None), P("frame", None, "group", None)),
        check_vma=False,
    )
```

time: 118 us -> 117 us (level)
  Pallas kernels: 11.3 us -> 18.9 us
  matrix products: 5.54 us -> 0 us
  waiting for transfers between devices: 4.5 us -> 0.73 us
  blocking collectives: 71.5 us -> 68.1 us
  local copies, waits for them, and re-layouts: 3.64 us -> 5.78 us
  other arithmetic: 3.57 us -> 5.37 us
    pallas_call x1 -> x3, Pallas kernels: 11.3 us -> 18.9 us  [the longest x2 13.9 us: conv3d_taps(): pl.pallas_call(conv3d_kernel, grid=(3 * pairs,), in_specs=[pl.BlockSpec(r...]
    conv_general_dilated x1 -> x0, matrix products: 5.54 us -> none  [shards(): lax.conv_general_dilated(rows_all[None], kernel2, (1, 1), ((1, 1), (0, 0)...]
    ppermute x2, waiting for transfers between devices: 4.49 us -> 0.73 us  [diagonal(): return lax.ppermute(value, ('group', 'frame'), pairs)]
    all_to_all x1, blocking collectives: 48.4 us -> 44.7 us  [shards(): cols = lax.all_to_all(pieces, 'frame', 0, 1, tiled=False)]
    concatenate x0 -> x1, other arithmetic: none -> 1.83 us  [shards(): centre = jnp.concatenate([cached, video], 0)]
    squeeze x1 -> x2, local copies, waits for them, and re-layouts: 1.32 us -> 2.64 us  [the longest x1 1.32 us: column_sum(): left = jnp.concatenate([zero, acc[0, :, :-1]], axis=1)]
    concatenate x1, other arithmetic: 2.3 us -> 1.1 us  [shards(): jnp.concatenate([jnp.concatenate([cached_above, above], 0), jnp.concatena...]
  transfers between devices with their start and end apart: 5 -> 5, of which waited for: 1 -> 1; matrix products, arithmetic and copies ran while one was open for 1% -> 2% of each run, Pallas kernels for 0% -> 4%
where the time goes in v3:
time: 117 us; the launch traced here: 116 us
  blocking collectives  68.1 us (58%)
  Pallas kernels  18.9 us (16%)
  starting transfers between devices  16.5 us (14%)
  local copies, waits for them, and re-layouts  5.78 us (5%)
  other arithmetic  5.37 us (5%)
    all_to_all x1, blocking collectives, shards(): cols = lax.all_to_all(pieces, 'frame', 0, 1, tiled=False)  44.7 us
    all_to_all x1, blocking collectives, shards(): pieces = lax.all_to_all(pieces, 'group', 0, 0, tiled=False)  23.4 us
    pallas_call x2, Pallas kernels, conv3d_taps(): pl.pallas_call(conv3d_kernel, grid=(3 * pairs,), in_specs=[pl.BlockSpec(r...  13.9 us
    ppermute x3, starting transfers between devices, shifted(): lax.ppermute(value, axis, [(source, source + steps) for source in range(f...  9.9 us
    ppermute x2, starting transfers between devices, diagonal(): return lax.ppermute(value, ('group', 'frame'), pairs)  6.58 us
    pallas_call x1, Pallas kernels, critic_conv(): pl.pallas_call(critic_kernel, grid=(3,), in_specs=[pl.BlockSpec(cols.shap...  4.91 us
  transfers between devices with their start and end apart: 5, of which 1 were waited for; matrix products, arithmetic and copies ran while one was open for 2% of the time, Pallas kernels for 4%

profile of v3, /device:TPU:1, one launch (start us, length us, event | category | flops | bytes accessed | tf_op | source)
XLA Modules:
  0.0 116.1 jit_solution(3376113404287906209)
XLA Ops:
  0.6 1.0 slice.85
  1.6 4.6 %collective-permute-start.4 = (bf16[2,1,128,384]{3,2,1,0:T(8,128)(2,1)S(1)}, bf16[2,1,128,384]{3,2,1,0:T(8,128)(2,1)S(1)}, u32[]{:S(2)}, u32[]{:S(2)}) collective-permute-start(bf16[2,1,128,384]{3,2,1,0:T(8,128)(2,1)S(1)} %slice.85), channel_id=1, source_target_pairs={{0,48},{48,96},{96,144},{144,192},{192,240},{240,288},{288,336},{3... | collective-permute-start | bytes 589832 | tf_op jit(solution)/shard_map/ppermute | solution.py:11
  6.2 4.0 %collective-permute-start.1 = (bf16[3,1,128,384]{3,2,1,0:T(8,128)(2,1)}, bf16[3,1,128,384]{3,2,1,0:T(8,128)(2,1)S(1)}, u32[]{:S(2)}, u32[]{:S(2)}) collective-permute-start(bf16[3,1,128,384]{3,2,1,0:T(8,128)(2,1)} %param.3), channel_id=1, source_target_pairs={{0,1},{1,2},{2,3},{3,4},{4,5},{5,6},{6,7},{7,8},{8,9},{9,10},{10,1... | collective-permute-start | bytes 884744 | tf_op jit(solution)/shard_map/ppermute | solution.py:11
  10.2 1.3 %collective-permute-start.3 = (bf16[3,1,128,384]{3,2,1,0:T(8,128)(2,1)}, bf16[3,1,128,384]{3,2,1,0:T(8,128)(2,1)S(1)}, u32[]{:S(2)}, u32[]{:S(2)}) collective-permute-start(bf16[3,1,128,384]{3,2,1,0:T(8,128)(2,1)} %param.3), channel_id=1, source_target_pairs={{1,0},{2,1},{3,2},{4,3},{5,4},{6,5},{7,6},{8,7},{9,8},{10,9},{11,1... | collective-permute-start | bytes 884744 | tf_op jit(solution)/shard_map/ppermute | solution.py:11
  11.5 1.3 %collective-permute-start.2 = (bf16[2,1,128,384]{3,2,1,0:T(8,128)(2,1)S(1)}, bf16[2,1,128,384]{3,2,1,0:T(8,128)(2,1)S(1)}, u32[]{:S(2)}, u32[]{:S(2)}) collective-permute-start(bf16[2,1,128,384]{3,2,1,0:T(8,128)(2,1)S(1)} %slice.85), channel_id=1, source_target_pairs={{1,48},{2,49},{3,50},{4,51},{5,52},{6,53},{7,54},{8,55},{9,56},{10... | collective-permute-start | bytes 589832 | tf_op jit(solution)/shard_map/ppermute | solution.py:22
  12.8 5.3 %collective-permute-start = (bf16[2,1,128,384]{3,2,1,0:T(8,128)(2,1)S(1)}, bf16[2,1,128,384]{3,2,1,0:T(8,128)(2,1)S(1)}, u32[]{:S(2)}, u32[]{:S(2)}) collective-permute-start(bf16[2,1,128,384]{3,2,1,0:T(8,128)(2,1)S(1)} %slice.85), channel_id=1, source_target_pairs={{0,49},{1,50},{2,51},{3,52},{4,53},{5,54},{6,55},{7,56},{8,57},{9,... | collective-permute-start | bytes 589832 | tf_op jit(solution)/shard_map/ppermute | solution.py:22
  18.1 0.0 collective-permute-done.4
  18.1 1.8 %pad_maximum_fusion.rows_ref = bf16[5,1,128,384]{3,2,1,0:T(8,128)(2,1)} fusion(bf16[3,1,128,384]{3,2,1,0:T(8,128)(2,1)} %param.3, bf16[2,1,128,384]{3,2,1,0:T(8,128)(2,1)S(1)} %collective-permute-done.4), kind=kLoop, calls=%fused_computation.13 | loop fusion | flops 245760 | bytes 983040 | tf_op jit(solution)/shard_map/concatenate | solution.py:119
  19.9 5.2 %shard_map.50.refs_0_ = f32[3,3,128,384]{3,2,1,0:T(8,128)} custom-call(bf16[5,1,128,384]{3,2,1,0:T(8,128)(2,1)} %pad_maximum_fusion.rows_ref, bf16[3,3,3,384,384]{4,3,2,1,0:T(8,128)(2,1)} %kernel_ref.4), custom_call_target="tpu_custom_call" | custom-call | tf_op jit(solution)/shard_map/pallas_call | solution.py:58
  25.2 0.7 collective-permute-done.2
  25.9 0.0 collective-permute-done
  25.9 0.0 collective-permute-done.1
  25.9 0.0 collective-permute-done.3
  25.9 1.1 maximum_maximum_fusion.rows_ref
  27.0 8.7 %shard_map.51 = f32[3,3,128,384]{3,2,1,0:T(8,128)} custom-call(bf16[5,2,128,384]{3,2,1,0:T(8,128)(2,1)} %maximum_maximum_fusion.rows_ref, bf16[3,3,3,384,384]{4,3,2,1,0:T(8,128)(2,1)} %kernel_ref.4, f32[3,3,128,384]{3,2,1,0:T(8,128)} %shard_map.50.refs_0_), custom_call_target="tpu_custom_call", output_to_operand_aliasing={{}: (2, {})} | custom-call | tf_op jit(solution)/shard_map/pallas_call | solution.py:58
  35.7 1.3 %slice_bitcast_fusion.5 = (f32[3,127,384]{2,1,0:T(8,128)S(1)}, f32[3,127,384]{2,1,0:T(8,128)S(1)}) fusion(f32[3,3,128,384]{3,2,1,0:T(8,128)} %shard_map.51), kind=kLoop, calls=%fused_computation.11 | loop fusion | bytes 2340864 | tf_op jit(solution)/shard_map/squeeze | solution.py:75
  37.1 1.3 %multiply_convert_fusion = bf16[3,128,384]{2,1,0:T(8,128)(2,1)S(1)} fusion(f32[3,3,128,384]{3,2,1,0:T(8,128)} %shard_map.51, f32[3,127,384]{2,1,0:T(8,128)S(1)} %get-tuple-element.11, f32[3,127,384]{2,1,0:T(8,128)S(1)} %get-tuple-element.10), kind=kLoop, calls=%fused_computation.12 | loop fusion | flops 1032192 | bytes 2055168 | tf_op jit(solution)/shard_map/convert_element_type | solution.py:125
  38.3 0.0 copy-start
  38.7 0.2 copy.12
  38.9 23.4 %all_to_all.20 = bf16[16,3,10,384]{3,1,2,0:T(4,128)(2,1)S(1)} all-to-all(bf16[16,3,10,384]{3,1,2,0:T(4,128)(2,1)S(1)} %copy.12), channel_id=1, replica_groups=mesh['group'=16,'frame'=48] {'group'}, dimensions={0} | all-to-all | bytes 737280 | tf_op jit(solution)/shard_map/all_to_all | solution.py:129
  62.3 0.0 copy-done
  62.3 0.1 copy.18
  62.4 44.7 %all_to_all.21 = bf16[48,10,1,384]{3,1,2,0:T(8,128)(2,1)S(1)} all-to-all(bf16[48,10,1,384]{3,1,2,0:T(8,128)(2,1)S(1)} %bitcast.106), channel_id=1, replica_groups=mesh['group'=16,'frame'=48] {'frame'}, dimensions={0} | all-to-all | bytes 737280 | tf_op jit(solution)/shard_map/all_to_all | solution.py:131
  107.1 0.8 copy.21
  108.0 4.9 %shard_map.52 = f32[3,8,48,384]{3,2,1,0:T(8,128)} custom-call(bf16[10,48,384]{2,1,0:T(8,128)(2,1)} %bitcast.107, bf16[3,3,384,384]{3,2,1,0:T(8,128)(2,1)} %kernel_ref.5), custom_call_target="tpu_custom_call" | custom-call | tf_op jit(solution)/shard_map/pallas_call | solution.py:94
  112.9 1.3 %slice_bitcast_fusion.2 = (f32[8,47,384]{2,1,0:T(8,128)S(1)}, f32[8,47,384]{2,1,0:T(8,128)S(1)}) fusion(f32[3,8,48,384]{3,2,1,0:T(8,128)} %shard_map.52), kind=kLoop, calls=%fused_computation.6 | loop fusion | bytes 2310144 | tf_op jit(solution)/shard_map/squeeze | solution.py:105
  114.2 1.2 %fusion.5 = bf16[1,48,8,384]{3,1,2,0:T(8,128)(2,1)S(1)} fusion(f32[8,47,384]{2,1,0:T(8,128)S(1)} %get-tuple-element.9, f32[3,8,48,384]{3,2,1,0:T(8,128)} %shard_map.52, f32[8,47,384]{2,1,0:T(8,128)S(1)} %get-tuple-element.8), kind=kLoop, calls=%fused_computation.15 | loop fusion | flops 442368 | bytes 2039808 | tf_op jit(solution)/shard_map/broadcast_in_dim | solution.py:133
  115.4 0.8 copy.17
  (16 shorter events, 0.3 us)
Async XLA Ops:
  1.6 16.5 %collective-permute-start.4 = (bf16[2,1,128,384]{3,2,1,0:T(8,128)(2,1)S(1)}, bf16[2,1,128,384]{3,2,1,0:T(8,128)(2,1)S(1)}, u32[]{:S(2)}, u32[]{:S(2)}) collective-permute-start(bf16[2,1,128,384]{3,2,1,0:T(8,128)(2,1)S(1)} %slice.85), channel_id=1, source_target_pairs={{0,48},{48,96},{96,144},{144,192},{192,240},{240,288},{288,336},{3... | collective-permute-start | bytes 589832 | tf_op jit(solution)/shard_map/ppermute | solution.py:11
  6.2 19.7 %collective-permute-start.1 = (bf16[3,1,128,384]{3,2,1,0:T(8,128)(2,1)}, bf16[3,1,128,384]{3,2,1,0:T(8,128)(2,1)S(1)}, u32[]{:S(2)}, u32[]{:S(2)}) collective-permute-start(bf16[3,1,128,384]{3,2,1,0:T(8,128)(2,1)} %param.3), channel_id=1, source_target_pairs={{0,1},{1,2},{2,3},{3,4},{4,5},{5,6},{6,7},{7,8},{8,9},{9,10},{10,1... | collective-permute-start | bytes 884744 | tf_op jit(solution)/shard_map/ppermute | solution.py:11
  10.2 15.7 %collective-permute-start.3 = (bf16[3,1,128,384]{3,2,1,0:T(8,128)(2,1)}, bf16[3,1,128,384]{3,2,1,0:T(8,128)(2,1)S(1)}, u32[]{:S(2)}, u32[]{:S(2)}) collective-permute-start(bf16[3,1,128,384]{3,2,1,0:T(8,128)(2,1)} %param.3), channel_id=1, source_target_pairs={{1,0},{2,1},{3,2},{4,3},{5,4},{6,5},{7,6},{8,7},{9,8},{10,9},{11,1... | collective-permute-start | bytes 884744 | tf_op jit(solution)/shard_map/ppermute | solution.py:11
  11.5 14.4 %collective-permute-start.2 = (bf16[2,1,128,384]{3,2,1,0:T(8,128)(2,1)S(1)}, bf16[2,1,128,384]{3,2,1,0:T(8,128)(2,1)S(1)}, u32[]{:S(2)}, u32[]{:S(2)}) collective-permute-start(bf16[2,1,128,384]{3,2,1,0:T(8,128)(2,1)S(1)} %slice.85), channel_id=1, source_target_pairs={{1,48},{2,49},{3,50},{4,51},{5,52},{6,53},{7,54},{8,55},{9,56},{10... | collective-permute-start | bytes 589832 | tf_op jit(solution)/shard_map/ppermute | solution.py:22
  12.8 13.1 %collective-permute-start = (bf16[2,1,128,384]{3,2,1,0:T(8,128)(2,1)S(1)}, bf16[2,1,128,384]{3,2,1,0:T(8,128)(2,1)S(1)}, u32[]{:S(2)}, u32[]{:S(2)}) collective-permute-start(bf16[2,1,128,384]{3,2,1,0:T(8,128)(2,1)S(1)} %slice.85), channel_id=1, source_target_pairs={{0,49},{1,50},{2,51},{3,52},{4,53},{5,54},{6,55},{7,56},{8,57},{9,... | collective-permute-start | bytes 589832 | tf_op jit(solution)/shard_map/ppermute | solution.py:22
  38.3 24.0 %copy-start = (bf16[3,128,384]{2,1,0:T(8,128)(2,1)}, bf16[3,128,384]{2,1,0:T(8,128)(2,1)S(1)}, u32[]{:S(2)}) copy-start(bf16[3,128,384]{2,1,0:T(8,128)(2,1)S(1)} %multiply_convert_fusion) | copy-start | bytes 884740

commit v4 on v1

v4 whole, which is shorter than its diff:
```python
import jax
import jax.numpy as jnp
from jax import lax
from jax.experimental import pallas as pl
from jax.experimental.pallas import tpu as pltpu
from jax.sharding import PartitionSpec as P


def shifted(value, axis, steps):
    count = lax.axis_size(axis)
    first, last = (max(0, -steps), min(count, count - steps))
    return lax.ppermute(value, axis, [(source, source + steps) for source in range(first, last)])


def diagonal(value, group_steps, frame_steps):
    groups, frames = lax.axis_size("group"), lax.axis_size("frame")
    pairs = []
    for g in range(groups):
        for f in range(frames):
            h, e = g + group_steps, f + frame_steps
            if 0 <= h < groups and 0 <= e < frames:
                pairs.append((g * frames + f, h * frames + e))
    return lax.ppermute(value, ("group", "frame"), pairs)


def shifted_columns(rows):
    width = rows.shape[-2]
    pad = [(0, 0)] * (rows.ndim - 2) + [(1, 1), (0, 0)]
    padded = jnp.pad(rows, pad)
    return jnp.concatenate([padded[..., c : c + width, :] for c in range(3)], axis=-1)


def conv3d_kernel(rows_ref, kernel_ref, *refs):
    out_ref, acc_ref = refs[-2], refs[-1]
    step = pl.program_id(0)
    last = pl.num_programs(0) - 1
    pairs = rows_ref.shape[1]
    frames, width, channels = out_ref.shape
    lhs = rows_ref[pl.ds(step // pairs, frames), step % pairs].reshape(frames * width, 3 * channels)
    part = jnp.dot(lhs, kernel_ref[0, 0], preferred_element_type=jnp.float32).reshape(out_ref.shape)
    if len(refs) == 2:

        @pl.when(step == 0)
        def _():
            acc_ref[...] = part

        @pl.when(step > 0)
        def _():
            acc_ref[...] += part

        @pl.when(step == last)
        def _():
            out_ref[...] = acc_ref[...]

    else:
        prior_ref = refs[0]

        @pl.when(step == 0)
        def _():
            acc_ref[...] = prior_ref[...] + part

        @pl.when(step > 0)
        def _():
            acc_ref[...] += part

        @pl.when(step == last)
        def _():
            out_ref[...] = jax.nn.silu(acc_ref[...]).astype(out_ref.dtype)


def conv3d_taps(rows, kernel3, row_taps, prior=None):
    frames, pairs, width, wide = rows.shape
    channels = wide // 3
    count = frames - 2
    taps = kernel3.reshape(3, 3, 1, wide, channels)
    if pairs == 1:
        index = lambda s: (s, row_taps[0], 0, 0, 0)
    else:
        index = lambda s: (s // 2, row_taps[0] + (row_taps[1] - row_taps[0]) * (s % 2), 0, 0, 0)
    block = (count, width, channels)
    full = pl.BlockSpec(block, lambda s: (0, 0, 0))
    dtype = jnp.float32 if prior is None else jnp.bfloat16
    operands = [rows, taps] + ([] if prior is None else [prior])
    return pl.pallas_call(
        conv3d_kernel,
        grid=(3 * pairs,),
        in_specs=[
            pl.BlockSpec(rows.shape, lambda s: (0, 0, 0, 0)),
            pl.BlockSpec((1, 1, 1, wide, channels), index),
        ]
        + ([] if prior is None else [full]),
        out_specs=full,
        out_shape=jax.ShapeDtypeStruct(block, dtype),
        scratch_shapes=[pltpu.VMEM(block, jnp.float32)],
    )(*operands)


def critic_kernel(lhs_ref, kernel_ref, out_ref):
    rows, width, channels = out_ref.shape
    lhs = lhs_ref[...].reshape(rows * width, lhs_ref.shape[-1])
    total = jnp.dot(lhs, kernel_ref[...], preferred_element_type=jnp.float32)
    out_ref[...] = total.reshape(out_ref.shape).astype(out_ref.dtype)


def critic_conv(features, kernel2):
    rows, span, channels = features.shape
    width = span - 2
    padded = jnp.pad(features, ((1, 1), (0, 0), (0, 0)))
    lhs = jnp.concatenate(
        [padded[b : b + rows, c : c + width] for b in range(3) for c in range(3)], axis=-1
    )
    return pl.pallas_call(
        critic_kernel,
        out_shape=jax.ShapeDtypeStruct((rows, width, channels), jnp.bfloat16),
    )(lhs, kernel2.reshape(9 * channels, channels))


def shards(video, kernel3, kernel2):
    length, _, width, channels = video.shape
    groups = lax.axis_size("group")
    cached = shifted(video[length - 2 :], "group", 1)
    above = shifted(video, "frame", 1)
    below = shifted(video, "frame", -1)
    cached_above = diagonal(video[length - 2 :], 1, 1)
    cached_below = diagonal(video[length - 2 :], 1, -1)
    centre = shifted_columns(jnp.concatenate([cached, video], 0))
    acc = conv3d_taps(centre, kernel3, (1,))
    edges = jnp.concatenate(
        [jnp.concatenate([cached_above, above], 0), jnp.concatenate([cached_below, below], 0)], 1
    )
    features = conv3d_taps(shifted_columns(edges), kernel3, (0, 2), acc)
    block = width // groups
    padded = jnp.pad(features, ((0, 0), (1, 1), (0, 0)))
    pieces = jnp.stack([padded[:, j * block : j * block + block + 2] for j in range(groups)], 0)
    pieces = lax.all_to_all(pieces, "group", 0, 0, tiled=False)
    pieces = pieces.reshape(groups * length, block + 2, channels)
    rows_all = lax.all_to_all(pieces, "frame", 0, 0, tiled=True)
    critic = critic_conv(rows_all, kernel2)
    return features[:, None], critic[None]


def solution(mesh):
    return jax.shard_map(
        shards,
        mesh=mesh,
        in_specs=(P("group", "frame", None, None), P(), P()),
        out_specs=(P("group", "frame", None, None), P("frame", None, "group", None)),
        check_vma=False,
    )
```

time: 123 us -> 142 us (1.15)
  blocking collectives: 23.1 us -> 68 us
  Pallas kernels: 0 us -> 33 us
  waiting for transfers between devices: 29.2 us -> 0.01 us
  starting transfers between devices: 38.9 us -> 16.5 us
  matrix products: 15.6 us -> 0 us
  local copies, waits for them, and re-layouts: 12.2 us -> 18.7 us
    all_to_all x0 -> x1, blocking collectives: none -> 45.3 us  [shards(): rows_all = lax.all_to_all(pieces, 'frame', 0, 0, tiled=True)]
    pallas_call x0 -> x3, Pallas kernels: none -> 33 us  [the longest x2 28.2 us: conv3d_taps(): pl.pallas_call(conv3d_kernel, grid=(3 * pairs,), in_specs=[pl.BlockSpec(r...]
    all_to_all x1 -> x0, waiting for transfers between devices: 24.7 us -> none  [shards(): rows_all = lax.all_to_all(pieces, 'frame', 0, 0, tiled=True)]
    all_to_all x1 -> x0, starting transfers between devices: 22 us -> none  [shards(): rows_all = lax.all_to_all(pieces, 'frame', 0, 0, tiled=True)]
    conv_general_dilated x2 -> x0, matrix products: 15.6 us -> none  [the longest x1 9.01 us: conv3d(): lax.conv_general_dilated(rows[None], kernel3, (1, 1, 1), ((0, 0), (0, 0),...]
    unnamed x21 -> x26, local copies, waits for them, and re-layouts: 1.82 us -> 14.9 us
    conv_general_dilated x5 -> x0, local copies, waits for them, and re-layouts: 6.63 us -> none  [conv3d(): lax.conv_general_dilated(rows[None], kernel3, (1, 1, 1), ((0, 0), (0, 0),...]
    ppermute x2, waiting for transfers between devices: 4.49 us -> 0.01 us  [diagonal(): return lax.ppermute(value, ('group', 'frame'), pairs)]
  transfers between devices with their start and end apart: 6 -> 5, of which waited for: 2 -> 0; matrix products, arithmetic and copies ran while one was open for 2% -> 2% of each run, Pallas kernels for 0% -> 7%
where the time goes in v4:
time: 142 us; the launch traced here: 140 us
  blocking collectives  68 us (48%)
  Pallas kernels  33 us (23%)
  local copies, waits for them, and re-layouts  18.7 us (13%)
  starting transfers between devices  16.5 us (12%)
  other arithmetic  3.38 us (2%)
    all_to_all x1, blocking collectives, shards(): rows_all = lax.all_to_all(pieces, 'frame', 0, 0, tiled=True)  45.3 us
    pallas_call x2, Pallas kernels, conv3d_taps(): pl.pallas_call(conv3d_kernel, grid=(3 * pairs,), in_specs=[pl.BlockSpec(r...  28.2 us
    all_to_all x1, blocking collectives, shards(): pieces = lax.all_to_all(pieces, 'group', 0, 0, tiled=False)  22.6 us
    unnamed x26, local copies, waits for them, and re-layouts  14.9 us
    ppermute x3, starting transfers between devices, shifted(): lax.ppermute(value, axis, [(source, source + steps) for source in range(f...  11.5 us
    ppermute x2, starting transfers between devices, diagonal(): return lax.ppermute(value, ('group', 'frame'), pairs)  5.03 us
    pallas_call x1, Pallas kernels, critic_conv(): pl.pallas_call(critic_kernel, out_shape=jax.ShapeDtypeStruct((rows, width...  4.81 us
    concatenate x2, other arithmetic, shifted_columns(): jnp.concatenate([padded[..., c:c + width, :] for c in range(3)], axis=-1)  3.1 us
  transfers between devices with their start and end apart: 5, of which 0 were waited for; matrix products, arithmetic and copies ran while one was open for 2% of the time, Pallas kernels for 7%

profile of v4, /device:TPU:1, one launch (start us, length us, event | category | flops | bytes accessed | tf_op | source)
XLA Modules:
  0.0 140.4 jit_solution(3914865855210992229)
XLA Ops:
  0.6 1.0 slice.111
  1.6 4.6 %collective-permute-start.4 = (bf16[2,1,128,384]{3,2,1,0:T(8,128)(2,1)S(1)}, bf16[2,1,128,384]{3,2,1,0:T(8,128)(2,1)S(1)}, u32[]{:S(2)}, u32[]{:S(2)}) collective-permute-start(bf16[2,1,128,384]{3,2,1,0:T(8,128)(2,1)S(1)} %slice.111), channel_id=1, source_target_pairs={{0,48},{48,96},{96,144},{144,192},{192,240},{240,288},{288,336},{3... | collective-permute-start | bytes 589832 | tf_op jit(solution)/shard_map/ppermute | solution.py:12
  6.2 3.7 %collective-permute-start = (bf16[2,1,128,384]{3,2,1,0:T(8,128)(2,1)S(1)}, bf16[2,1,128,384]{3,2,1,0:T(8,128)(2,1)S(1)}, u32[]{:S(2)}, u32[]{:S(2)}) collective-permute-start(bf16[2,1,128,384]{3,2,1,0:T(8,128)(2,1)S(1)} %slice.111), channel_id=1, source_target_pairs={{0,49},{1,50},{2,51},{3,52},{4,53},{5,54},{6,55},{7,56},{8,57},{9,... | collective-permute-start | bytes 589832 | tf_op jit(solution)/shard_map/ppermute | solution.py:23
  9.9 1.3 collective-permute-start.2
  11.2 5.6 %collective-permute-start.1 = (bf16[3,1,128,384]{3,2,1,0:T(8,128)(2,1)}, bf16[3,1,128,384]{3,2,1,0:T(8,128)(2,1)S(1)}, u32[]{:S(2)}, u32[]{:S(2)}) collective-permute-start(bf16[3,1,128,384]{3,2,1,0:T(8,128)(2,1)} %param.3), channel_id=1, source_target_pairs={{0,1},{1,2},{2,3},{3,4},{4,5},{5,6},{6,7},{7,8},{8,9},{9,10},{10,1... | collective-permute-start | bytes 884744 | tf_op jit(solution)/shard_map/ppermute | solution.py:12
  16.8 1.3 collective-permute-start.3
  18.1 1.0 constant_dynamic-update-slice_fusion
  19.4 1.3 pad_maximum_fusion.1.rows_ref
  20.7 10.0 %shard_map.50.refs_0_ = f32[3,128,384]{2,1,0:T(8,128)} custom-call(bf16[5,1,128,1152]{3,2,1,0:T(8,128)(2,1)} %pad_maximum_fusion.1.rows_ref, bf16[3,3,1,1152,384]{4,3,2,1,0:T(8,128)(2,1)} %bitcast.71), custom_call_target="tpu_custom_call" | custom-call | tf_op jit(solution)/shard_map/pallas_call | solution.py:84
  31.0 0.4 fusion.13
  31.4 1.8 %pad_maximum_fusion.rows_ref = bf16[5,2,128,1152]{3,2,1,0:T(8,128)(2,1)} fusion(bf16[5,2,128,384]{3,2,1,0:T(8,128)(2,1)S(1)} %get-tuple-element.7, bf16[3,1,128,384]{3,2,1,0:T(8,128)(2,1)S(1)} %collective-permute-done.3, bf16[2,1,128,384]{3,2,1,0:T(8,128)(2,1)S(1)} %collective-permute-done.2, bf16[3,1,128,384]{3,2,1,0:T(8,128)(2,1)S(1)} %collective-permute-done.1, ...), kind=kLoop, calls=%fused_computation.2 | loop fusion | flops 17694720 | bytes 5898240 | tf_op jit(solution)/shard_map/concatenate | solution.py:30
  33.2 18.2 %shard_map.51 = bf16[3,128,384]{2,1,0:T(8,128)(2,1)} custom-call(bf16[5,2,128,1152]{3,2,1,0:T(8,128)(2,1)} %pad_maximum_fusion.rows_ref, bf16[3,3,1,1152,384]{4,3,2,1,0:T(8,128)(2,1)} %bitcast.72, f32[3,128,384]{2,1,0:T(8,128)} %shard_map.50.refs_0_), custom_call_target="tpu_custom_call" | custom-call | tf_op jit(solution)/shard_map/pallas_call | solution.py:84
  51.4 0.8 constant_dynamic-update-slice_fusion.17
  52.2 0.8 constant_dynamic-update-slice_fusion.16
  53.0 0.8 constant_dynamic-update-slice_fusion.15
  53.9 0.8 constant_dynamic-update-slice_fusion.14
  54.7 0.8 constant_dynamic-update-slice_fusion.13
  55.5 0.8 constant_dynamic-update-slice_fusion.12
  56.4 0.8 constant_dynamic-update-slice_fusion.11
  57.2 0.8 constant_dynamic-update-slice_fusion.10
  58.1 0.8 constant_dynamic-update-slice_fusion.9
  58.9 0.8 constant_dynamic-update-slice_fusion.8
  59.8 0.8 constant_dynamic-update-slice_fusion.7
  60.6 0.8 constant_dynamic-update-slice_fusion.6
  61.4 0.8 constant_dynamic-update-slice_fusion.5
  62.3 0.8 constant_dynamic-update-slice_fusion.4
  63.1 0.8 constant_dynamic-update-slice_fusion.3
  64.0 0.8 constant_dynamic-update-slice_fusion.2
  64.9 22.6 %all_to_all.10 = bf16[16,3,10,384]{3,1,2,0:T(4,128)(2,1)S(1)} all-to-all(bf16[16,3,10,384]{3,1,2,0:T(4,128)(2,1)S(1)} %copy.6), channel_id=1, replica_groups=mesh['group'=16,'frame'=48] {'group'}, dimensions={0} | all-to-all | bytes 737280 | tf_op jit(solution)/shard_map/all_to_all | solution.py:135
  87.7 45.3 %all_to_all.11 = bf16[48,10,384]{2,1,0:T(8,128)(2,1)S(1)} all-to-all(bf16[48,10,384]{2,1,0:T(8,128)(2,1)S(1)} %bitcast.75), channel_id=1, replica_groups=mesh['group'=16,'frame'=48] {'frame'}, dimensions={0} | all-to-all | bytes 737280 | tf_op jit(solution)/shard_map/all_to_all | solution.py:137
  134.0 1.5 %copy-done = bf16[48,8,3456]{2,1,0:T(8,128)(2,1)} copy-done((bf16[48,8,3456]{2,1,0:T(8,128)(2,1)}, bf16[48,8,3456]{2,1,0:T(8,128)(2,1)S(1)}, u32[]{:S(2)}) %copy-start) | copy-done | bytes 2654232
  135.5 4.8 %shard_map.52 = bf16[48,8,384]{2,1,0:T(8,128)(2,1)} custom-call(bf16[48,8,3456]{2,1,0:T(8,128)(2,1)} %copy-done, bf16[3456,384]{1,0:T(8,128)(2,1)} %bitcast.74), custom_call_target="tpu_custom_call" | custom-call | tf_op jit(solution)/shard_map/pallas_call | solution.py:112
  (20 shorter events, 1.8 us)
Async XLA Ops:
  1.6 16.5 %collective-permute-start.4 = (bf16[2,1,128,384]{3,2,1,0:T(8,128)(2,1)S(1)}, bf16[2,1,128,384]{3,2,1,0:T(8,128)(2,1)S(1)}, u32[]{:S(2)}, u32[]{:S(2)}) collective-permute-start(bf16[2,1,128,384]{3,2,1,0:T(8,128)(2,1)S(1)} %slice.111), channel_id=1, source_target_pairs={{0,48},{48,96},{96,144},{144,192},{192,240},{240,288},{288,336},{3... | collective-permute-start | bytes 589832 | tf_op jit(solution)/shard_map/ppermute | solution.py:12
  6.2 24.5 %collective-permute-start = (bf16[2,1,128,384]{3,2,1,0:T(8,128)(2,1)S(1)}, bf16[2,1,128,384]{3,2,1,0:T(8,128)(2,1)S(1)}, u32[]{:S(2)}, u32[]{:S(2)}) collective-permute-start(bf16[2,1,128,384]{3,2,1,0:T(8,128)(2,1)S(1)} %slice.111), channel_id=1, source_target_pairs={{0,49},{1,50},{2,51},{3,52},{4,53},{5,54},{6,55},{7,56},{8,57},{9,... | collective-permute-start | bytes 589832 | tf_op jit(solution)/shard_map/ppermute | solution.py:23
  9.9 20.8 %collective-permute-start.2 = (bf16[2,1,128,384]{3,2,1,0:T(8,128)(2,1)S(1)}, bf16[2,1,128,384]{3,2,1,0:T(8,128)(2,1)S(1)}, u32[]{:S(2)}, u32[]{:S(2)}) collective-permute-start(bf16[2,1,128,384]{3,2,1,0:T(8,128)(2,1)S(1)} %slice.111), channel_id=1, source_target_pairs={{1,48},{2,49},{3,50},{4,51},{5,52},{6,53},{7,54},{8,55},{9,56},{10... | collective-permute-start | bytes 589832 | tf_op jit(solution)/shard_map/ppermute | solution.py:23
  11.2 19.5 %collective-permute-start.1 = (bf16[3,1,128,384]{3,2,1,0:T(8,128)(2,1)}, bf16[3,1,128,384]{3,2,1,0:T(8,128)(2,1)S(1)}, u32[]{:S(2)}, u32[]{:S(2)}) collective-permute-start(bf16[3,1,128,384]{3,2,1,0:T(8,128)(2,1)} %param.3), channel_id=1, source_target_pairs={{0,1},{1,2},{2,3},{3,4},{4,5},{5,6},{6,7},{7,8},{8,9},{9,10},{10,1... | collective-permute-start | bytes 884744 | tf_op jit(solution)/shard_map/ppermute | solution.py:12
  16.8 13.9 %collective-permute-start.3 = (bf16[3,1,128,384]{3,2,1,0:T(8,128)(2,1)}, bf16[3,1,128,384]{3,2,1,0:T(8,128)(2,1)S(1)}, u32[]{:S(2)}, u32[]{:S(2)}) collective-permute-start(bf16[3,1,128,384]{3,2,1,0:T(8,128)(2,1)} %param.3), channel_id=1, source_target_pairs={{1,0},{2,1},{3,2},{4,3},{5,4},{6,5},{7,6},{8,7},{9,8},{10,9},{11,1... | collective-permute-start | bytes 884744 | tf_op jit(solution)/shard_map/ppermute | solution.py:12
  134.0 1.5 %copy-start = (bf16[48,8,3456]{2,1,0:T(8,128)(2,1)}, bf16[48,8,3456]{2,1,0:T(8,128)(2,1)S(1)}, u32[]{:S(2)}) copy-start(bf16[48,8,3456]{2,1,0:T(8,128)(2,1)S(1)} %fusion.10.lhs_ref) | copy-start | bytes 7962628

commit v5 on v2

--- a/solution.py
+++ b/solution.py
@@ -2,6 +2,7 @@
 import jax.numpy as jnp
 from jax import lax
 from jax.experimental import pallas as pl
+from jax.experimental.pallas import tpu as pltpu
 from jax.sharding import PartitionSpec as P
 
 
@@ -22,38 +23,63 @@
     return lax.ppermute(value, ("group", "frame"), pairs)
 
 
-def conv3d_kernel(rows_ref, kernel_ref, acc_ref):
+def conv3d_kernel(rows_ref, kernel_ref, *refs):
+    out_ref, acc_ref = refs[-2], refs[-1]
     step = pl.program_id(0)
+    pairs = rows_ref.shape[1]
     frames, width, channels = acc_ref.shape[1:]
 
     @pl.when(step == 0)
     def _():
-        acc_ref[...] = jnp.zeros_like(acc_ref)
+        if len(refs) == 2:
+            acc_ref[...] = jnp.zeros_like(acc_ref)
+        else:
+            acc_ref[...] = refs[0][...]
 
-    lhs = rows_ref[pl.ds(step // 3, frames), step % 3].reshape(frames * width, channels)
+    lhs = rows_ref[pl.ds(step // pairs, frames), step % pairs].reshape(frames * width, channels)
     for c in range(3):
-        part = jnp.dot(lhs, kernel_ref[0, c], preferred_element_type=jnp.float32)
+        part = jnp.dot(lhs, kernel_ref[0, 0, c], preferred_element_type=jnp.float32)
         acc_ref[c] += part.reshape(frames, width, channels)
 
+    @pl.when(step == pl.num_programs(0) - 1)
+    def _():
+        if len(refs) == 2:
+            out_ref[...] = acc_ref[...]
+        else:
+            column = lax.broadcasted_iota(jnp.int32, (frames, width, channels), 1)
+            left = jnp.where(column == 0, 0.0, pltpu.roll(acc_ref[0], 1, 1))
+            right = jnp.where(column == width - 1, 0.0, pltpu.roll(acc_ref[2], width - 1, 1))
+            total = left + acc_ref[1] + right
+            out_ref[...] = (total / (1.0 + jnp.exp(-total))).astype(out_ref.dtype)
 
-def conv3d(rows, kernel3):
-    frames, _, width, channels = rows.shape
+
+def conv3d_taps(rows, kernel3, row_taps, acc=None):
+    frames, pairs, width, channels = rows.shape
     count = frames - 2
-    taps = kernel3.reshape(9, 3, channels, channels)
-    acc = pl.pallas_call(
+    if pairs == 1:
+        index = lambda s: (s, row_taps[0], 0, 0, 0)
+    else:
+        index = lambda s: (s // 2, row_taps[0] + (row_taps[1] - row_taps[0]) * (s % 2), 0, 0, 0)
+    acc_block = (3, count, width, channels)
+    acc_spec = pl.BlockSpec(acc_block, lambda s: (0, 0, 0, 0))
+    if acc is None:
+        out_spec, out_shape = acc_spec, jax.ShapeDtypeStruct(acc_block, jnp.float32)
+    else:
+        out_spec = pl.BlockSpec((count, width, channels), lambda s: (0, 0, 0))
+        out_shape = jax.ShapeDtypeStruct((count, width, channels), jnp.bfloat16)
+    operands = [rows, kernel3] + ([] if acc is None else [acc])
+    return pl.pallas_call(
         conv3d_kernel,
-        grid=(9,),
+        grid=(3 * pairs,),
         in_specs=[
             pl.BlockSpec(rows.shape, lambda s: (0, 0, 0, 0)),
-            pl.BlockSpec((1, 3, channels, channels), lambda s: (s, 0, 0, 0)),
-        ],
-        out_specs=pl.BlockSpec((3, count, width, channels), lambda s: (0, 0, 0, 0)),
-        out_shape=jax.ShapeDtypeStruct((3, count, width, channels), jnp.float32),
-    )(rows, taps)
-    zero = jnp.zeros((count, 1, channels), jnp.float32)
-    left = jnp.concatenate([zero, acc[0, :, :-1]], axis=1)
-    right = jnp.concatenate([acc[2, :, 1:], zero], axis=1)
-    return left + acc[1] + right
+            pl.BlockSpec((1, 1, 3, channels, channels), index),
+        ]
+        + ([] if acc is None else [acc_spec]),
+        out_specs=out_spec,
+        out_shape=out_shape,
+        scratch_shapes=[pltpu.VMEM(acc_block, jnp.float32)],
+    )(*operands)
 
 
 def shards(video, kernel3, kernel2):
@@ -64,16 +90,12 @@
     below = shifted(video, "frame", -1)
     cached_above = diagonal(video[length - 2 :], 1, 1)
     cached_below = diagonal(video[length - 2 :], 1, -1)
-    rows = jnp.concatenate(
-        [
-            jnp.concatenate([cached_above, above], 0),
-            jnp.concatenate([cached, video], 0),
-            jnp.concatenate([cached_below, below], 0),
-        ],
-        1,
+    centre = jnp.concatenate([cached, video], 0)
+    acc = conv3d_taps(centre, kernel3, (1,))
+    edges = jnp.concatenate(
+        [jnp.concatenate([cached_above, above], 0), jnp.concatenate([cached_below, below], 0)], 1
     )
-    conv = conv3d(rows, kernel3)
-    features = jax.nn.silu(conv).astype(jnp.bfloat16)
+    features = conv3d_taps(edges, kernel3, (0, 2), acc)
     block = width // groups
     padded = jnp.pad(features, ((0, 0), (1, 1), (0, 0)))
     pieces = jnp.stack([padded[:, j * block : j * block + block + 2] for j in range(groups)], 0)

time: 118 us -> 126 us (1.068)
  local copies, waits for them, and re-layouts: 3.64 us -> 15.5 us
  waiting for transfers between devices: 4.5 us -> 0.07 us
  blocking collectives: 71.5 us -> 68.1 us
  Pallas kernels: 11.3 us -> 13.8 us
    unnamed x20 -> x18, local copies, waits for them, and re-layouts: 1.07 us -> 13.3 us
    ppermute x2, waiting for transfers between devices: 4.49 us -> 0.06 us  [diagonal(): return lax.ppermute(value, ('group', 'frame'), pairs)]
    all_to_all x1, blocking collectives: 48.4 us -> 44.7 us  [shards(): rows_all = lax.all_to_all(pieces, 'frame', 0, 0, tiled=True)]
    pallas_call x1 -> x2, Pallas kernels: 11.3 us -> 13.8 us  [conv3d_taps(): pl.pallas_call(conv3d_kernel, grid=(3 * pairs,), in_specs=[pl.BlockSpec(r...]
    concatenate x0 -> x1, other arithmetic: none -> 1.82 us  [shards(): centre = jnp.concatenate([cached, video], 0)]
    squeeze x1 -> x0, local copies, waits for them, and re-layouts: 1.32 us -> none  [conv3d(): left = jnp.concatenate([zero, acc[0, :, :-1]], axis=1)]
    convert_element_type x1 -> x0, other arithmetic: 1.27 us -> none  [shards(): features = jax.nn.silu(conv).astype(jnp.bfloat16)]
  transfers between devices with their start and end apart: 5 -> 5, of which waited for: 1 -> 1; matrix products, arithmetic and copies ran while one was open for 1% -> 1% of each run, Pallas kernels for 0% -> 4%
where the time goes in v5:
time: 126 us; the launch traced here: 125 us
  blocking collectives  68.1 us (54%)
  starting transfers between devices  17.2 us (14%)
  local copies, waits for them, and re-layouts  15.5 us (12%)
  Pallas kernels  13.8 us (11%)
  matrix products  5.54 us (4%)
  other arithmetic  3.94 us (3%)
    all_to_all x1, blocking collectives, shards(): rows_all = lax.all_to_all(pieces, 'frame', 0, 0, tiled=True)  44.7 us
    all_to_all x1, blocking collectives, shards(): pieces = lax.all_to_all(pieces, 'group', 0, 0, tiled=False)  23.4 us
    pallas_call x2, Pallas kernels, conv3d_taps(): pl.pallas_call(conv3d_kernel, grid=(3 * pairs,), in_specs=[pl.BlockSpec(r...  13.8 us
    unnamed x18, local copies, waits for them, and re-layouts  13.3 us
    ppermute x3, starting transfers between devices, shifted(): lax.ppermute(value, axis, [(source, source + steps) for source in range(f...  9.9 us
    ppermute x2, starting transfers between devices, diagonal(): return lax.ppermute(value, ('group', 'frame'), pairs)  7.26 us
    conv_general_dilated x1, matrix products, shards(): lax.conv_general_dilated(rows_all[None], kernel2, (1, 1), ((1, 1), (0, 0)...  5.54 us
  transfers between devices with their start and end apart: 5, of which 1 were waited for; matrix products, arithmetic and copies ran while one was open for 1% of the time, Pallas kernels for 4%

profile of v5, /device:TPU:1, one launch (start us, length us, event | category | flops | bytes accessed | tf_op | source)
XLA Modules:
  0.0 124.8 jit_solution(3238986287625244988)
XLA Ops:
  0.6 1.1 slice.67
  1.7 4.6 %collective-permute-start.4 = (bf16[2,1,128,384]{3,2,1,0:T(8,128)(2,1)S(1)}, bf16[2,1,128,384]{3,2,1,0:T(8,128)(2,1)S(1)}, u32[]{:S(2)}, u32[]{:S(2)}) collective-permute-start(bf16[2,1,128,384]{3,2,1,0:T(8,128)(2,1)S(1)} %slice.67), channel_id=1, source_target_pairs={{0,48},{48,96},{96,144},{144,192},{192,240},{240,288},{288,336},{3... | collective-permute-start | bytes 589832 | tf_op jit(solution)/shard_map/ppermute | solution.py:12
  6.4 4.0 %collective-permute-start.1 = (bf16[3,1,128,384]{3,2,1,0:T(8,128)(2,1)}, bf16[3,1,128,384]{3,2,1,0:T(8,128)(2,1)S(1)}, u32[]{:S(2)}, u32[]{:S(2)}) collective-permute-start(bf16[3,1,128,384]{3,2,1,0:T(8,128)(2,1)} %param.3), channel_id=1, source_target_pairs={{0,1},{1,2},{2,3},{3,4},{4,5},{5,6},{6,7},{7,8},{8,9},{9,10},{10,1... | collective-permute-start | bytes 884744 | tf_op jit(solution)/shard_map/ppermute | solution.py:12
  10.4 1.3 %collective-permute-start.3 = (bf16[3,1,128,384]{3,2,1,0:T(8,128)(2,1)}, bf16[3,1,128,384]{3,2,1,0:T(8,128)(2,1)S(1)}, u32[]{:S(2)}, u32[]{:S(2)}) collective-permute-start(bf16[3,1,128,384]{3,2,1,0:T(8,128)(2,1)} %param.3), channel_id=1, source_target_pairs={{1,0},{2,1},{3,2},{4,3},{5,4},{6,5},{7,6},{8,7},{9,8},{10,9},{11,1... | collective-permute-start | bytes 884744 | tf_op jit(solution)/shard_map/ppermute | solution.py:12
  11.7 1.3 %collective-permute-start.2 = (bf16[2,1,128,384]{3,2,1,0:T(8,128)(2,1)S(1)}, bf16[2,1,128,384]{3,2,1,0:T(8,128)(2,1)}, u32[]{:S(2)}, u32[]{:S(2)}) collective-permute-start(bf16[2,1,128,384]{3,2,1,0:T(8,128)(2,1)S(1)} %slice.67), channel_id=1, source_target_pairs={{1,48},{2,49},{3,50},{4,51},{5,52},{6,53},{7,54},{8,55},{9,56},{10... | collective-permute-start | bytes 589832 | tf_op jit(solution)/shard_map/ppermute | solution.py:23
  13.0 6.0 %collective-permute-start = (bf16[2,1,128,384]{3,2,1,0:T(8,128)(2,1)S(1)}, bf16[2,1,128,384]{3,2,1,0:T(8,128)(2,1)}, u32[]{:S(2)}, u32[]{:S(2)}) collective-permute-start(bf16[2,1,128,384]{3,2,1,0:T(8,128)(2,1)S(1)} %slice.67), channel_id=1, source_target_pairs={{0,49},{1,50},{2,51},{3,52},{4,53},{5,54},{6,55},{7,56},{8,57},{9,... | collective-permute-start | bytes 589832 | tf_op jit(solution)/shard_map/ppermute | solution.py:23
  18.9 1.8 %pad_maximum_fusion.rows_ref = bf16[5,1,128,384]{3,2,1,0:T(8,128)(2,1)} fusion(bf16[3,1,128,384]{3,2,1,0:T(8,128)(2,1)} %param.3, bf16[2,1,128,384]{3,2,1,0:T(8,128)(2,1)S(1)} %collective-permute-done.4), kind=kLoop, calls=%fused_computation.3 | loop fusion | flops 245760 | bytes 983040 | tf_op jit(solution)/shard_map/concatenate | solution.py:93
  20.8 5.3 %shard_map.50.refs_0_ = f32[3,3,128,384]{3,2,1,0:T(8,128)} custom-call(bf16[5,1,128,384]{3,2,1,0:T(8,128)(2,1)} %pad_maximum_fusion.rows_ref, bf16[3,3,3,384,384]{4,3,2,1,0:T(8,128)(2,1)} %kernel_ref.3), custom_call_target="tpu_custom_call" | custom-call | tf_op jit(solution)/shard_map/pallas_call | solution.py:71
  26.2 2.1 %maximum_maximum_fusion.rows_ref = bf16[5,2,128,384]{3,2,1,0:T(8,128)(2,1)} fusion(bf16[3,1,128,384]{3,2,1,0:T(8,128)(2,1)S(1)} %collective-permute-done.3, bf16[2,1,128,384]{3,2,1,0:T(8,128)(2,1)} %collective-permute-done.2, bf16[3,1,128,384]{3,2,1,0:T(8,128)(2,1)S(1)} %collective-permute-done.1, bf16[2,1,128,384]{3,2,1,0:T(8,128)(2,1)} %collective-permute-done), kind=kLoop, calls=%fused_computation.1 | loop fusion | flops 1474560 | bytes 1966080 | tf_op jit(solution)/shard_map/concatenate | solution.py:95
  28.3 8.5 %shard_map.51 = bf16[3,128,384]{2,1,0:T(8,128)(2,1)} custom-call(bf16[5,2,128,384]{3,2,1,0:T(8,128)(2,1)} %maximum_maximum_fusion.rows_ref, bf16[3,3,3,384,384]{4,3,2,1,0:T(8,128)(2,1)} %kernel_ref.3, f32[3,3,128,384]{3,2,1,0:T(8,128)} %shard_map.50.refs_0_), custom_call_target="tpu_custom_call" | custom-call | tf_op jit(solution)/shard_map/pallas_call | solution.py:71
  36.7 0.8 fusion.2
  37.5 0.8 fusion.18
  38.4 0.8 fusion.17
  39.2 0.8 fusion.16
  40.1 0.8 fusion.15
  40.9 0.8 fusion.14
  41.7 0.8 fusion.13
  42.6 0.8 fusion.12
  43.4 0.8 fusion.11
  44.3 0.8 fusion.10
  45.1 0.8 fusion.9
  45.9 0.8 fusion.8
  46.8 0.8 fusion.7
  47.6 0.8 fusion.6
  48.5 0.8 fusion.5
  49.3 0.8 fusion.4
  50.1 0.2 copy.16
  50.3 23.4 %all_to_all.10 = bf16[16,3,10,384]{3,1,2,0:T(4,128)(2,1)S(1)} all-to-all(bf16[16,3,10,384]{3,1,2,0:T(4,128)(2,1)S(1)} %copy.16), channel_id=1, replica_groups=mesh['group'=16,'frame'=48] {'group'}, dimensions={0} | all-to-all | bytes 737280 | tf_op jit(solution)/shard_map/all_to_all | solution.py:102
  73.7 0.1 copy.23
  73.8 44.7 %all_to_all.11 = bf16[48,10,384]{2,1,0:T(8,128)(2,1)S(1)} all-to-all(bf16[48,10,384]{2,1,0:T(8,128)(2,1)S(1)} %bitcast.71), channel_id=1, replica_groups=mesh['group'=16,'frame'=48] {'frame'}, dimensions={0} | all-to-all | bytes 737280 | tf_op jit(solution)/shard_map/all_to_all | solution.py:104
  118.5 5.5 %convolution_convert_fusion = bf16[1,48,8,384]{3,0,2,1:T(2,128)(2,1)S(1)} fusion(bf16[3,3,384,384]{3,2,1,0:T(8,128)(2,1)S(1)} %copy-done, bf16[1,48,10,384]{3,2,1,0:T(8,128)(2,1)S(1)} %bitcast.72), kind=kOutput, calls=%fused_computation | convolution fusion | flops 1005207552 | bytes 3317760 | tf_op jit(solution)/shard_map/conv_general_dilated | solution.py:105
  124.0 0.8 copy.22
  (7 shorter events, 0.1 us)
Async XLA Ops:
  0.6 117.9 %copy-start = (bf16[3,3,384,384]{3,2,1,0:T(8,128)(2,1)S(1)}, bf16[3,3,384,384]{3,2,1,0:T(8,128)(2,1)}, u32[]{:S(2)}) copy-start(bf16[3,3,384,384]{3,2,1,0:T(8,128)(2,1)} %param.5) | copy-start | bytes 7962628
  1.7 17.2 %collective-permute-start.4 = (bf16[2,1,128,384]{3,2,1,0:T(8,128)(2,1)S(1)}, bf16[2,1,128,384]{3,2,1,0:T(8,128)(2,1)S(1)}, u32[]{:S(2)}, u32[]{:S(2)}) collective-permute-start(bf16[2,1,128,384]{3,2,1,0:T(8,128)(2,1)S(1)} %slice.67), channel_id=1, source_target_pairs={{0,48},{48,96},{96,144},{144,192},{192,240},{240,288},{288,336},{3... | collective-permute-start | bytes 589832 | tf_op jit(solution)/shard_map/ppermute | solution.py:12
  6.4 19.8 %collective-permute-start.1 = (bf16[3,1,128,384]{3,2,1,0:T(8,128)(2,1)}, bf16[3,1,128,384]{3,2,1,0:T(8,128)(2,1)S(1)}, u32[]{:S(2)}, u32[]{:S(2)}) collective-permute-start(bf16[3,1,128,384]{3,2,1,0:T(8,128)(2,1)} %param.3), channel_id=1, source_target_pairs={{0,1},{1,2},{2,3},{3,4},{4,5},{5,6},{6,7},{7,8},{8,9},{9,10},{10,1... | collective-permute-start | bytes 884744 | tf_op jit(solution)/shard_map/ppermute | solution.py:12
  10.4 15.8 %collective-permute-start.3 = (bf16[3,1,128,384]{3,2,1,0:T(8,128)(2,1)}, bf16[3,1,128,384]{3,2,1,0:T(8,128)(2,1)S(1)}, u32[]{:S(2)}, u32[]{:S(2)}) collective-permute-start(bf16[3,1,128,384]{3,2,1,0:T(8,128)(2,1)} %param.3), channel_id=1, source_target_pairs={{1,0},{2,1},{3,2},{4,3},{5,4},{6,5},{7,6},{8,7},{9,8},{10,9},{11,1... | collective-permute-start | bytes 884744 | tf_op jit(solution)/shard_map/ppermute | solution.py:12
  11.7 14.5 %collective-permute-start.2 = (bf16[2,1,128,384]{3,2,1,0:T(8,128)(2,1)S(1)}, bf16[2,1,128,384]{3,2,1,0:T(8,128)(2,1)}, u32[]{:S(2)}, u32[]{:S(2)}) collective-permute-start(bf16[2,1,128,384]{3,2,1,0:T(8,128)(2,1)S(1)} %slice.67), channel_id=1, source_target_pairs={{1,48},{2,49},{3,50},{4,51},{5,52},{6,53},{7,54},{8,55},{9,56},{10... | collective-permute-start | bytes 589832 | tf_op jit(solution)/shard_map/ppermute | solution.py:23
  13.0 13.2 %collective-permute-start = (bf16[2,1,128,384]{3,2,1,0:T(8,128)(2,1)S(1)}, bf16[2,1,128,384]{3,2,1,0:T(8,128)(2,1)}, u32[]{:S(2)}, u32[]{:S(2)}) collective-permute-start(bf16[2,1,128,384]{3,2,1,0:T(8,128)(2,1)S(1)} %slice.67), channel_id=1, source_target_pairs={{0,49},{1,50},{2,51},{3,52},{4,53},{5,54},{6,55},{7,56},{8,57},{9,... | collective-permute-start | bytes 589832 | tf_op jit(solution)/shard_map/ppermute | solution.py:23

commit v6 on v3

--- a/solution.py
+++ b/solution.py
@@ -77,37 +77,6 @@
     return left + acc[1] + right
 
 
-def critic_kernel(cols_ref, kernel_ref, out_ref):
-    width = out_ref.shape[1]
-    rows, channels = cols_ref.shape[1:]
-    total = None
-    for c in range(3):
-        lhs = cols_ref[c : c + width].reshape(width * rows, channels)
-        part = jnp.dot(lhs, kernel_ref[0, c], preferred_element_type=jnp.float32)
-        total = part if total is None else total + part
-    out_ref[0] = total.reshape(width, rows, channels)
-
-
-def critic_conv(cols, kernel2):
-    span, rows, channels = cols.shape
-    width = span - 2
-    acc = pl.pallas_call(
-        critic_kernel,
-        grid=(3,),
-        in_specs=[
-            pl.BlockSpec(cols.shape, lambda s: (0, 0, 0)),
-            pl.BlockSpec((1, 3, channels, channels), lambda s: (s, 0, 0, 0)),
-        ],
-        out_specs=pl.BlockSpec((1, width, rows, channels), lambda s: (s, 0, 0, 0)),
-        out_shape=jax.ShapeDtypeStruct((3, width, rows, channels), jnp.float32),
-    )(cols, kernel2)
-    zero = jnp.zeros((width, 1, channels), jnp.float32)
-    above = jnp.concatenate([zero, acc[0, :, :-1]], axis=1)
-    below = jnp.concatenate([acc[2, :, 1:], zero], axis=1)
-    total = above + acc[1] + below
-    return jnp.transpose(total, (1, 0, 2)).astype(jnp.bfloat16)
-
-
 def shards(video, kernel3, kernel2):
     length, _, width, channels = video.shape
     groups = lax.axis_size("group")
@@ -128,9 +97,16 @@
     pieces = jnp.stack([padded[:, j * block : j * block + block + 2] for j in range(groups)], 0)
     pieces = lax.all_to_all(pieces, "group", 0, 0, tiled=False)
     pieces = pieces.reshape(groups * length, block + 2, channels)
-    cols = lax.all_to_all(pieces, "frame", 0, 1, tiled=False)
-    critic = critic_conv(cols, kernel2)
-    return features[:, None], critic[None]
+    rows_all = lax.all_to_all(pieces, "frame", 0, 0, tiled=True)
+    critic = lax.conv_general_dilated(
+        rows_all[None],
+        kernel2,
+        (1, 1),
+        ((1, 1), (0, 0)),
+        dimension_numbers=("NHWC", "HWIO", "NHWC"),
+        preferred_element_type=jnp.float32,
+    ).astype(jnp.bfloat16)
+    return features[:, None], critic
 
 
 def solution(mesh):

time: 117 us -> 115 us (0.983)
  matrix products: 0 us -> 5.54 us
  Pallas kernels: 18.9 us -> 13.9 us
  local copies, waits for them, and re-layouts: 5.78 us -> 3.79 us
    conv_general_dilated x0 -> x1, matrix products: none -> 5.54 us  [shards(): lax.conv_general_dilated(rows_all[None], kernel2, (1, 1), ((1, 1), (0, 0)...]
    pallas_call x1 -> x0, Pallas kernels: 4.91 us -> none  [critic_conv(): pl.pallas_call(critic_kernel, grid=(3,), in_specs=[pl.BlockSpec(cols.shap...]
    squeeze x1 -> x0, local copies, waits for them, and re-layouts: 1.32 us -> none  [critic_conv(): above = jnp.concatenate([zero, acc[0, :, :-1]], axis=1)]
  transfers between devices with their start and end apart: 5 -> 5, of which waited for: 1 -> 1; matrix products, arithmetic and copies ran while one was open for 2% -> 2% of each run, Pallas kernels for 4% -> 5%
where the time goes in v6:
time: 115 us
  blocking collectives  68.1 us (59%)
  starting transfers between devices  17.2 us (15%)
  Pallas kernels  13.9 us (12%)
  matrix products  5.54 us (5%)
  other arithmetic  5.23 us (5%)
  local copies, waits for them, and re-layouts  3.79 us (3%)
    all_to_all x1, blocking collectives, shards(): rows_all = lax.all_to_all(pieces, 'frame', 0, 0, tiled=True)  44.7 us
    all_to_all x1, blocking collectives, shards(): pieces = lax.all_to_all(pieces, 'group', 0, 0, tiled=False)  23.4 us
    pallas_call x2, Pallas kernels, conv3d_taps(): pl.pallas_call(conv3d_kernel, grid=(3 * pairs,), in_specs=[pl.BlockSpec(r...  13.9 us
    ppermute x3, starting transfers between devices, shifted(): lax.ppermute(value, axis, [(source, source + steps) for source in range(f...  9.9 us
    ppermute x2, starting transfers between devices, diagonal(): return lax.ppermute(value, ('group', 'frame'), pairs)  7.27 us
    conv_general_dilated x1, matrix products, shards(): lax.conv_general_dilated(rows_all[None], kernel2, (1, 1), ((1, 1), (0, 0)...  5.54 us
  transfers between devices with their start and end apart: 5, of which 1 were waited for; matrix products, arithmetic and copies ran while one was open for 2% of the time, Pallas kernels for 5%

profile of v6, /device:TPU:1, one launch (start us, length us, event | category | flops | bytes accessed | tf_op | source)
XLA Modules:
  0.0 114.7 jit_solution(16628385304107604022)
XLA Ops:
  0.6 0.0 copy-start
  0.6 1.1 slice.76
  1.7 4.6 %collective-permute-start.4 = (bf16[2,1,128,384]{3,2,1,0:T(8,128)(2,1)S(1)}, bf16[2,1,128,384]{3,2,1,0:T(8,128)(2,1)S(1)}, u32[]{:S(2)}, u32[]{:S(2)}) collective-permute-start(bf16[2,1,128,384]{3,2,1,0:T(8,128)(2,1)S(1)} %slice.76), channel_id=1, source_target_pairs={{0,48},{48,96},{96,144},{144,192},{192,240},{240,288},{288,336},{3... | collective-permute-start | bytes 589832 | tf_op jit(solution)/shard_map/ppermute | solution.py:11
  6.4 4.0 %collective-permute-start.1 = (bf16[3,1,128,384]{3,2,1,0:T(8,128)(2,1)}, bf16[3,1,128,384]{3,2,1,0:T(8,128)(2,1)S(1)}, u32[]{:S(2)}, u32[]{:S(2)}) collective-permute-start(bf16[3,1,128,384]{3,2,1,0:T(8,128)(2,1)} %param.3), channel_id=1, source_target_pairs={{0,1},{1,2},{2,3},{3,4},{4,5},{5,6},{6,7},{7,8},{8,9},{9,10},{10,1... | collective-permute-start | bytes 884744 | tf_op jit(solution)/shard_map/ppermute | solution.py:11
  10.4 1.3 %collective-permute-start.3 = (bf16[3,1,128,384]{3,2,1,0:T(8,128)(2,1)}, bf16[3,1,128,384]{3,2,1,0:T(8,128)(2,1)S(1)}, u32[]{:S(2)}, u32[]{:S(2)}) collective-permute-start(bf16[3,1,128,384]{3,2,1,0:T(8,128)(2,1)} %param.3), channel_id=1, source_target_pairs={{1,0},{2,1},{3,2},{4,3},{5,4},{6,5},{7,6},{8,7},{9,8},{10,9},{11,1... | collective-permute-start | bytes 884744 | tf_op jit(solution)/shard_map/ppermute | solution.py:11
  11.7 1.3 %collective-permute-start.2 = (bf16[2,1,128,384]{3,2,1,0:T(8,128)(2,1)S(1)}, bf16[2,1,128,384]{3,2,1,0:T(8,128)(2,1)}, u32[]{:S(2)}, u32[]{:S(2)}) collective-permute-start(bf16[2,1,128,384]{3,2,1,0:T(8,128)(2,1)S(1)} %slice.76), channel_id=1, source_target_pairs={{1,48},{2,49},{3,50},{4,51},{5,52},{6,53},{7,54},{8,55},{9,56},{10... | collective-permute-start | bytes 589832 | tf_op jit(solution)/shard_map/ppermute | solution.py:22
  13.0 6.0 %collective-permute-start = (bf16[2,1,128,384]{3,2,1,0:T(8,128)(2,1)S(1)}, bf16[2,1,128,384]{3,2,1,0:T(8,128)(2,1)}, u32[]{:S(2)}, u32[]{:S(2)}) collective-permute-start(bf16[2,1,128,384]{3,2,1,0:T(8,128)(2,1)S(1)} %slice.76), channel_id=1, source_target_pairs={{0,49},{1,50},{2,51},{3,52},{4,53},{5,54},{6,55},{7,56},{8,57},{9,... | collective-permute-start | bytes 589832 | tf_op jit(solution)/shard_map/ppermute | solution.py:22
  18.9 0.0 collective-permute-done.4
  19.0 1.8 %pad_maximum_fusion.rows_ref = bf16[5,1,128,384]{3,2,1,0:T(8,128)(2,1)} fusion(bf16[3,1,128,384]{3,2,1,0:T(8,128)(2,1)} %param.3, bf16[2,1,128,384]{3,2,1,0:T(8,128)(2,1)S(1)} %collective-permute-done.4), kind=kLoop, calls=%fused_computation.9 | loop fusion | flops 245760 | bytes 983040 | tf_op jit(solution)/shard_map/concatenate | solution.py:88
  20.8 5.2 %shard_map.50.refs_0_ = f32[3,3,128,384]{3,2,1,0:T(8,128)} custom-call(bf16[5,1,128,384]{3,2,1,0:T(8,128)(2,1)} %pad_maximum_fusion.rows_ref, bf16[3,3,3,384,384]{4,3,2,1,0:T(8,128)(2,1)} %kernel_ref.3), custom_call_target="tpu_custom_call" | custom-call | tf_op jit(solution)/shard_map/pallas_call | solution.py:58
  26.0 0.2 collective-permute-done.2
  26.2 0.0 collective-permute-done
  26.2 0.0 collective-permute-done.1
  26.2 0.0 collective-permute-done.3
  26.2 2.1 %maximum_maximum_fusion.rows_ref = bf16[5,2,128,384]{3,2,1,0:T(8,128)(2,1)} fusion(bf16[3,1,128,384]{3,2,1,0:T(8,128)(2,1)S(1)} %collective-permute-done.3, bf16[2,1,128,384]{3,2,1,0:T(8,128)(2,1)} %collective-permute-done.2, bf16[3,1,128,384]{3,2,1,0:T(8,128)(2,1)S(1)} %collective-permute-done.1, bf16[2,1,128,384]{3,2,1,0:T(8,128)(2,1)} %collective-permute-done), kind=kLoop, calls=%fused_computation.1 | loop fusion | flops 1474560 | bytes 1966080 | tf_op jit(solution)/shard_map/concatenate | solution.py:90
  28.3 8.7 %shard_map.51 = f32[3,3,128,384]{3,2,1,0:T(8,128)} custom-call(bf16[5,2,128,384]{3,2,1,0:T(8,128)(2,1)} %maximum_maximum_fusion.rows_ref, bf16[3,3,3,384,384]{4,3,2,1,0:T(8,128)(2,1)} %kernel_ref.3, f32[3,3,128,384]{3,2,1,0:T(8,128)} %shard_map.50.refs_0_), custom_call_target="tpu_custom_call", output_to_operand_aliasing={{}: (2, {})} | custom-call | tf_op jit(solution)/shard_map/pallas_call | solution.py:58
  37.0 1.3 %slice_bitcast_fusion.2 = (f32[3,127,384]{2,1,0:T(8,128)S(1)}, f32[3,127,384]{2,1,0:T(8,128)S(1)}) fusion(f32[3,3,128,384]{3,2,1,0:T(8,128)} %shard_map.51), kind=kLoop, calls=%fused_computation.7 | loop fusion | bytes 2340864 | tf_op jit(solution)/shard_map/squeeze | solution.py:75
  38.4 1.3 %multiply_convert_fusion = bf16[3,128,384]{2,1,0:T(8,128)(2,1)S(1)} fusion(f32[3,3,128,384]{3,2,1,0:T(8,128)} %shard_map.51, f32[3,127,384]{2,1,0:T(8,128)S(1)} %get-tuple-element.11, f32[3,127,384]{2,1,0:T(8,128)S(1)} %get-tuple-element.10), kind=kLoop, calls=%fused_computation.8 | loop fusion | flops 1032192 | bytes 2055168 | tf_op jit(solution)/shard_map/convert_element_type | solution.py:94
  39.6 0.0 copy-start.1
  40.0 0.2 copy.17
  40.2 23.4 %all_to_all.10 = bf16[16,3,10,384]{3,1,2,0:T(4,128)(2,1)S(1)} all-to-all(bf16[16,3,10,384]{3,1,2,0:T(4,128)(2,1)S(1)} %copy.17), channel_id=1, replica_groups=mesh['group'=16,'frame'=48] {'group'}, dimensions={0} | all-to-all | bytes 737280 | tf_op jit(solution)/shard_map/all_to_all | solution.py:98
  63.6 0.1 copy.24
  63.7 44.7 %all_to_all.11 = bf16[48,10,384]{2,1,0:T(8,128)(2,1)S(1)} all-to-all(bf16[48,10,384]{2,1,0:T(8,128)(2,1)S(1)} %bitcast.83), channel_id=1, replica_groups=mesh['group'=16,'frame'=48] {'frame'}, dimensions={0} | all-to-all | bytes 737280 | tf_op jit(solution)/shard_map/all_to_all | solution.py:100
  108.4 0.0 copy-done.1
  108.4 0.0 copy-done
  108.4 5.5 %convolution_convert_fusion = bf16[1,48,8,384]{3,0,2,1:T(2,128)(2,1)S(1)} fusion(bf16[3,3,384,384]{3,2,1,0:T(8,128)(2,1)S(1)} %copy-done, bf16[1,48,10,384]{3,2,1,0:T(8,128)(2,1)S(1)} %bitcast.84), kind=kOutput, calls=%fused_computation | convolution fusion | flops 1005207552 | bytes 3317760 | tf_op jit(solution)/shard_map/conv_general_dilated | solution.py:101
  114.0 0.8 copy.23
  (16 shorter events, 0.3 us)
Async XLA Ops:
  0.6 107.8 %copy-start = (bf16[3,3,384,384]{3,2,1,0:T(8,128)(2,1)S(1)}, bf16[3,3,384,384]{3,2,1,0:T(8,128)(2,1)}, u32[]{:S(2)}) copy-start(bf16[3,3,384,384]{3,2,1,0:T(8,128)(2,1)} %param.5) | copy-start | bytes 7962628
  1.7 17.2 %collective-permute-start.4 = (bf16[2,1,128,384]{3,2,1,0:T(8,128)(2,1)S(1)}, bf16[2,1,128,384]{3,2,1,0:T(8,128)(2,1)S(1)}, u32[]{:S(2)}, u32[]{:S(2)}) collective-permute-start(bf16[2,1,128,384]{3,2,1,0:T(8,128)(2,1)S(1)} %slice.76), channel_id=1, source_target_pairs={{0,48},{48,96},{96,144},{144,192},{192,240},{240,288},{288,336},{3... | collective-permute-start | bytes 589832 | tf_op jit(solution)/shard_map/ppermute | solution.py:11
  6.4 19.8 %collective-permute-start.1 = (bf16[3,1,128,384]{3,2,1,0:T(8,128)(2,1)}, bf16[3,1,128,384]{3,2,1,0:T(8,128)(2,1)S(1)}, u32[]{:S(2)}, u32[]{:S(2)}) collective-permute-start(bf16[3,1,128,384]{3,2,1,0:T(8,128)(2,1)} %param.3), channel_id=1, source_target_pairs={{0,1},{1,2},{2,3},{3,4},{4,5},{5,6},{6,7},{7,8},{8,9},{9,10},{10,1... | collective-permute-start | bytes 884744 | tf_op jit(solution)/shard_map/ppermute | solution.py:11
  10.4 15.8 %collective-permute-start.3 = (bf16[3,1,128,384]{3,2,1,0:T(8,128)(2,1)}, bf16[3,1,128,384]{3,2,1,0:T(8,128)(2,1)S(1)}, u32[]{:S(2)}, u32[]{:S(2)}) collective-permute-start(bf16[3,1,128,384]{3,2,1,0:T(8,128)(2,1)} %param.3), channel_id=1, source_target_pairs={{1,0},{2,1},{3,2},{4,3},{5,4},{6,5},{7,6},{8,7},{9,8},{10,9},{11,1... | collective-permute-start | bytes 884744 | tf_op jit(solution)/shard_map/ppermute | solution.py:11
  11.7 14.5 %collective-permute-start.2 = (bf16[2,1,128,384]{3,2,1,0:T(8,128)(2,1)S(1)}, bf16[2,1,128,384]{3,2,1,0:T(8,128)(2,1)}, u32[]{:S(2)}, u32[]{:S(2)}) collective-permute-start(bf16[2,1,128,384]{3,2,1,0:T(8,128)(2,1)S(1)} %slice.76), channel_id=1, source_target_pairs={{1,48},{2,49},{3,50},{4,51},{5,52},{6,53},{7,54},{8,55},{9,56},{10... | collective-permute-start | bytes 589832 | tf_op jit(solution)/shard_map/ppermute | solution.py:22
  13.0 13.2 %collective-permute-start = (bf16[2,1,128,384]{3,2,1,0:T(8,128)(2,1)S(1)}, bf16[2,1,128,384]{3,2,1,0:T(8,128)(2,1)}, u32[]{:S(2)}, u32[]{:S(2)}) collective-permute-start(bf16[2,1,128,384]{3,2,1,0:T(8,128)(2,1)S(1)} %slice.76), channel_id=1, source_target_pairs={{0,49},{1,50},{2,51},{3,52},{4,53},{5,54},{6,55},{7,56},{8,57},{9,... | collective-permute-start | bytes 589832 | tf_op jit(solution)/shard_map/ppermute | solution.py:22
  39.6 68.8 %copy-start.1 = (bf16[3,128,384]{2,1,0:T(8,128)(2,1)}, bf16[3,128,384]{2,1,0:T(8,128)(2,1)S(1)}, u32[]{:S(2)}) copy-start(bf16[3,128,384]{2,1,0:T(8,128)(2,1)S(1)} %multiply_convert_fusion) | copy-start | bytes 884740

commit v7 on v6

--- a/solution.py
+++ b/solution.py
@@ -2,6 +2,7 @@
 import jax.numpy as jnp
 from jax import lax
 from jax.experimental import pallas as pl
+from jax.experimental.pallas import tpu as pltpu
 from jax.sharding import PartitionSpec as P
 
 
@@ -77,21 +78,53 @@
     return left + acc[1] + right
 
 
+def row_partials_kernel(rows_ref, kernel_ref, out_ref, acc_ref):
+    step = pl.program_id(0)
+    tap = step % 3
+    frames, width, channels = out_ref.shape[1:]
+
+    @pl.when(tap == 0)
+    def _():
+        acc_ref[...] = jnp.zeros_like(acc_ref)
+
+    lhs = rows_ref[pl.ds(tap, frames), 0].reshape(frames * width, channels)
+    for c in range(3):
+        part = jnp.dot(lhs, kernel_ref[0, 0, c], preferred_element_type=jnp.float32)
+        acc_ref[c] += part.reshape(frames, width, channels)
+
+    @pl.when(tap == 2)
+    def _():
+        column = lax.broadcasted_iota(jnp.int32, (frames, width, channels), 1)
+        left = jnp.where(column == 0, 0.0, pltpu.roll(acc_ref[0], 1, 1))
+        right = jnp.where(column == width - 1, 0.0, pltpu.roll(acc_ref[2], width - 1, 1))
+        out_ref[0] = left + acc_ref[1] + right
+
+
+def row_partials(rows, kernel3):
+    frames, _, width, channels = rows.shape
+    count = frames - 2
+    return pl.pallas_call(
+        row_partials_kernel,
+        grid=(9,),
+        in_specs=[
+            pl.BlockSpec(rows.shape, lambda s: (0, 0, 0, 0)),
+            pl.BlockSpec((1, 1, 3, channels, channels), lambda s: (s % 3, s // 3, 0, 0, 0)),
+        ],
+        out_specs=pl.BlockSpec((1, count, width, channels), lambda s: (s // 3, 0, 0, 0)),
+        out_shape=jax.ShapeDtypeStruct((3, count, width, channels), jnp.float32),
+        scratch_shapes=[pltpu.VMEM((3, count, width, channels), jnp.float32)],
+    )(rows, kernel3)
+
+
 def shards(video, kernel3, kernel2):
     length, _, width, channels = video.shape
     groups = lax.axis_size("group")
     cached = shifted(video[length - 2 :], "group", 1)
-    above = shifted(video, "frame", 1)
-    below = shifted(video, "frame", -1)
-    cached_above = diagonal(video[length - 2 :], 1, 1)
-    cached_below = diagonal(video[length - 2 :], 1, -1)
-    centre = jnp.concatenate([cached, video], 0)
-    acc = conv3d_taps(centre, kernel3, (1,))
-    edges = jnp.concatenate(
-        [jnp.concatenate([cached_above, above], 0), jnp.concatenate([cached_below, below], 0)], 1
-    )
-    acc = conv3d_taps(edges, kernel3, (0, 2), acc)
-    features = jax.nn.silu(column_sum(acc)).astype(jnp.bfloat16)
+    partials = row_partials(jnp.concatenate([cached, video], 0), kernel3)
+    from_above = shifted(partials[0].astype(jnp.bfloat16), "frame", 1)
+    from_below = shifted(partials[2].astype(jnp.bfloat16), "frame", -1)
+    conv = partials[1] + from_above.astype(jnp.float32) + from_below.astype(jnp.float32)
+    features = jax.nn.silu(conv).astype(jnp.bfloat16)
     block = width // groups
     padded = jnp.pad(features, ((0, 0), (1, 1), (0, 0)))
     pieces = jnp.stack([padded[:, j * block : j * block + block + 2] for j in range(groups)], 0)

time: 115 us -> 116 us (level)
  waiting for transfers between devices: 0.17 us -> 17.2 us
  starting transfers between devices: 17.2 us -> 7.19 us
  Pallas kernels: 13.9 us -> 11.2 us
  blocking collectives: 68.1 us -> 66.8 us
  local copies, waits for them, and re-layouts: 3.79 us -> 2.53 us
    ppermute x3, waiting for transfers between devices: 0.01 us -> 17.2 us  [shifted(): lax.ppermute(value, axis, [(source, source + steps) for source in range(f...]
    ppermute x2 -> x0, starting transfers between devices: 7.27 us -> none  [diagonal(): return lax.ppermute(value, ('group', 'frame'), pairs)]
    pallas_call x2 -> x1, Pallas kernels: 13.9 us -> 11.2 us  [row_partials(): pl.pallas_call(row_partials_kernel, grid=(9,), in_specs=[pl.BlockSpec(row...]
    ppermute x3, starting transfers between devices: 9.9 us -> 7.19 us  [shifted(): lax.ppermute(value, axis, [(source, source + steps) for source in range(f...]
    concatenate x2 -> x1, other arithmetic: 3.96 us -> 1.82 us  [shards(): partials = row_partials(jnp.concatenate([cached, video], 0), kernel3)]
    another operation x0 -> x1, other arithmetic: none -> 1.58 us
    squeeze x1 -> x0, local copies, waits for them, and re-layouts: 1.32 us -> none  [column_sum(): left = jnp.concatenate([zero, acc[0, :, :-1]], axis=1)]
    all_to_all x1, blocking collectives: 23.4 us -> 22.1 us  [shards(): pieces = lax.all_to_all(pieces, 'group', 0, 0, tiled=False)]
  transfers between devices with their start and end apart: 5 -> 3, of which waited for: 1 -> 3; matrix products, arithmetic and copies ran while one was open for 2% -> 0% of each run, Pallas kernels for 5% -> 0%
where the time goes in v7:
time: 116 us
  blocking collectives  66.8 us (58%)
  waiting for transfers between devices  17.2 us (15%)
  Pallas kernels  11.2 us (10%)
  starting transfers between devices  7.19 us (6%)
  matrix products  5.54 us (5%)
  other arithmetic  4.66 us (4%)
  local copies, waits for them, and re-layouts  2.53 us (2%)
    all_to_all x1, blocking collectives, shards(): rows_all = lax.all_to_all(pieces, 'frame', 0, 0, tiled=True)  44.7 us
    all_to_all x1, blocking collectives, shards(): pieces = lax.all_to_all(pieces, 'group', 0, 0, tiled=False)  22.1 us
    ppermute x3, waiting for transfers between devices, shifted(): lax.ppermute(value, axis, [(source, source + steps) for source in range(f...  17.2 us
    pallas_call x1, Pallas kernels, row_partials(): pl.pallas_call(row_partials_kernel, grid=(9,), in_specs=[pl.BlockSpec(row...  11.2 us
    ppermute x3, starting transfers between devices, shifted(): lax.ppermute(value, axis, [(source, source + steps) for source in range(f...  7.19 us
    conv_general_dilated x1, matrix products, shards(): lax.conv_general_dilated(rows_all[None], kernel2, (1, 1), ((1, 1), (0, 0)...  5.54 us
  transfers between devices with their start and end apart: 3, of which 3 were waited for; matrix products, arithmetic and copies ran while one was open for 0% of the time, Pallas kernels for 0%

profile of v7, /device:TPU:1, one launch (start us, length us, event | category | flops | bytes accessed | tf_op | source)
XLA Modules:
  0.0 115.9 jit_solution(17234553755164190575)
XLA Ops:
  0.6 0.0 copy-start
  0.6 1.1 slice.76
  1.7 4.6 %collective-permute-start = (bf16[2,1,128,384]{3,2,1,0:T(8,128)(2,1)S(1)}, bf16[2,1,128,384]{3,2,1,0:T(8,128)(2,1)S(1)}, u32[]{:S(2)}, u32[]{:S(2)}) collective-permute-start(bf16[2,1,128,384]{3,2,1,0:T(8,128)(2,1)S(1)} %slice.76), channel_id=1, source_target_pairs={{0,48},{48,96},{96,144},{144,192},{192,240},{240,288},{288,336},{3... | collective-permute-start | bytes 589832 | tf_op jit(solution)/shard_map/ppermute | solution.py:12
  6.4 8.1 %collective-permute-done = bf16[2,1,128,384]{3,2,1,0:T(8,128)(2,1)S(1)} collective-permute-done((bf16[2,1,128,384]{3,2,1,0:T(8,128)(2,1)S(1)}, bf16[2,1,128,384]{3,2,1,0:T(8,128)(2,1)S(1)}, u32[]{:S(2)}, u32[]{:S(2)}) %collective-permute-start) | collective-permute-done | bytes 196640 | tf_op jit(solution)/shard_map/ppermute | solution.py:12
  14.5 1.8 %pad_maximum_fusion.rows_ref = bf16[5,1,128,384]{3,2,1,0:T(8,128)(2,1)} fusion(bf16[3,1,128,384]{3,2,1,0:T(8,128)(2,1)} %param.3, bf16[2,1,128,384]{3,2,1,0:T(8,128)(2,1)S(1)} %collective-permute-done), kind=kLoop, calls=%fused_computation.6 | loop fusion | flops 245760 | bytes 983040 | tf_op jit(solution)/shard_map/concatenate | solution.py:123
  16.3 11.2 %shard_map.50 = f32[3,3,128,384]{3,2,1,0:T(8,128)} custom-call(bf16[5,1,128,384]{3,2,1,0:T(8,128)(2,1)} %pad_maximum_fusion.rows_ref, bf16[3,3,3,384,384]{4,3,2,1,0:T(8,128)(2,1)} %kernel_ref.1), custom_call_target="tpu_custom_call" | custom-call | tf_op jit(solution)/shard_map/pallas_call | solution.py:106
  27.5 1.6 %convert.4 = bf16[3,3,128,384]{3,2,1,0:T(8,128)(2,1)S(1)} convert(f32[3,3,128,384]{3,2,1,0:T(8,128)} %shard_map.50) | non-fusion elementwise | flops 442368 | bytes 2654208 | tf_op jit(solution)/shard_map/convert.1
  29.0 0.1 slice_bitcast_fusion.2
  29.1 1.3 %collective-permute-start.1 = (bf16[3,128,384]{2,1,0:T(8,128)(2,1)S(1)}, bf16[3,128,384]{2,1,0:T(8,128)(2,1)S(1)}, u32[]{:S(2)}, u32[]{:S(2)}) collective-permute-start(bf16[3,128,384]{2,1,0:T(8,128)(2,1)S(1)} %get-tuple-element.10), channel_id=1, source_target_pairs={{0,1},{1,2},{2,3},{3,4},{4,5},{5,6},{6,7},{7,8},{8,9},{9,10},{10,1... | collective-permute-start | bytes 884744 | tf_op jit(solution)/shard_map/ppermute | solution.py:12
  30.4 1.3 %collective-permute-start.2 = (bf16[3,128,384]{2,1,0:T(8,128)(2,1)S(1)}, bf16[3,128,384]{2,1,0:T(8,128)(2,1)S(1)}, u32[]{:S(2)}, u32[]{:S(2)}) collective-permute-start(bf16[3,128,384]{2,1,0:T(8,128)(2,1)S(1)} %get-tuple-element.11), channel_id=1, source_target_pairs={{1,0},{2,1},{3,2},{4,3},{5,4},{6,5},{7,6},{8,7},{9,8},{10,9},{11,1... | collective-permute-start | bytes 884744 | tf_op jit(solution)/shard_map/ppermute | solution.py:12
  31.7 5.2 %collective-permute-done.1 = bf16[3,128,384]{2,1,0:T(8,128)(2,1)S(1)} collective-permute-done((bf16[3,128,384]{2,1,0:T(8,128)(2,1)S(1)}, bf16[3,128,384]{2,1,0:T(8,128)(2,1)S(1)}, u32[]{:S(2)}, u32[]{:S(2)}) %collective-permute-start.1) | collective-permute-done | bytes 294944 | tf_op jit(solution)/shard_map/ppermute | solution.py:12
  36.9 3.9 %collective-permute-done.2 = bf16[3,128,384]{2,1,0:T(8,128)(2,1)S(1)} collective-permute-done((bf16[3,128,384]{2,1,0:T(8,128)(2,1)S(1)}, bf16[3,128,384]{2,1,0:T(8,128)(2,1)S(1)}, u32[]{:S(2)}, u32[]{:S(2)}) %collective-permute-start.2) | collective-permute-done | bytes 294944 | tf_op jit(solution)/shard_map/ppermute | solution.py:12
  40.8 1.3 %multiply_convert_fusion = bf16[3,128,384]{2,1,0:T(8,128)(2,1)S(1)} fusion(f32[3,3,128,384]{3,2,1,0:T(8,128)} %shard_map.50, bf16[3,128,384]{2,1,0:T(8,128)(2,1)S(1)} %collective-permute-done.2, bf16[3,128,384]{2,1,0:T(8,128)(2,1)S(1)} %collective-permute-done.1), kind=kLoop, calls=%fused_computation.5 | loop fusion | flops 1327104 | bytes 1474560 | tf_op jit(solution)/shard_map/convert_element_type | solution.py:127
  42.1 0.0 copy-start.1
  42.5 0.2 copy.16
  42.7 22.1 %all_to_all.10 = bf16[16,3,10,384]{3,1,2,0:T(4,128)(2,1)S(1)} all-to-all(bf16[16,3,10,384]{3,1,2,0:T(4,128)(2,1)S(1)} %copy.16), channel_id=1, replica_groups=mesh['group'=16,'frame'=48] {'group'}, dimensions={0} | all-to-all | bytes 737280 | tf_op jit(solution)/shard_map/all_to_all | solution.py:131
  64.8 0.1 copy.23
  64.9 44.7 %all_to_all.11 = bf16[48,10,384]{2,1,0:T(8,128)(2,1)S(1)} all-to-all(bf16[48,10,384]{2,1,0:T(8,128)(2,1)S(1)} %bitcast.83), channel_id=1, replica_groups=mesh['group'=16,'frame'=48] {'frame'}, dimensions={0} | all-to-all | bytes 737280 | tf_op jit(solution)/shard_map/all_to_all | solution.py:133
  109.6 0.0 copy-done.1
  109.6 0.0 copy-done
  109.6 5.5 %convolution_convert_fusion = bf16[1,48,8,384]{3,0,2,1:T(2,128)(2,1)S(1)} fusion(bf16[3,3,384,384]{3,2,1,0:T(8,128)(2,1)S(1)} %copy-done, bf16[1,48,10,384]{3,2,1,0:T(8,128)(2,1)S(1)} %bitcast.84), kind=kOutput, calls=%fused_computation | convolution fusion | flops 1005207552 | bytes 3317760 | tf_op jit(solution)/shard_map/conv_general_dilated | solution.py:134
  115.1 0.8 copy.22
  (16 shorter events, 0.3 us)
Async XLA Ops:
  0.6 108.9 %copy-start = (bf16[3,3,384,384]{3,2,1,0:T(8,128)(2,1)S(1)}, bf16[3,3,384,384]{3,2,1,0:T(8,128)(2,1)}, u32[]{:S(2)}) copy-start(bf16[3,3,384,384]{3,2,1,0:T(8,128)(2,1)} %param.5) | copy-start | bytes 7962628
  1.7 12.7 %collective-permute-start = (bf16[2,1,128,384]{3,2,1,0:T(8,128)(2,1)S(1)}, bf16[2,1,128,384]{3,2,1,0:T(8,128)(2,1)S(1)}, u32[]{:S(2)}, u32[]{:S(2)}) collective-permute-start(bf16[2,1,128,384]{3,2,1,0:T(8,128)(2,1)S(1)} %slice.76), channel_id=1, source_target_pairs={{0,48},{48,96},{96,144},{144,192},{192,240},{240,288},{288,336},{3... | collective-permute-start | bytes 589832 | tf_op jit(solution)/shard_map/ppermute | solution.py:12
  29.1 7.8 %collective-permute-start.1 = (bf16[3,128,384]{2,1,0:T(8,128)(2,1)S(1)}, bf16[3,128,384]{2,1,0:T(8,128)(2,1)S(1)}, u32[]{:S(2)}, u32[]{:S(2)}) collective-permute-start(bf16[3,128,384]{2,1,0:T(8,128)(2,1)S(1)} %get-tuple-element.10), channel_id=1, source_target_pairs={{0,1},{1,2},{2,3},{3,4},{4,5},{5,6},{6,7},{7,8},{8,9},{9,10},{10,1... | collective-permute-start | bytes 884744 | tf_op jit(solution)/shard_map/ppermute | solution.py:12
  30.4 10.4 %collective-permute-start.2 = (bf16[3,128,384]{2,1,0:T(8,128)(2,1)S(1)}, bf16[3,128,384]{2,1,0:T(8,128)(2,1)S(1)}, u32[]{:S(2)}, u32[]{:S(2)}) collective-permute-start(bf16[3,128,384]{2,1,0:T(8,128)(2,1)S(1)} %get-tuple-element.11), channel_id=1, source_target_pairs={{1,0},{2,1},{3,2},{4,3},{5,4},{6,5},{7,6},{8,7},{9,8},{10,9},{11,1... | collective-permute-start | bytes 884744 | tf_op jit(solution)/shard_map/ppermute | solution.py:12
  42.1 67.5 %copy-start.1 = (bf16[3,128,384]{2,1,0:T(8,128)(2,1)}, bf16[3,128,384]{2,1,0:T(8,128)(2,1)S(1)}, u32[]{:S(2)}) copy-start(bf16[3,128,384]{2,1,0:T(8,128)(2,1)S(1)} %multiply_convert_fusion) | copy-start | bytes 884740

commit v8 on v7

--- a/solution.py
+++ b/solution.py
@@ -100,18 +100,19 @@
         out_ref[0] = left + acc_ref[1] + right
 
 
-def row_partials(rows, kernel3):
+def row_partials(rows, kernel3, row_taps):
     frames, _, width, channels = rows.shape
     count = frames - 2
+    first, stride = row_taps[0], (row_taps[-1] - row_taps[0]) if len(row_taps) > 1 else 0
     return pl.pallas_call(
         row_partials_kernel,
-        grid=(9,),
+        grid=(3 * len(row_taps),),
         in_specs=[
             pl.BlockSpec(rows.shape, lambda s: (0, 0, 0, 0)),
-            pl.BlockSpec((1, 1, 3, channels, channels), lambda s: (s % 3, s // 3, 0, 0, 0)),
+            pl.BlockSpec((1, 1, 3, channels, channels), lambda s: (s % 3, first + stride * (s // 3), 0, 0, 0)),
         ],
         out_specs=pl.BlockSpec((1, count, width, channels), lambda s: (s // 3, 0, 0, 0)),
-        out_shape=jax.ShapeDtypeStruct((3, count, width, channels), jnp.float32),
+        out_shape=jax.ShapeDtypeStruct((len(row_taps), count, width, channels), jnp.float32),
         scratch_shapes=[pltpu.VMEM((3, count, width, channels), jnp.float32)],
     )(rows, kernel3)
 
@@ -120,10 +121,12 @@
     length, _, width, channels = video.shape
     groups = lax.axis_size("group")
     cached = shifted(video[length - 2 :], "group", 1)
-    partials = row_partials(jnp.concatenate([cached, video], 0), kernel3)
-    from_above = shifted(partials[0].astype(jnp.bfloat16), "frame", 1)
-    from_below = shifted(partials[2].astype(jnp.bfloat16), "frame", -1)
-    conv = partials[1] + from_above.astype(jnp.float32) + from_below.astype(jnp.float32)
+    rows = jnp.concatenate([cached, video], 0)
+    edges = row_partials(rows, kernel3, (0, 2))
+    from_above = shifted(edges[0].astype(jnp.bfloat16), "frame", 1)
+    from_below = shifted(edges[1].astype(jnp.bfloat16), "frame", -1)
+    centre = row_partials(rows, kernel3, (1,))[0]
+    conv = centre + from_above.astype(jnp.float32) + from_below.astype(jnp.float32)
     features = jax.nn.silu(conv).astype(jnp.bfloat16)
     block = width // groups
     padded = jnp.pad(features, ((0, 0), (1, 1), (0, 0)))

time: 116 us -> 113 us (0.974)
  waiting for transfers between devices: 17.2 us -> 12.3 us
  other arithmetic: 4.66 us -> 2.68 us
  local copies, waits for them, and re-layouts: 2.53 us -> 4.36 us
  Pallas kernels: 11.2 us -> 12.9 us
    ppermute x3, waiting for transfers between devices: 17.2 us -> 12.3 us  [shifted(): lax.ppermute(value, axis, [(source, source + steps) for source in range(f...]
    concatenate x1 -> x0, other arithmetic: 1.82 us -> none  [shards(): partials = row_partials(jnp.concatenate([cached, video], 0), kernel3)]
    pallas_call x1 -> x2, Pallas kernels: 11.2 us -> 12.9 us  [row_partials(): pl.pallas_call(row_partials_kernel, grid=(3 * len(row_taps),), in_specs=[...]
  transfers between devices with their start and end apart: 3 -> 3, of which waited for: 3 -> 3; matrix products, arithmetic and copies ran while one was open for 0% -> 0% of each run, Pallas kernels for 0% -> 4%
where the time goes in v8:
time: 113 us
  blocking collectives  66.8 us (59%)
  Pallas kernels  12.9 us (11%)
  waiting for transfers between devices  12.3 us (11%)
  starting transfers between devices  7.19 us (6%)
  matrix products  5.54 us (5%)
  local copies, waits for them, and re-layouts  4.36 us (4%)
  other arithmetic  2.68 us (2%)
    all_to_all x1, blocking collectives, shards(): rows_all = lax.all_to_all(pieces, 'frame', 0, 0, tiled=True)  44.7 us
    all_to_all x1, blocking collectives, shards(): pieces = lax.all_to_all(pieces, 'group', 0, 0, tiled=False)  22.1 us
    pallas_call x2, Pallas kernels, row_partials(): pl.pallas_call(row_partials_kernel, grid=(3 * len(row_taps),), in_specs=[...  12.9 us
    ppermute x3, waiting for transfers between devices, shifted(): lax.ppermute(value, axis, [(source, source + steps) for source in range(f...  12.3 us
    ppermute x3, starting transfers between devices, shifted(): lax.ppermute(value, axis, [(source, source + steps) for source in range(f...  7.19 us
    conv_general_dilated x1, matrix products, shards(): lax.conv_general_dilated(rows_all[None], kernel2, (1, 1), ((1, 1), (0, 0)...  5.54 us
  transfers between devices with their start and end apart: 3, of which 3 were waited for; matrix products, arithmetic and copies ran while one was open for 0% of the time, Pallas kernels for 4%

profile of v8, /device:TPU:1, one launch (start us, length us, event | category | flops | bytes accessed | tf_op | source)
XLA Modules:
  0.0 112.6 jit_solution(17599687253353305803)
XLA Ops:
  0.6 0.0 copy-start
  0.6 1.1 slice.73
  1.7 4.6 %collective-permute-start = (bf16[2,1,128,384]{3,2,1,0:T(8,128)(2,1)S(1)}, bf16[2,1,128,384]{3,2,1,0:T(8,128)(2,1)S(1)}, u32[]{:S(2)}, u32[]{:S(2)}) collective-permute-start(bf16[2,1,128,384]{3,2,1,0:T(8,128)(2,1)S(1)} %slice.73), channel_id=1, source_target_pairs={{0,48},{48,96},{96,144},{144,192},{192,240},{240,288},{288,336},{3... | collective-permute-start | bytes 589832 | tf_op jit(solution)/shard_map/ppermute | solution.py:12
  6.4 8.1 %collective-permute-done = bf16[2,1,128,384]{3,2,1,0:T(8,128)(2,1)S(1)} collective-permute-done((bf16[2,1,128,384]{3,2,1,0:T(8,128)(2,1)S(1)}, bf16[2,1,128,384]{3,2,1,0:T(8,128)(2,1)S(1)}, u32[]{:S(2)}, u32[]{:S(2)}) %collective-permute-start) | collective-permute-done | bytes 196640 | tf_op jit(solution)/shard_map/ppermute | solution.py:12
  14.5 1.0 constant_dynamic-update-slice_fusion.rows_ref
  15.5 0.0 copy-start.2
  15.5 0.8 copy-done.2
  16.3 7.9 %shard_map.51 = f32[2,3,128,384]{3,2,1,0:T(8,128)} custom-call(bf16[5,1,128,384]{3,2,1,0:T(8,128)(2,1)} %copy-done.2, bf16[3,3,3,384,384]{4,3,2,1,0:T(8,128)(2,1)} %kernel_ref.3), custom_call_target="tpu_custom_call" | custom-call | tf_op jit(solution)/shard_map/pallas_call | solution.py:107
  24.2 1.3 %convert.4 = bf16[2,3,128,384]{3,2,1,0:T(8,128)(2,1)S(1)} convert(f32[2,3,128,384]{3,2,1,0:T(8,128)} %shard_map.51) | non-fusion elementwise | flops 294912 | bytes 1769472 | tf_op jit(solution)/shard_map/convert.1
  25.6 0.1 slice_bitcast_fusion.1
  25.6 1.3 %collective-permute-start.1 = (bf16[3,128,384]{2,1,0:T(8,128)(2,1)S(1)}, bf16[3,128,384]{2,1,0:T(8,128)(2,1)S(1)}, u32[]{:S(2)}, u32[]{:S(2)}) collective-permute-start(bf16[3,128,384]{2,1,0:T(8,128)(2,1)S(1)} %get-tuple-element.10), channel_id=1, source_target_pairs={{0,1},{1,2},{2,3},{3,4},{4,5},{5,6},{6,7},{7,8},{8,9},{9,10},{10,1... | collective-permute-start | bytes 884744 | tf_op jit(solution)/shard_map/ppermute | solution.py:12
  27.0 1.3 %collective-permute-start.2 = (bf16[3,128,384]{2,1,0:T(8,128)(2,1)S(1)}, bf16[3,128,384]{2,1,0:T(8,128)(2,1)}, u32[]{:S(2)}, u32[]{:S(2)}) collective-permute-start(bf16[3,128,384]{2,1,0:T(8,128)(2,1)S(1)} %get-tuple-element.11), channel_id=1, source_target_pairs={{1,0},{2,1},{3,2},{4,3},{5,4},{6,5},{7,6},{8,7},{9,8},{10,9},{11,1... | collective-permute-start | bytes 884744 | tf_op jit(solution)/shard_map/ppermute | solution.py:12
  28.3 5.0 %shard_map.50 = f32[1,3,128,384]{3,2,1,0:T(8,128)} custom-call(bf16[5,1,128,384]{3,2,1,0:T(8,128)(2,1)} %copy-done.2, bf16[3,3,3,384,384]{4,3,2,1,0:T(8,128)(2,1)} %kernel_ref.3), custom_call_target="tpu_custom_call" | custom-call | tf_op jit(solution)/shard_map/pallas_call | solution.py:107
  33.2 0.2 collective-permute-done.1
  33.4 4.0 %collective-permute-done.2 = bf16[3,128,384]{2,1,0:T(8,128)(2,1)} collective-permute-done((bf16[3,128,384]{2,1,0:T(8,128)(2,1)S(1)}, bf16[3,128,384]{2,1,0:T(8,128)(2,1)}, u32[]{:S(2)}, u32[]{:S(2)}) %collective-permute-start.2) | collective-permute-done | bytes 294944 | tf_op jit(solution)/shard_map/ppermute | solution.py:12
  37.4 1.3 %multiply_convert_fusion = bf16[3,128,384]{2,1,0:T(8,128)(2,1)S(1)} fusion(f32[1,3,128,384]{3,2,1,0:T(8,128)} %shard_map.50, bf16[3,128,384]{2,1,0:T(8,128)(2,1)} %collective-permute-done.2, bf16[3,128,384]{2,1,0:T(8,128)(2,1)S(1)} %collective-permute-done.1), kind=kLoop, calls=%fused_computation.4 | loop fusion | flops 1327104 | bytes 1474560 | tf_op jit(solution)/shard_map/convert_element_type | solution.py:130
  38.8 0.0 copy-start.1
  39.2 0.2 copy.16
  39.4 22.1 %all_to_all.10 = bf16[16,3,10,384]{3,1,2,0:T(4,128)(2,1)S(1)} all-to-all(bf16[16,3,10,384]{3,1,2,0:T(4,128)(2,1)S(1)} %copy.16), channel_id=1, replica_groups=mesh['group'=16,'frame'=48] {'group'}, dimensions={0} | all-to-all | bytes 737280 | tf_op jit(solution)/shard_map/all_to_all | solution.py:134
  61.5 0.1 copy.23
  61.6 44.7 %all_to_all.11 = bf16[48,10,384]{2,1,0:T(8,128)(2,1)S(1)} all-to-all(bf16[48,10,384]{2,1,0:T(8,128)(2,1)S(1)} %bitcast.81), channel_id=1, replica_groups=mesh['group'=16,'frame'=48] {'frame'}, dimensions={0} | all-to-all | bytes 737280 | tf_op jit(solution)/shard_map/all_to_all | solution.py:136
  106.3 0.0 copy-done.1
  106.3 0.0 copy-done
  106.3 5.5 %convolution_convert_fusion = bf16[1,48,8,384]{3,0,2,1:T(2,128)(2,1)S(1)} fusion(bf16[3,3,384,384]{3,2,1,0:T(8,128)(2,1)S(1)} %copy-done, bf16[1,48,10,384]{3,2,1,0:T(8,128)(2,1)S(1)} %bitcast.82), kind=kOutput, calls=%fused_computation | convolution fusion | flops 1005207552 | bytes 3317760 | tf_op jit(solution)/shard_map/conv_general_dilated | solution.py:137
  111.8 0.8 copy.22
  (17 shorter events, 0.3 us)
Async XLA Ops:
  0.6 105.7 %copy-start = (bf16[3,3,384,384]{3,2,1,0:T(8,128)(2,1)S(1)}, bf16[3,3,384,384]{3,2,1,0:T(8,128)(2,1)}, u32[]{:S(2)}) copy-start(bf16[3,3,384,384]{3,2,1,0:T(8,128)(2,1)} %param.5) | copy-start | bytes 7962628
  1.7 12.7 %collective-permute-start = (bf16[2,1,128,384]{3,2,1,0:T(8,128)(2,1)S(1)}, bf16[2,1,128,384]{3,2,1,0:T(8,128)(2,1)S(1)}, u32[]{:S(2)}, u32[]{:S(2)}) collective-permute-start(bf16[2,1,128,384]{3,2,1,0:T(8,128)(2,1)S(1)} %slice.73), channel_id=1, source_target_pairs={{0,48},{48,96},{96,144},{144,192},{192,240},{240,288},{288,336},{3... | collective-permute-start | bytes 589832 | tf_op jit(solution)/shard_map/ppermute | solution.py:12
  15.5 0.8 copy-start.2
  25.6 7.8 %collective-permute-start.1 = (bf16[3,128,384]{2,1,0:T(8,128)(2,1)S(1)}, bf16[3,128,384]{2,1,0:T(8,128)(2,1)S(1)}, u32[]{:S(2)}, u32[]{:S(2)}) collective-permute-start(bf16[3,128,384]{2,1,0:T(8,128)(2,1)S(1)} %get-tuple-element.10), channel_id=1, source_target_pairs={{0,1},{1,2},{2,3},{3,4},{4,5},{5,6},{6,7},{7,8},{8,9},{9,10},{10,1... | collective-permute-start | bytes 884744 | tf_op jit(solution)/shard_map/ppermute | solution.py:12
  27.0 10.5 %collective-permute-start.2 = (bf16[3,128,384]{2,1,0:T(8,128)(2,1)S(1)}, bf16[3,128,384]{2,1,0:T(8,128)(2,1)}, u32[]{:S(2)}, u32[]{:S(2)}) collective-permute-start(bf16[3,128,384]{2,1,0:T(8,128)(2,1)S(1)} %get-tuple-element.11), channel_id=1, source_target_pairs={{1,0},{2,1},{3,2},{4,3},{5,4},{6,5},{7,6},{8,7},{9,8},{10,9},{11,1... | collective-permute-start | bytes 884744 | tf_op jit(solution)/shard_map/ppermute | solution.py:12
  38.8 67.5 %copy-start.1 = (bf16[3,128,384]{2,1,0:T(8,128)(2,1)}, bf16[3,128,384]{2,1,0:T(8,128)(2,1)S(1)}, u32[]{:S(2)}) copy-start(bf16[3,128,384]{2,1,0:T(8,128)(2,1)S(1)} %multiply_convert_fusion) | copy-start | bytes 884740

commit v9 on v5

v9 whole, which is shorter than its diff:
```python
import functools

import jax
import jax.numpy as jnp
from jax import lax
from jax.experimental import pallas as pl
from jax.experimental.pallas import tpu as pltpu
from jax.sharding import PartitionSpec as P


def shifted(value, axis, steps):
    count = lax.axis_size(axis)
    first, last = (max(0, -steps), min(count, count - steps))
    return lax.ppermute(value, axis, [(source, source + steps) for source in range(first, last)])


def diagonal(value, group_steps, frame_steps):
    groups, frames = lax.axis_size("group"), lax.axis_size("frame")
    pairs = []
    for g in range(groups):
        for f in range(frames):
            h, e = g + group_steps, f + frame_steps
            if 0 <= h < groups and 0 <= e < frames:
                pairs.append((g * frames + f, h * frames + e))
    return lax.ppermute(value, ("group", "frame"), pairs)


def conv3d_kernel(*refs, pairs, final):
    sources, kernel_ref = refs[: 2 * pairs], refs[2 * pairs]
    out_ref, acc_ref, rows_ref = refs[-3:]
    step = pl.program_id(0)
    frames, width, channels = acc_ref.shape[1:]
    cached = sources[0].shape[0]

    @pl.when(step == 0)
    def _():
        for p in range(pairs):
            rows_ref[p, :cached] = sources[2 * p][:, 0]
            rows_ref[p, cached:] = sources[2 * p + 1][:, 0]
        if final:
            acc_ref[...] = refs[2 * pairs + 1][...]
        else:
            acc_ref[...] = jnp.zeros_like(acc_ref)

    lhs = rows_ref[step % pairs, pl.ds(step // pairs, frames)].reshape(frames * width, channels)
    for c in range(3):
        part = jnp.dot(lhs, kernel_ref[0, 0, c], preferred_element_type=jnp.float32)
        acc_ref[c] += part.reshape(frames, width, channels)

    @pl.when(step == pl.num_programs(0) - 1)
    def _():
        if final:
            column = lax.broadcasted_iota(jnp.int32, (frames, width, channels), 1)
            left = jnp.where(column == 0, 0.0, pltpu.roll(acc_ref[0], 1, 1))
            right = jnp.where(column == width - 1, 0.0, pltpu.roll(acc_ref[2], width - 1, 1))
            out_ref[...] = left + acc_ref[1] + right
        else:
            out_ref[...] = acc_ref[...]


def conv3d_taps(sources, kernel3, row_taps, acc=None):
    pairs = len(row_taps)
    cached, _, width, channels = sources[0].shape
    count = sources[1].shape[0]
    if pairs == 1:
        index = lambda s: (s, row_taps[0], 0, 0, 0)
    else:
        index = lambda s: (s // 2, row_taps[0] + (row_taps[1] - row_taps[0]) * (s % 2), 0, 0, 0)
    acc_block = (3, count, width, channels)
    acc_spec = pl.BlockSpec(acc_block, lambda s: (0, 0, 0, 0))
    if acc is None:
        out_spec, out_block = acc_spec, acc_block
    else:
        out_spec, out_block = pl.BlockSpec(acc_block[1:], lambda s: (0, 0, 0)), acc_block[1:]
    whole = lambda x: pl.BlockSpec(x.shape, lambda s: (0,) * x.ndim)
    return pl.pallas_call(
        functools.partial(conv3d_kernel, pairs=pairs, final=acc is not None),
        grid=(3 * pairs,),
        in_specs=[whole(x) for x in sources]
        + [pl.BlockSpec((1, 1, 3, channels, channels), index)]
        + ([] if acc is None else [acc_spec]),
        out_specs=out_spec,
        out_shape=jax.ShapeDtypeStruct(out_block, jnp.float32),
        scratch_shapes=[
            pltpu.VMEM(acc_block, jnp.float32),
            pltpu.VMEM((pairs, cached + count, width, channels), sources[0].dtype),
        ],
    )(*sources, kernel3, *([] if acc is None else [acc]))


def shards(video, kernel3, kernel2):
    length, _, width, channels = video.shape
    groups = lax.axis_size("group")
    cached = shifted(video[length - 2 :], "group", 1)
    above = shifted(video, "frame", 1)
    below = shifted(video, "frame", -1)
    cached_above = diagonal(video[length - 2 :], 1, 1)
    cached_below = diagonal(video[length - 2 :], 1, -1)
    acc = conv3d_taps((cached, video), kernel3, (1,))
    conv = conv3d_taps((cached_above, above, cached_below, below), kernel3, (0, 2), acc)
    features = jax.nn.silu(conv).astype(jnp.bfloat16)
    block = width // groups
    padded = jnp.pad(features, ((0, 0), (1, 1), (0, 0)))
    pieces = jnp.stack([padded[:, j * block : j * block + block + 2] for j in range(groups)], 0)
    pieces = lax.all_to_all(pieces, "group", 0, 0, tiled=False)
    pieces = pieces.reshape(groups * length, block + 2, channels)
    rows_all = lax.all_to_all(pieces, "frame", 0, 0, tiled=True)
    critic = lax.conv_general_dilated(
        rows_all[None],
        kernel2,
        (1, 1),
        ((1, 1), (0, 0)),
        dimension_numbers=("NHWC", "HWIO", "NHWC"),
        preferred_element_type=jnp.float32,
    ).astype(jnp.bfloat16)
    return features[:, None], critic


def solution(mesh):
    return jax.shard_map(
        shards,
        mesh=mesh,
        in_specs=(P("group", "frame", None, None), P(), P()),
        out_specs=(P("group", "frame", None, None), P("frame", None, "group", None)),
        check_vma=False,
    )
```

time: 126 us -> 116 us (0.921)
  blocking collectives: 68.1 us -> 22.6 us
  waiting for transfers between devices: 0.07 us -> 26.4 us
  starting transfers between devices: 17.2 us -> 38.2 us
  local copies, waits for them, and re-layouts: 15.5 us -> 4.56 us
  other arithmetic: 3.94 us -> 2.11 us
    all_to_all x1 -> x0, blocking collectives: 44.7 us -> none  [shards(): rows_all = lax.all_to_all(pieces, 'frame', 0, 0, tiled=True)]
    all_to_all x0 -> x1, waiting for transfers between devices: none -> 26 us  [shards(): rows_all = lax.all_to_all(pieces, 'frame', 0, 0, tiled=True)]
    all_to_all x0 -> x1, starting transfers between devices: none -> 20.5 us  [shards(): rows_all = lax.all_to_all(pieces, 'frame', 0, 0, tiled=True)]
    unnamed x18 -> x24, local copies, waits for them, and re-layouts: 13.3 us -> 2.48 us
    concatenate x2 -> x0, other arithmetic: 3.94 us -> none  [the longest x1 2.12 us: shards(): jnp.concatenate([jnp.concatenate([cached_above, above], 0), jnp.concatena...]
  transfers between devices with their start and end apart: 5 -> 6, of which waited for: 1 -> 2; matrix products, arithmetic and copies ran while one was open for 1% -> 2% of each run, Pallas kernels for 4% -> 5%
where the time goes in v9:
time: 116 us; the launch traced here: 115 us
  starting transfers between devices  38.2 us (33%)
  waiting for transfers between devices  26.4 us (23%)
  blocking collectives  22.6 us (19%)
  Pallas kernels  13.9 us (12%)
  matrix products  6.56 us (6%)
  local copies, waits for them, and re-layouts  4.56 us (4%)
  other arithmetic  2.11 us (2%)
    all_to_all x1, waiting for transfers between devices, shards(): rows_all = lax.all_to_all(pieces, 'frame', 0, 0, tiled=True)  26 us
    all_to_all x1, blocking collectives, shards(): pieces = lax.all_to_all(pieces, 'group', 0, 0, tiled=False)  22.6 us
    all_to_all x1, starting transfers between devices, shards(): rows_all = lax.all_to_all(pieces, 'frame', 0, 0, tiled=True)  20.5 us
    pallas_call x2, Pallas kernels, conv3d_taps(): pl.pallas_call(functools.partial(conv3d_kernel, pairs=pairs, final=acc is...  13.9 us
    ppermute x3, starting transfers between devices, shifted(): lax.ppermute(value, axis, [(source, source + steps) for source in range(f...  10.4 us
    ppermute x2, starting transfers between devices, diagonal(): return lax.ppermute(value, ('group', 'frame'), pairs)  7.27 us
    conv_general_dilated x1, matrix products, shards(): lax.conv_general_dilated(rows_all[None], kernel2, (1, 1), ((1, 1), (0, 0)...  6.56 us
    unnamed x24, local copies, waits for them, and re-layouts  2.48 us
  transfers between devices with their start and end apart: 6, of which 2 were waited for; matrix products, arithmetic and copies ran while one was open for 2% of the time, Pallas kernels for 5%

profile of v9, /device:TPU:1, one launch (start us, length us, event | category | flops | bytes accessed | tf_op | source)
XLA Modules:
  0.0 115.1 jit_solution(14507783726238189443)
XLA Ops:
  0.6 0.0 copy-start
  0.6 5.1 %collective-permute-start.1 = (bf16[3,1,128,384]{3,2,1,0:T(8,128)(2,1)}, bf16[3,1,128,384]{3,2,1,0:T(8,128)(2,1)S(1)}, u32[]{:S(2)}, u32[]{:S(2)}) collective-permute-start(bf16[3,1,128,384]{3,2,1,0:T(8,128)(2,1)} %refs_1_.1), channel_id=1, source_target_pairs={{0,1},{1,2},{2,3},{3,4},{4,5},{5,6},{6,7},{7,8},{8,9},{9,10},{10,1... | collective-permute-start | bytes 884744 | tf_op jit(solution)/shard_map/ppermute | solution.py:14
  5.8 1.3 %collective-permute-start.3 = (bf16[3,1,128,384]{3,2,1,0:T(8,128)(2,1)}, bf16[3,1,128,384]{3,2,1,0:T(8,128)(2,1)S(1)}, u32[]{:S(2)}, u32[]{:S(2)}) collective-permute-start(bf16[3,1,128,384]{3,2,1,0:T(8,128)(2,1)} %refs_1_.1), channel_id=1, source_target_pairs={{1,0},{2,1},{3,2},{4,3},{5,4},{6,5},{7,6},{8,7},{9,8},{10,9},{11,1... | collective-permute-start | bytes 884744 | tf_op jit(solution)/shard_map/ppermute | solution.py:14
  7.1 1.0 slice.67
  8.0 4.0 %collective-permute-start.4 = (bf16[2,1,128,384]{3,2,1,0:T(8,128)(2,1)S(1)}, bf16[2,1,128,384]{3,2,1,0:T(8,128)(2,1)}, u32[]{:S(2)}, u32[]{:S(2)}) collective-permute-start(bf16[2,1,128,384]{3,2,1,0:T(8,128)(2,1)S(1)} %slice.67), channel_id=1, source_target_pairs={{0,48},{48,96},{96,144},{144,192},{192,240},{240,288},{288,336},{3... | collective-permute-start | bytes 589832 | tf_op jit(solution)/shard_map/ppermute | solution.py:14
  12.1 1.3 %collective-permute-start.2 = (bf16[2,1,128,384]{3,2,1,0:T(8,128)(2,1)S(1)}, bf16[2,1,128,384]{3,2,1,0:T(8,128)(2,1)}, u32[]{:S(2)}, u32[]{:S(2)}) collective-permute-start(bf16[2,1,128,384]{3,2,1,0:T(8,128)(2,1)S(1)} %slice.67), channel_id=1, source_target_pairs={{1,48},{2,49},{3,50},{4,51},{5,52},{6,53},{7,54},{8,55},{9,56},{10... | collective-permute-start | bytes 589832 | tf_op jit(solution)/shard_map/ppermute | solution.py:25
  13.4 6.0 %collective-permute-start = (bf16[2,1,128,384]{3,2,1,0:T(8,128)(2,1)S(1)}, bf16[2,1,128,384]{3,2,1,0:T(8,128)(2,1)}, u32[]{:S(2)}, u32[]{:S(2)}) collective-permute-start(bf16[2,1,128,384]{3,2,1,0:T(8,128)(2,1)S(1)} %slice.67), channel_id=1, source_target_pairs={{0,49},{1,50},{2,51},{3,52},{4,53},{5,54},{6,55},{7,56},{8,57},{9,... | collective-permute-start | bytes 589832 | tf_op jit(solution)/shard_map/ppermute | solution.py:25
  19.3 0.0 collective-permute-done.4.refs_0_
  19.3 5.3 %shard_map.50.refs_5_ = f32[3,3,128,384]{3,2,1,0:T(8,128)} custom-call(bf16[2,1,128,384]{3,2,1,0:T(8,128)(2,1)} %collective-permute-done.4.refs_0_, bf16[3,1,128,384]{3,2,1,0:T(8,128)(2,1)} %refs_1_.1, bf16[3,3,3,384,384]{4,3,2,1,0:T(8,128)(2,1)} %refs_4_.1), custom_call_target="tpu_custom_call" | custom-call | tf_op jit(solution)/shard_map/pallas_call | solution.py:76
  24.7 0.4 collective-permute-done.2.refs_2_
  25.1 0.0 collective-permute-done.refs_0_
  25.1 0.0 collective-permute-done.1.refs_1_
  25.1 0.0 copy-start.2
  25.1 0.0 collective-permute-done.3.refs_3_
  25.1 0.7 copy-done.2
  25.8 0.0 copy-start.3
  25.8 0.7 copy-done.3
  26.6 8.5 %shard_map.51 = f32[3,128,384]{2,1,0:T(8,128)} custom-call(bf16[2,1,128,384]{3,2,1,0:T(8,128)(2,1)} %collective-permute-done.refs_0_, bf16[3,1,128,384]{3,2,1,0:T(8,128)(2,1)} %copy-done.2, bf16[2,1,128,384]{3,2,1,0:T(8,128)(2,1)} %collective-permute-done.2.refs_2_, bf16[3,1,128,384]{3,2,1,0:T(8,128)(2,1)} %copy-done.3, ...), custom_call_target="tpu_custom_call" | custom-call | tf_op jit(solution)/shard_map/pallas_call | solution.py:76
  35.1 1.2 %multiply_convert_fusion = bf16[3,128,384]{2,1,0:T(8,128)(2,1)S(1)} fusion(f32[3,128,384]{2,1,0:T(8,128)} %shard_map.51), kind=kLoop, calls=%fused_computation.2 | loop fusion | flops 737280 | bytes 884736 | tf_op jit(solution)/shard_map/convert_element_type | solution.py:101
  36.5 0.0 copy-start.1
  36.7 0.2 copy.16
  36.9 22.6 %all_to_all.10 = bf16[16,3,10,384]{3,1,2,0:T(4,128)(2,1)S(1)} all-to-all(bf16[16,3,10,384]{3,1,2,0:T(4,128)(2,1)S(1)} %copy.16), channel_id=1, replica_groups=mesh['group'=16,'frame'=48] {'group'}, dimensions={0} | all-to-all | bytes 737280 | tf_op jit(solution)/shard_map/all_to_all | solution.py:105
  59.5 0.9 copy.23
  60.4 20.5 %all-to-all-start.1 = ((bf16[48,10,384]{2,1,0:T(8,128)(2,1)}), bf16[48,10,384]{2,1,0:T(8,128)(2,1)}, u32[]{:S(2)}, u32[]{:S(2)}) async-start(bf16[48,10,384]{2,1,0:T(8,128)(2,1)} %bitcast.71), calls=%async_computation.1 | async-start | bytes 1179648 | tf_op jit(solution)/shard_map/all_to_all | solution.py:107
  80.9 0.0 copy-done.1
  80.9 0.9 fusion.20
  81.8 26.0 %all-to-all-done.1 = bf16[48,10,384]{2,1,0:T(8,128)(2,1)} async-done(((bf16[48,10,384]{2,1,0:T(8,128)(2,1)}), bf16[48,10,384]{2,1,0:T(8,128)(2,1)}, u32[]{:S(2)}, u32[]{:S(2)}) %all-to-all-start.1) | async-done | bytes 368672 | tf_op jit(solution)/shard_map/all_to_all | solution.py:107
  107.8 0.0 copy-done
  107.8 6.6 %convolution_convert_fusion = bf16[1,48,8,384]{3,0,2,1:T(2,128)(2,1)S(1)} fusion(bf16[3,3,384,384]{3,2,1,0:T(8,128)(2,1)S(1)} %copy-done, bf16[1,48,10,384]{3,2,1,0:T(8,128)(2,1)} %bitcast.19), kind=kOutput, calls=%fused_computation | convolution fusion | flops 1005207552 | bytes 3317760 | tf_op jit(solution)/shard_map/conv_general_dilated | solution.py:108
  114.3 0.8 copy.22
  (16 shorter events, 0.3 us)
Async XLA Ops:
  0.6 107.1 %copy-start = (bf16[3,3,384,384]{3,2,1,0:T(8,128)(2,1)S(1)}, bf16[3,3,384,384]{3,2,1,0:T(8,128)(2,1)}, u32[]{:S(2)}) copy-start(bf16[3,3,384,384]{3,2,1,0:T(8,128)(2,1)} %param.5) | copy-start | bytes 7962628
  0.6 24.5 %collective-permute-start.1 = (bf16[3,1,128,384]{3,2,1,0:T(8,128)(2,1)}, bf16[3,1,128,384]{3,2,1,0:T(8,128)(2,1)S(1)}, u32[]{:S(2)}, u32[]{:S(2)}) collective-permute-start(bf16[3,1,128,384]{3,2,1,0:T(8,128)(2,1)} %refs_1_.1), channel_id=1, source_target_pairs={{0,1},{1,2},{2,3},{3,4},{4,5},{5,6},{6,7},{7,8},{8,9},{9,10},{10,1... | collective-permute-start | bytes 884744 | tf_op jit(solution)/shard_map/ppermute | solution.py:14
  5.8 19.4 %collective-permute-start.3 = (bf16[3,1,128,384]{3,2,1,0:T(8,128)(2,1)}, bf16[3,1,128,384]{3,2,1,0:T(8,128)(2,1)S(1)}, u32[]{:S(2)}, u32[]{:S(2)}) collective-permute-start(bf16[3,1,128,384]{3,2,1,0:T(8,128)(2,1)} %refs_1_.1), channel_id=1, source_target_pairs={{1,0},{2,1},{3,2},{4,3},{5,4},{6,5},{7,6},{8,7},{9,8},{10,9},{11,1... | collective-permute-start | bytes 884744 | tf_op jit(solution)/shard_map/ppermute | solution.py:14
  8.0 11.3 %collective-permute-start.4 = (bf16[2,1,128,384]{3,2,1,0:T(8,128)(2,1)S(1)}, bf16[2,1,128,384]{3,2,1,0:T(8,128)(2,1)}, u32[]{:S(2)}, u32[]{:S(2)}) collective-permute-start(bf16[2,1,128,384]{3,2,1,0:T(8,128)(2,1)S(1)} %slice.67), channel_id=1, source_target_pairs={{0,48},{48,96},{96,144},{144,192},{192,240},{240,288},{288,336},{3... | collective-permute-start | bytes 589832 | tf_op jit(solution)/shard_map/ppermute | solution.py:14
  12.1 13.1 %collective-permute-start.2 = (bf16[2,1,128,384]{3,2,1,0:T(8,128)(2,1)S(1)}, bf16[2,1,128,384]{3,2,1,0:T(8,128)(2,1)}, u32[]{:S(2)}, u32[]{:S(2)}) collective-permute-start(bf16[2,1,128,384]{3,2,1,0:T(8,128)(2,1)S(1)} %slice.67), channel_id=1, source_target_pairs={{1,48},{2,49},{3,50},{4,51},{5,52},{6,53},{7,54},{8,55},{9,56},{10... | collective-permute-start | bytes 589832 | tf_op jit(solution)/shard_map/ppermute | solution.py:25
  13.4 11.8 %collective-permute-start = (bf16[2,1,128,384]{3,2,1,0:T(8,128)(2,1)S(1)}, bf16[2,1,128,384]{3,2,1,0:T(8,128)(2,1)}, u32[]{:S(2)}, u32[]{:S(2)}) collective-permute-start(bf16[2,1,128,384]{3,2,1,0:T(8,128)(2,1)S(1)} %slice.67), channel_id=1, source_target_pairs={{0,49},{1,50},{2,51},{3,52},{4,53},{5,54},{6,55},{7,56},{8,57},{9,... | collective-permute-start | bytes 589832 | tf_op jit(solution)/shard_map/ppermute | solution.py:25
  25.1 0.7 copy-start.2
  25.8 0.7 copy-start.3
  36.5 44.5 %copy-start.1 = (f32[3,128,384]{2,1,0:T(8,128)S(1)}, f32[3,128,384]{2,1,0:T(8,128)}, u32[]{:S(2)}) copy-start(f32[3,128,384]{2,1,0:T(8,128)} %shard_map.51) | copy-start | bytes 1769476
  60.4 47.3 %all-to-all-start.1 = ((bf16[48,10,384]{2,1,0:T(8,128)(2,1)}), bf16[48,10,384]{2,1,0:T(8,128)(2,1)}, u32[]{:S(2)}, u32[]{:S(2)}) async-start(bf16[48,10,384]{2,1,0:T(8,128)(2,1)} %bitcast.71), calls=%async_computation.1 | async-start | bytes 1179648 | tf_op jit(solution)/shard_map/all_to_all | solution.py:107

commit v10 on v6

--- a/solution.py
+++ b/solution.py
@@ -98,14 +98,17 @@
     pieces = lax.all_to_all(pieces, "group", 0, 0, tiled=False)
     pieces = pieces.reshape(groups * length, block + 2, channels)
     rows_all = lax.all_to_all(pieces, "frame", 0, 0, tiled=True)
-    critic = lax.conv_general_dilated(
-        rows_all[None],
-        kernel2,
-        (1, 1),
-        ((1, 1), (0, 0)),
-        dimension_numbers=("NHWC", "HWIO", "NHWC"),
+    rows, span = rows_all.shape[:2]
+    padded = jnp.pad(rows_all, ((1, 1), (0, 0), (0, 0)))
+    lhs = jnp.concatenate(
+        [padded[b : b + rows, c : c + span - 2] for b in range(3) for c in range(3)], axis=-1
+    )
+    critic = jnp.dot(
+        lhs.reshape(rows * (span - 2), 9 * channels),
+        kernel2.reshape(9 * channels, channels),
         preferred_element_type=jnp.float32,
-    ).astype(jnp.bfloat16)
+    )
+    critic = critic.reshape(1, rows, span - 2, channels).astype(jnp.bfloat16)
     return features[:, None], critic
 
 

time: 115 us -> 112 us (0.974)
  matrix products: 5.54 us -> 2.26 us
    conv_general_dilated x1 -> x0, matrix products: 5.54 us -> none  [shards(): lax.conv_general_dilated(rows_all[None], kernel2, (1, 1), ((1, 1), (0, 0)...]
    dot_general x0 -> x1, matrix products: none -> 2.26 us  [shards(): jnp.dot(lhs.reshape(rows * (span - 2), 9 * channels), kernel2.reshape(9 *...]
where the time goes in v10:
time: 112 us
  blocking collectives  68.1 us (61%)
  starting transfers between devices  17.2 us (15%)
  Pallas kernels  13.9 us (12%)
  other arithmetic  5.23 us (5%)
  local copies, waits for them, and re-layouts  4.02 us (4%)
  matrix products  2.26 us (2%)
    all_to_all x1, blocking collectives, shards(): rows_all = lax.all_to_all(pieces, 'frame', 0, 0, tiled=True)  44.7 us
    all_to_all x1, blocking collectives, shards(): pieces = lax.all_to_all(pieces, 'group', 0, 0, tiled=False)  23.4 us
    pallas_call x2, Pallas kernels, conv3d_taps(): pl.pallas_call(conv3d_kernel, grid=(3 * pairs,), in_specs=[pl.BlockSpec(r...  13.9 us
    ppermute x3, starting transfers between devices, shifted(): lax.ppermute(value, axis, [(source, source + steps) for source in range(f...  9.9 us
    ppermute x2, starting transfers between devices, diagonal(): return lax.ppermute(value, ('group', 'frame'), pairs)  7.27 us
    dot_general x1, matrix products, shards(): jnp.dot(lhs.reshape(rows * (span - 2), 9 * channels), kernel2.reshape(9 *...  2.26 us
  transfers between devices with their start and end apart: 5, of which 1 were waited for; matrix products, arithmetic and copies ran while one was open for 2% of the time, Pallas kernels for 5%

profile of v10, /device:TPU:1, one launch (start us, length us, event | category | flops | bytes accessed | tf_op | source)
XLA Modules:
  0.0 111.7 jit_solution(2884479225727460460)
XLA Ops:
  0.6 0.0 copy-start
  0.6 1.1 slice.106
  1.7 4.6 %collective-permute-start.4 = (bf16[2,1,128,384]{3,2,1,0:T(8,128)(2,1)S(1)}, bf16[2,1,128,384]{3,2,1,0:T(8,128)(2,1)S(1)}, u32[]{:S(2)}, u32[]{:S(2)}) collective-permute-start(bf16[2,1,128,384]{3,2,1,0:T(8,128)(2,1)S(1)} %slice.106), channel_id=1, source_target_pairs={{0,48},{48,96},{96,144},{144,192},{192,240},{240,288},{288,336},{3... | collective-permute-start | bytes 589832 | tf_op jit(solution)/shard_map/ppermute | solution.py:11
  6.4 4.0 %collective-permute-start.1 = (bf16[3,1,128,384]{3,2,1,0:T(8,128)(2,1)}, bf16[3,1,128,384]{3,2,1,0:T(8,128)(2,1)S(1)}, u32[]{:S(2)}, u32[]{:S(2)}) collective-permute-start(bf16[3,1,128,384]{3,2,1,0:T(8,128)(2,1)} %param.3), channel_id=1, source_target_pairs={{0,1},{1,2},{2,3},{3,4},{4,5},{5,6},{6,7},{7,8},{8,9},{9,10},{10,1... | collective-permute-start | bytes 884744 | tf_op jit(solution)/shard_map/ppermute | solution.py:11
  10.4 1.3 %collective-permute-start.3 = (bf16[3,1,128,384]{3,2,1,0:T(8,128)(2,1)}, bf16[3,1,128,384]{3,2,1,0:T(8,128)(2,1)S(1)}, u32[]{:S(2)}, u32[]{:S(2)}) collective-permute-start(bf16[3,1,128,384]{3,2,1,0:T(8,128)(2,1)} %param.3), channel_id=1, source_target_pairs={{1,0},{2,1},{3,2},{4,3},{5,4},{6,5},{7,6},{8,7},{9,8},{10,9},{11,1... | collective-permute-start | bytes 884744 | tf_op jit(solution)/shard_map/ppermute | solution.py:11
  11.7 1.3 %collective-permute-start.2 = (bf16[2,1,128,384]{3,2,1,0:T(8,128)(2,1)S(1)}, bf16[2,1,128,384]{3,2,1,0:T(8,128)(2,1)}, u32[]{:S(2)}, u32[]{:S(2)}) collective-permute-start(bf16[2,1,128,384]{3,2,1,0:T(8,128)(2,1)S(1)} %slice.106), channel_id=1, source_target_pairs={{1,48},{2,49},{3,50},{4,51},{5,52},{6,53},{7,54},{8,55},{9,56},{10... | collective-permute-start | bytes 589832 | tf_op jit(solution)/shard_map/ppermute | solution.py:22
  13.0 6.0 %collective-permute-start = (bf16[2,1,128,384]{3,2,1,0:T(8,128)(2,1)S(1)}, bf16[2,1,128,384]{3,2,1,0:T(8,128)(2,1)}, u32[]{:S(2)}, u32[]{:S(2)}) collective-permute-start(bf16[2,1,128,384]{3,2,1,0:T(8,128)(2,1)S(1)} %slice.106), channel_id=1, source_target_pairs={{0,49},{1,50},{2,51},{3,52},{4,53},{5,54},{6,55},{7,56},{8,57},{9,... | collective-permute-start | bytes 589832 | tf_op jit(solution)/shard_map/ppermute | solution.py:22
  18.9 0.0 collective-permute-done.4
  19.0 1.8 %pad_maximum_fusion.rows_ref = bf16[5,1,128,384]{3,2,1,0:T(8,128)(2,1)} fusion(bf16[3,1,128,384]{3,2,1,0:T(8,128)(2,1)} %param.3, bf16[2,1,128,384]{3,2,1,0:T(8,128)(2,1)S(1)} %collective-permute-done.4), kind=kLoop, calls=%fused_computation.9 | loop fusion | flops 245760 | bytes 983040 | tf_op jit(solution)/shard_map/concatenate | solution.py:88
  20.8 5.2 %shard_map.50.refs_0_ = f32[3,3,128,384]{3,2,1,0:T(8,128)} custom-call(bf16[5,1,128,384]{3,2,1,0:T(8,128)(2,1)} %pad_maximum_fusion.rows_ref, bf16[3,3,3,384,384]{4,3,2,1,0:T(8,128)(2,1)} %kernel_ref.3), custom_call_target="tpu_custom_call" | custom-call | tf_op jit(solution)/shard_map/pallas_call | solution.py:58
  26.0 0.2 collective-permute-done.2
  26.2 0.0 collective-permute-done
  26.2 0.0 collective-permute-done.1
  26.2 0.0 collective-permute-done.3
  26.2 2.1 %maximum_maximum_fusion.rows_ref = bf16[5,2,128,384]{3,2,1,0:T(8,128)(2,1)} fusion(bf16[3,1,128,384]{3,2,1,0:T(8,128)(2,1)S(1)} %collective-permute-done.3, bf16[2,1,128,384]{3,2,1,0:T(8,128)(2,1)} %collective-permute-done.2, bf16[3,1,128,384]{3,2,1,0:T(8,128)(2,1)S(1)} %collective-permute-done.1, bf16[2,1,128,384]{3,2,1,0:T(8,128)(2,1)} %collective-permute-done), kind=kLoop, calls=%fused_computation.2 | loop fusion | flops 1474560 | bytes 1966080 | tf_op jit(solution)/shard_map/concatenate | solution.py:90
  28.3 8.7 %shard_map.51 = f32[3,3,128,384]{3,2,1,0:T(8,128)} custom-call(bf16[5,2,128,384]{3,2,1,0:T(8,128)(2,1)} %maximum_maximum_fusion.rows_ref, bf16[3,3,3,384,384]{4,3,2,1,0:T(8,128)(2,1)} %kernel_ref.3, f32[3,3,128,384]{3,2,1,0:T(8,128)} %shard_map.50.refs_0_), custom_call_target="tpu_custom_call", output_to_operand_aliasing={{}: (2, {})} | custom-call | tf_op jit(solution)/shard_map/pallas_call | solution.py:58
  37.0 1.3 %slice_bitcast_fusion.2 = (f32[3,127,384]{2,1,0:T(8,128)S(1)}, f32[3,127,384]{2,1,0:T(8,128)S(1)}) fusion(f32[3,3,128,384]{3,2,1,0:T(8,128)} %shard_map.51), kind=kLoop, calls=%fused_computation.7 | loop fusion | bytes 2340864 | tf_op jit(solution)/shard_map/squeeze | solution.py:75
  38.4 1.3 %multiply_convert_fusion = bf16[3,128,384]{2,1,0:T(8,128)(2,1)S(1)} fusion(f32[3,3,128,384]{3,2,1,0:T(8,128)} %shard_map.51, f32[3,127,384]{2,1,0:T(8,128)S(1)} %get-tuple-element.7, f32[3,127,384]{2,1,0:T(8,128)S(1)} %get-tuple-element.6), kind=kLoop, calls=%fused_computation.8 | loop fusion | flops 1032192 | bytes 2055168 | tf_op jit(solution)/shard_map/convert_element_type | solution.py:94
  39.6 0.0 copy-start.1
  40.0 0.2 copy.7
  40.2 23.4 %all_to_all.10 = bf16[16,3,10,384]{3,1,2,0:T(4,128)(2,1)S(1)} all-to-all(bf16[16,3,10,384]{3,1,2,0:T(4,128)(2,1)S(1)} %copy.7), channel_id=1, replica_groups=mesh['group'=16,'frame'=48] {'group'}, dimensions={0} | all-to-all | bytes 737280 | tf_op jit(solution)/shard_map/all_to_all | solution.py:98
  63.6 0.1 copy.8
  63.7 44.7 %all_to_all.11 = bf16[48,10,384]{2,1,0:T(8,128)(2,1)S(1)} all-to-all(bf16[48,10,384]{2,1,0:T(8,128)(2,1)S(1)} %bitcast.89), channel_id=1, replica_groups=mesh['group'=16,'frame'=48] {'frame'}, dimensions={0} | all-to-all | bytes 737280 | tf_op jit(solution)/shard_map/all_to_all | solution.py:100
  108.4 0.0 copy-done.1
  108.5 0.1 fusion.4
  108.6 0.1 fusion.5
  108.8 0.1 slice_dynamic-update-slice_fusion.1
  109.0 0.1 slice_dynamic-update-slice_fusion
  109.2 0.1 fusion.7
  109.3 0.1 fusion.8
  109.5 0.0 copy-done
  109.5 2.3 %fusion = bf16[1,48,8,384]{3,2,1,0:T(8,128)(2,1)} fusion(bf16[48,8,3456]{2,1,0:T(8,128)(2,1)S(1)} %fusion.8, bf16[3456,384,1]{1,0,2:T(8,128)(2,1)S(1)} %bitcast.87), kind=kOutput, calls=%fused_computation.1 | convolution fusion | flops 1019363328 | bytes 5603328 | tf_op jit(solution)/shard_map/dot_general | solution.py:106
  (19 shorter events, 0.4 us)
Async XLA Ops:
  0.6 108.8 %copy-start = (bf16[3,3,384,384]{3,2,1,0:T(8,128)(2,1)S(1)}, bf16[3,3,384,384]{3,2,1,0:T(8,128)(2,1)}, u32[]{:S(2)}) copy-start(bf16[3,3,384,384]{3,2,1,0:T(8,128)(2,1)} %param.5) | copy-start | bytes 7962628
  1.7 17.2 %collective-permute-start.4 = (bf16[2,1,128,384]{3,2,1,0:T(8,128)(2,1)S(1)}, bf16[2,1,128,384]{3,2,1,0:T(8,128)(2,1)S(1)}, u32[]{:S(2)}, u32[]{:S(2)}) collective-permute-start(bf16[2,1,128,384]{3,2,1,0:T(8,128)(2,1)S(1)} %slice.106), channel_id=1, source_target_pairs={{0,48},{48,96},{96,144},{144,192},{192,240},{240,288},{288,336},{3... | collective-permute-start | bytes 589832 | tf_op jit(solution)/shard_map/ppermute | solution.py:11
  6.4 19.8 %collective-permute-start.1 = (bf16[3,1,128,384]{3,2,1,0:T(8,128)(2,1)}, bf16[3,1,128,384]{3,2,1,0:T(8,128)(2,1)S(1)}, u32[]{:S(2)}, u32[]{:S(2)}) collective-permute-start(bf16[3,1,128,384]{3,2,1,0:T(8,128)(2,1)} %param.3), channel_id=1, source_target_pairs={{0,1},{1,2},{2,3},{3,4},{4,5},{5,6},{6,7},{7,8},{8,9},{9,10},{10,1... | collective-permute-start | bytes 884744 | tf_op jit(solution)/shard_map/ppermute | solution.py:11
  10.4 15.8 %collective-permute-start.3 = (bf16[3,1,128,384]{3,2,1,0:T(8,128)(2,1)}, bf16[3,1,128,384]{3,2,1,0:T(8,128)(2,1)S(1)}, u32[]{:S(2)}, u32[]{:S(2)}) collective-permute-start(bf16[3,1,128,384]{3,2,1,0:T(8,128)(2,1)} %param.3), channel_id=1, source_target_pairs={{1,0},{2,1},{3,2},{4,3},{5,4},{6,5},{7,6},{8,7},{9,8},{10,9},{11,1... | collective-permute-start | bytes 884744 | tf_op jit(solution)/shard_map/ppermute | solution.py:11
  11.7 14.5 %collective-permute-start.2 = (bf16[2,1,128,384]{3,2,1,0:T(8,128)(2,1)S(1)}, bf16[2,1,128,384]{3,2,1,0:T(8,128)(2,1)}, u32[]{:S(2)}, u32[]{:S(2)}) collective-permute-start(bf16[2,1,128,384]{3,2,1,0:T(8,128)(2,1)S(1)} %slice.106), channel_id=1, source_target_pairs={{1,48},{2,49},{3,50},{4,51},{5,52},{6,53},{7,54},{8,55},{9,56},{10... | collective-permute-start | bytes 589832 | tf_op jit(solution)/shard_map/ppermute | solution.py:22
  13.0 13.2 %collective-permute-start = (bf16[2,1,128,384]{3,2,1,0:T(8,128)(2,1)S(1)}, bf16[2,1,128,384]{3,2,1,0:T(8,128)(2,1)}, u32[]{:S(2)}, u32[]{:S(2)}) collective-permute-start(bf16[2,1,128,384]{3,2,1,0:T(8,128)(2,1)S(1)} %slice.106), channel_id=1, source_target_pairs={{0,49},{1,50},{2,51},{3,52},{4,53},{5,54},{6,55},{7,56},{8,57},{9,... | collective-permute-start | bytes 589832 | tf_op jit(solution)/shard_map/ppermute | solution.py:22
  39.6 68.8 %copy-start.1 = (bf16[3,128,384]{2,1,0:T(8,128)(2,1)}, bf16[3,128,384]{2,1,0:T(8,128)(2,1)S(1)}, u32[]{:S(2)}) copy-start(bf16[3,128,384]{2,1,0:T(8,128)(2,1)S(1)} %multiply_convert_fusion) | copy-start | bytes 884740

commit v11 on v10

--- a/solution.py
+++ b/solution.py
@@ -85,13 +85,24 @@
     below = shifted(video, "frame", -1)
     cached_above = diagonal(video[length - 2 :], 1, 1)
     cached_below = diagonal(video[length - 2 :], 1, -1)
-    centre = jnp.concatenate([cached, video], 0)
-    acc = conv3d_taps(centre, kernel3, (1,))
-    edges = jnp.concatenate(
-        [jnp.concatenate([cached_above, above], 0), jnp.concatenate([cached_below, below], 0)], 1
+    rows = jnp.concatenate(
+        [
+            jnp.concatenate([cached_above, above], 0),
+            jnp.concatenate([cached, video], 0),
+            jnp.concatenate([cached_below, below], 0),
+        ],
+        1,
     )
-    acc = conv3d_taps(edges, kernel3, (0, 2), acc)
-    features = jax.nn.silu(column_sum(acc)).astype(jnp.bfloat16)
+    padded = jnp.pad(rows, ((0, 0), (0, 0), (1, 1), (0, 0)))
+    lhs = jnp.concatenate(
+        [padded[a : a + length, b, c : c + width] for a in range(3) for b in range(3) for c in range(3)], axis=-1
+    )
+    conv = jnp.dot(
+        lhs.reshape(length * width, 27 * channels),
+        kernel3.reshape(27 * channels, channels),
+        preferred_element_type=jnp.float32,
+    )
+    features = jax.nn.silu(conv.reshape(length, width, channels)).astype(jnp.bfloat16)
     block = width // groups
     padded = jnp.pad(features, ((0, 0), (1, 1), (0, 0)))
     pieces = jnp.stack([padded[:, j * block : j * block + block + 2] for j in range(groups)], 0)

time: 112 us -> 109 us (0.973)
  Pallas kernels: 13.9 us -> 0 us
  matrix products: 2.26 us -> 6.6 us
  waiting for transfers between devices: 0.17 us -> 4.2 us
  other arithmetic: 5.23 us -> 1.6 us
  blocking collectives: 68.1 us -> 71.4 us
  local copies, waits for them, and re-layouts: 4.02 us -> 6.16 us
    pallas_call x2 -> x0, Pallas kernels: 13.9 us -> none  [conv3d_taps(): pl.pallas_call(conv3d_kernel, grid=(3 * pairs,), in_specs=[pl.BlockSpec(r...]
    dot_general x0 -> x1, matrix products: none -> 4.34 us  [shards(): jnp.dot(lhs.reshape(length * width, 27 * channels), kernel3.reshape(27 *...]
    ppermute x3, waiting for transfers between devices: 0.01 us -> 4.19 us  [shifted(): lax.ppermute(value, axis, [(source, source + steps) for source in range(f...]
    unnamed x27 -> x59, local copies, waits for them, and re-layouts: 1.15 us -> 4.41 us
    concatenate x1 -> x0, other arithmetic: 1.83 us -> none  [shards(): centre = jnp.concatenate([cached, video], 0)]
    all_to_all x1, blocking collectives: 44.7 us -> 46.5 us  [shards(): rows_all = lax.all_to_all(pieces, 'frame', 0, 0, tiled=True)]
    all_to_all x1, blocking collectives: 23.4 us -> 24.9 us  [shards(): pieces = lax.all_to_all(pieces, 'group', 0, 0, tiled=False)]
    squeeze x1 -> x0, local copies, waits for them, and re-layouts: 1.32 us -> none  [column_sum(): left = jnp.concatenate([zero, acc[0, :, :-1]], axis=1)]
  transfers between devices with their start and end apart: 5 -> 5, of which waited for: 1 -> 2; matrix products, arithmetic and copies ran while one was open for 2% -> 0% of each run, Pallas kernels for 5% -> 0%
where the time goes in v11:
time: 109 us; the launch traced here: 108 us
  blocking collectives  71.4 us (66%)
  starting transfers between devices  17.1 us (16%)
  matrix products  6.6 us (6%)
  local copies, waits for them, and re-layouts  6.16 us (6%)
  waiting for transfers between devices  4.2 us (4%)
  other arithmetic  1.6 us (1%)
  between operations  1.09 us (1%)
    all_to_all x1, blocking collectives, shards(): rows_all = lax.all_to_all(pieces, 'frame', 0, 0, tiled=True)  46.5 us
    all_to_all x1, blocking collectives, shards(): pieces = lax.all_to_all(pieces, 'group', 0, 0, tiled=False)  24.9 us
    ppermute x3, starting transfers between devices, shifted(): lax.ppermute(value, axis, [(source, source + steps) for source in range(f...  9.41 us
    ppermute x2, starting transfers between devices, diagonal(): return lax.ppermute(value, ('group', 'frame'), pairs)  7.7 us
    unnamed x59, local copies, waits for them, and re-layouts  4.41 us
    dot_general x1, matrix products, shards(): jnp.dot(lhs.reshape(length * width, 27 * channels), kernel3.reshape(27 *...  4.34 us
    ppermute x3, waiting for transfers between devices, shifted(): lax.ppermute(value, axis, [(source, source + steps) for source in range(f...  4.19 us
    dot_general x1, matrix products, shards(): jnp.dot(lhs.reshape(rows * (span - 2), 9 * channels), kernel2.reshape(9 *...  2.26 us
  transfers between devices with their start and end apart: 5, of which 2 were waited for; matrix products, arithmetic and copies ran while one was open for 0% of the time, Pallas kernels for 0%

profile of v11, /device:TPU:1, one launch (start us, length us, event | category | flops | bytes accessed | tf_op | source)
XLA Modules:
  0.0 108.2 jit_solution(12531021636405535775)
XLA Ops:
  0.7 1.1 %slice.240 = bf16[2,1,128,384]{3,2,0,1:T(8,128)(2,1)S(1)} slice(bf16[3,1,128,384]{3,2,0,1:T(8,128)(2,1)} %bitcast.187), slice={[1:3], [0:1], [0:128], [0:384]} | slice | bytes 393216 | tf_op jit(solution)/shard_map/slice | solution.py:86
  1.8 6.4 %collective-permute-start = (bf16[2,1,128,384]{3,2,0,1:T(8,128)(2,1)S(1)}, bf16[2,1,128,384]{3,2,0,1:T(8,128)(2,1)S(1)}, u32[]{:S(2)}, u32[]{:S(2)}) collective-permute-start(bf16[2,1,128,384]{3,2,0,1:T(8,128)(2,1)S(1)} %slice.240), channel_id=1, source_target_pairs={{0,49},{1,50},{2,51},{3,52},{4,53},{5,54},{6,55},{7,56},{8,57},{9,... | collective-permute-start | bytes 589832 | tf_op jit(solution)/shard_map/ppermute | solution.py:22
  8.2 1.3 %collective-permute-start.3 = (bf16[2,1,128,384]{3,2,0,1:T(8,128)(2,1)S(1)}, bf16[2,1,128,384]{3,2,0,1:T(8,128)(2,1)S(1)}, u32[]{:S(2)}, u32[]{:S(2)}) collective-permute-start(bf16[2,1,128,384]{3,2,0,1:T(8,128)(2,1)S(1)} %slice.240), channel_id=1, source_target_pairs={{1,48},{2,49},{3,50},{4,51},{5,52},{6,53},{7,54},{8,55},{9,56},{10... | collective-permute-start | bytes 589832 | tf_op jit(solution)/shard_map/ppermute | solution.py:22
  9.5 1.3 %collective-permute-start.4 = (bf16[3,1,128,384]{3,2,0,1:T(8,128)(2,1)}, bf16[3,1,128,384]{3,2,0,1:T(8,128)(2,1)S(1)}, u32[]{:S(2)}, u32[]{:S(2)}) collective-permute-start(bf16[3,1,128,384]{3,2,0,1:T(8,128)(2,1)} %bitcast.188), channel_id=1, source_target_pairs={{1,0},{2,1},{3,2},{4,3},{5,4},{6,5},{7,6},{8,7},{9,8},{10,9},{11,1... | collective-permute-start | bytes 884744 | tf_op jit(solution)/shard_map/ppermute | solution.py:11
  10.8 1.9 %collective-permute-start.2 = (bf16[2,1,128,384]{3,2,0,1:T(8,128)(2,1)S(1)}, bf16[2,1,128,384]{3,2,0,1:T(8,128)(2,1)S(1)}, u32[]{:S(2)}, u32[]{:S(2)}) collective-permute-start(bf16[2,1,128,384]{3,2,0,1:T(8,128)(2,1)S(1)} %slice.240), channel_id=1, source_target_pairs={{0,48},{48,96},{96,144},{144,192},{192,240},{240,288},{288,336},{3... | collective-permute-start | bytes 589832 | tf_op jit(solution)/shard_map/ppermute | solution.py:11
  12.7 6.2 %collective-permute-start.1 = (bf16[3,1,128,384]{3,2,0,1:T(8,128)(2,1)}, bf16[3,1,128,384]{3,2,0,1:T(8,128)(2,1)S(1)}, u32[]{:S(2)}, u32[]{:S(2)}) collective-permute-start(bf16[3,1,128,384]{3,2,0,1:T(8,128)(2,1)} %bitcast.189), channel_id=1, source_target_pairs={{0,1},{1,2},{2,3},{3,4},{4,5},{5,6},{6,7},{7,8},{8,9},{9,10},{10,1... | collective-permute-start | bytes 884744 | tf_op jit(solution)/shard_map/ppermute | solution.py:11
  19.0 2.9 %collective-permute-done.4 = bf16[3,1,128,384]{3,2,0,1:T(8,128)(2,1)S(1)} collective-permute-done((bf16[3,1,128,384]{3,2,0,1:T(8,128)(2,1)}, bf16[3,1,128,384]{3,2,0,1:T(8,128)(2,1)S(1)}, u32[]{:S(2)}, u32[]{:S(2)}) %collective-permute-start.4) | collective-permute-done | bytes 294944 | tf_op jit(solution)/shard_map/ppermute | solution.py:11
  21.9 1.3 %collective-permute-done.1 = bf16[3,1,128,384]{3,2,0,1:T(8,128)(2,1)S(1)} collective-permute-done((bf16[3,1,128,384]{3,2,0,1:T(8,128)(2,1)}, bf16[3,1,128,384]{3,2,0,1:T(8,128)(2,1)S(1)}, u32[]{:S(2)}, u32[]{:S(2)}) %collective-permute-start.1) | collective-permute-done | bytes 294944 | tf_op jit(solution)/shard_map/ppermute | solution.py:11
  23.3 1.5 %select_maximum_fusion = bf16[5,3,130,384]{3,2,0,1:T(8,128)(2,1)S(1)} fusion(bf16[5,1,128,384]{3,2,0,1:T(8,128)(2,1)S(1)} %constant_dynamic-update-slice_fusion.2, bf16[5,1,128,384]{3,2,0,1:T(8,128)(2,1)S(1)} %constant_dynamic-update-slice_fusion, bf16[3,1,128,384]{3,2,0,1:T(8,128)(2,1)} %bitcast.190, bf16[2,1,128,384]{3,2,0,1:T(8,128)(2,1)S(1)} %collective-permute-done.2), kind=kLoop, calls=%fused_computation.3 | loop fusion | flops 11232000 | bytes 2972160 | tf_op jit(solution)/shard_map/concatenate | solution.py:88
  24.9 0.1 fusion.35
  25.1 0.1 fusion.33
  25.4 0.1 fusion.30
  25.6 0.1 fusion.27
  25.8 0.1 fusion.23
  26.0 0.1 fusion.20
  26.3 0.1 fusion.18
  26.5 0.1 fusion.16
  26.7 0.1 fusion.14
  26.8 0.2 slice-done
  27.0 1.4 %slice-done.1 = s8[3768320]{0:T(1024)(128)(4,1)S(1)} async-done(((s8[7962624]{0:T(1024)(128)(4,1)}), s8[3768320]{0:T(1024)(128)(4,1)S(1)}, s32[]{:S(2)}) %slice-start.1) | async-done | bytes 3768344
  28.4 4.3 %multiply_convert_fusion = bf16[3,128,384]{2,1,0:T(8,128)(2,1)S(1)} fusion(bf16[3,128,10368]{2,1,0:T(8,128)(2,1)S(1)} %fusion.14, bf16[10368,384,1]{1,0,2:T(8,128)(2,1)S(1)} %bitcast.197), kind=kOutput, calls=%fused_computation.10 | convolution fusion | flops 3058384896 | bytes 16220160 | tf_op jit(solution)/shard_map/dot_general | solution.py:100
  33.2 0.2 copy.14
  33.4 24.9 %all_to_all.10 = bf16[16,3,10,384]{3,1,2,0:T(4,128)(2,1)S(1)} all-to-all(bf16[16,3,10,384]{3,1,2,0:T(4,128)(2,1)S(1)} %copy.14), channel_id=1, replica_groups=mesh['group'=16,'frame'=48] {'group'}, dimensions={0} | all-to-all | bytes 737280 | tf_op jit(solution)/shard_map/all_to_all | solution.py:109
  58.3 0.1 copy.15
  58.4 46.5 %all_to_all.11 = bf16[48,10,384]{2,1,0:T(8,128)(2,1)S(1)} all-to-all(bf16[48,10,384]{2,1,0:T(8,128)(2,1)S(1)} %bitcast.194), channel_id=1, replica_groups=mesh['group'=16,'frame'=48] {'frame'}, dimensions={0} | all-to-all | bytes 737280 | tf_op jit(solution)/shard_map/all_to_all | solution.py:111
  104.9 0.1 fusion.6
  105.1 0.1 fusion.7
  105.3 0.1 slice_dynamic-update-slice_fusion.1
  105.4 0.1 slice_dynamic-update-slice_fusion
  105.6 0.1 fusion.9
  105.8 0.1 fusion.10
  105.9 2.3 %fusion.4 = bf16[1,48,8,384]{3,2,1,0:T(8,128)(2,1)} fusion(bf16[48,8,3456]{2,1,0:T(8,128)(2,1)S(1)} %fusion.10, bf16[3456,384,1]{1,0,2:T(8,128)(2,1)S(1)} %bitcast.186), kind=kOutput, calls=%fused_computation.9 | convolution fusion | flops 1019363328 | bytes 5603328 | tf_op jit(solution)/shard_map/dot_general | solution.py:117
  (53 shorter events, 1.5 us)
Async XLA Ops:
  0.6 105.3 %copy-start = (bf16[3,3,384,384]{3,2,1,0:T(8,128)(2,1)S(1)}, bf16[3,3,384,384]{3,2,1,0:T(8,128)(2,1)}, u32[]{:S(2)}) copy-start(bf16[3,3,384,384]{3,2,1,0:T(8,128)(2,1)} %param.5) | copy-start | bytes 7962628
  0.6 24.4 %copy-start.1 = (bf16[3,1,128,384]{3,2,1,0:T(8,128)(2,1)S(1)}, bf16[3,1,128,384]{3,2,1,0:T(8,128)(2,1)}, u32[]{:S(2)}) copy-start(bf16[3,1,128,384]{3,2,1,0:T(8,128)(2,1)} %param.3) | copy-start | bytes 884740
  1.8 17.2 %collective-permute-start = (bf16[2,1,128,384]{3,2,0,1:T(8,128)(2,1)S(1)}, bf16[2,1,128,384]{3,2,0,1:T(8,128)(2,1)S(1)}, u32[]{:S(2)}, u32[]{:S(2)}) collective-permute-start(bf16[2,1,128,384]{3,2,0,1:T(8,128)(2,1)S(1)} %slice.240), channel_id=1, source_target_pairs={{0,49},{1,50},{2,51},{3,52},{4,53},{5,54},{6,55},{7,56},{8,57},{9,... | collective-permute-start | bytes 589832 | tf_op jit(solution)/shard_map/ppermute | solution.py:22
  8.2 10.8 %collective-permute-start.3 = (bf16[2,1,128,384]{3,2,0,1:T(8,128)(2,1)S(1)}, bf16[2,1,128,384]{3,2,0,1:T(8,128)(2,1)S(1)}, u32[]{:S(2)}, u32[]{:S(2)}) collective-permute-start(bf16[2,1,128,384]{3,2,0,1:T(8,128)(2,1)S(1)} %slice.240), channel_id=1, source_target_pairs={{1,48},{2,49},{3,50},{4,51},{5,52},{6,53},{7,54},{8,55},{9,56},{10... | collective-permute-start | bytes 589832 | tf_op jit(solution)/shard_map/ppermute | solution.py:22
  9.5 12.4 %collective-permute-start.4 = (bf16[3,1,128,384]{3,2,0,1:T(8,128)(2,1)}, bf16[3,1,128,384]{3,2,0,1:T(8,128)(2,1)S(1)}, u32[]{:S(2)}, u32[]{:S(2)}) collective-permute-start(bf16[3,1,128,384]{3,2,0,1:T(8,128)(2,1)} %bitcast.188), channel_id=1, source_target_pairs={{1,0},{2,1},{3,2},{4,3},{5,4},{6,5},{7,6},{8,7},{9,8},{10,9},{11,1... | collective-permute-start | bytes 884744 | tf_op jit(solution)/shard_map/ppermute | solution.py:11
  10.8 12.5 %collective-permute-start.2 = (bf16[2,1,128,384]{3,2,0,1:T(8,128)(2,1)S(1)}, bf16[2,1,128,384]{3,2,0,1:T(8,128)(2,1)S(1)}, u32[]{:S(2)}, u32[]{:S(2)}) collective-permute-start(bf16[2,1,128,384]{3,2,0,1:T(8,128)(2,1)S(1)} %slice.240), channel_id=1, source_target_pairs={{0,48},{48,96},{96,144},{144,192},{192,240},{240,288},{288,336},{3... | collective-permute-start | bytes 589832 | tf_op jit(solution)/shard_map/ppermute | solution.py:11
  12.7 10.5 %collective-permute-start.1 = (bf16[3,1,128,384]{3,2,0,1:T(8,128)(2,1)}, bf16[3,1,128,384]{3,2,0,1:T(8,128)(2,1)S(1)}, u32[]{:S(2)}, u32[]{:S(2)}) collective-permute-start(bf16[3,1,128,384]{3,2,0,1:T(8,128)(2,1)} %bitcast.189), channel_id=1, source_target_pairs={{0,1},{1,2},{2,3},{3,4},{4,5},{5,6},{6,7},{7,8},{8,9},{9,10},{10,1... | collective-permute-start | bytes 884744 | tf_op jit(solution)/shard_map/ppermute | solution.py:11
  24.8 2.2 %slice-start = ((s8[7962624]{0:T(1024)(128)(4,1)}), s8[4194304]{0:T(1024)(128)(4,1)S(1)}, s32[]{:S(2)}) async-start(s8[7962624]{0:T(1024)(128)(4,1)} %bitcast.195), calls=%async_computation.2 | async-start | bytes 8388608
  25.7 2.7 %slice-start.1 = ((s8[7962624]{0:T(1024)(128)(4,1)}), s8[3768320]{0:T(1024)(128)(4,1)S(1)}, s32[]{:S(2)}) async-start(s8[7962624]{0:T(1024)(128)(4,1)} %bitcast.195), calls=%async_computation.3 | async-start | bytes 7536640
  32.8 75.4 %copy-start.2 = (bf16[3,128,384]{2,1,0:T(8,128)(2,1)}, bf16[3,128,384]{2,1,0:T(8,128)(2,1)S(1)}, u32[]{:S(2)}) copy-start(bf16[3,128,384]{2,1,0:T(8,128)(2,1)S(1)} %multiply_convert_fusion) | copy-start | bytes 884740

commit v12 on v11

--- a/solution.py
+++ b/solution.py
@@ -94,14 +94,17 @@
         1,
     )
     padded = jnp.pad(rows, ((0, 0), (0, 0), (1, 1), (0, 0)))
-    lhs = jnp.concatenate(
-        [padded[a : a + length, b, c : c + width] for a in range(3) for b in range(3) for c in range(3)], axis=-1
-    )
-    conv = jnp.dot(
-        lhs.reshape(length * width, 27 * channels),
-        kernel3.reshape(27 * channels, channels),
-        preferred_element_type=jnp.float32,
-    )
+    conv = None
+    for a in range(3):
+        lhs = jnp.concatenate(
+            [padded[a : a + length, b, c : c + width] for b in range(3) for c in range(3)], axis=-1
+        )
+        part = jnp.dot(
+            lhs.reshape(length * width, 9 * channels),
+            kernel3[a].reshape(9 * channels, channels),
+            preferred_element_type=jnp.float32,
+        )
+        conv = part if conv is None else conv + part
     features = jax.nn.silu(conv.reshape(length, width, channels)).astype(jnp.bfloat16)
     block = width // groups
     padded = jnp.pad(features, ((0, 0), (1, 1), (0, 0)))

time: 109 us -> 110 us (level)
  blocking collectives: 71.4 us -> 25.2 us
  starting transfers between devices: 17.1 us -> 38.6 us
  waiting for transfers between devices: 4.2 us -> 25 us
  local copies, waits for them, and re-layouts: 6.16 us -> 9.83 us
  other arithmetic: 1.6 us -> 3.05 us
    all_to_all x1 -> x0, blocking collectives: 46.5 us -> none  [shards(): rows_all = lax.all_to_all(pieces, 'frame', 0, 0, tiled=True)]
    all_to_all x0 -> x1, waiting for transfers between devices: none -> 25 us  [shards(): rows_all = lax.all_to_all(pieces, 'frame', 0, 0, tiled=True)]
    all_to_all x0 -> x1, starting transfers between devices: none -> 21.3 us  [shards(): rows_all = lax.all_to_all(pieces, 'frame', 0, 0, tiled=True)]
    slice x0 -> x5, local copies, waits for them, and re-layouts: none -> 5.18 us  [the longest x1 3.94 us: shards(): kernel3[a].reshape(9 * channels, channels)]
    ppermute x3, waiting for transfers between devices: 4.19 us -> 0.01 us  [shifted(): lax.ppermute(value, axis, [(source, source + steps) for source in range(f...]
    convert_element_type x0 -> x2, other arithmetic: none -> 2.47 us  [shards(): jax.nn.silu(conv.reshape(length, width, channels)).astype(jnp.bfloat16)]
    unnamed x59 -> x56, local copies, waits for them, and re-layouts: 4.41 us -> 2.32 us
    ppermute x3, starting transfers between devices: 9.41 us -> 10.8 us  [shifted(): lax.ppermute(value, axis, [(source, source + steps) for source in range(f...]
  transfers between devices with their start and end apart: 5 -> 6, of which waited for: 2 -> 1; matrix products, arithmetic and copies ran while one was open for 0% -> 6% of each run, Pallas kernels for 0% -> 0%
where the time goes in v12:
time: 110 us
  starting transfers between devices  38.6 us (35%)
  blocking collectives  25.2 us (23%)
  waiting for transfers between devices  25 us (23%)
  local copies, waits for them, and re-layouts  9.83 us (9%)
  matrix products  6.9 us (6%)
  other arithmetic  3.05 us (3%)
  between operations  1.22 us (1%)
    all_to_all x1, blocking collectives, shards(): pieces = lax.all_to_all(pieces, 'group', 0, 0, tiled=False)  25.2 us
    all_to_all x1, waiting for transfers between devices, shards(): rows_all = lax.all_to_all(pieces, 'frame', 0, 0, tiled=True)  25 us
    all_to_all x1, starting transfers between devices, shards(): rows_all = lax.all_to_all(pieces, 'frame', 0, 0, tiled=True)  21.3 us
    ppermute x3, starting transfers between devices, shifted(): lax.ppermute(value, axis, [(source, source + steps) for source in range(f...  10.8 us
    ppermute x2, starting transfers between devices, diagonal(): return lax.ppermute(value, ('group', 'frame'), pairs)  6.55 us
    dot_general x3, matrix products, shards(): jnp.dot(lhs.reshape(length * width, 9 * channels), kernel3[a].reshape(9 *...  4.64 us
    slice x1, local copies, waits for them, and re-layouts, shards(): kernel3[a].reshape(9 * channels, channels)  3.94 us
    convert_element_type x2, other arithmetic, shards(): jax.nn.silu(conv.reshape(length, width, channels)).astype(jnp.bfloat16)  2.47 us
  transfers between devices with their start and end apart: 6, of which 1 were waited for; matrix products, arithmetic and copies ran while one was open for 6% of the time, Pallas kernels for 0%

profile of v12, /device:TPU:1, one launch (start us, length us, event | category | flops | bytes accessed | tf_op | source)
XLA Modules:
  0.0 109.8 jit_solution(14140836930054854233)
XLA Ops:
  0.6 0.0 copy-start
  0.6 1.6 %collective-permute-start.4 = (bf16[3,1,128,384]{3,2,1,0:T(8,128)(2,1)}, bf16[3,1,128,384]{3,2,1,0:T(8,128)(2,1)S(1)}, u32[]{:S(2)}, u32[]{:S(2)}) collective-permute-start(bf16[3,1,128,384]{3,2,1,0:T(8,128)(2,1)} %param.3), channel_id=1, source_target_pairs={{1,0},{2,1},{3,2},{4,3},{5,4},{6,5},{7,6},{8,7},{9,8},{10,9},{11,1... | collective-permute-start | bytes 884744 | tf_op jit(solution)/shard_map/ppermute | solution.py:11
  2.2 1.0 slice.199
  3.2 0.0 copy-start.2
  3.2 1.4 %collective-permute-start.3 = (bf16[2,1,128,384]{3,2,1,0:T(8,128)(2,1)S(1)}, bf16[2,1,128,384]{3,2,1,0:T(8,128)(2,1)S(1)}, u32[]{:S(2)}, u32[]{:S(2)}) collective-permute-start(bf16[2,1,128,384]{3,2,1,0:T(8,128)(2,1)S(1)} %slice.199), channel_id=1, source_target_pairs={{1,48},{2,49},{3,50},{4,51},{5,52},{6,53},{7,54},{8,55},{9,56},{10... | collective-permute-start | bytes 589832 | tf_op jit(solution)/shard_map/ppermute | solution.py:22
  4.6 4.6 %collective-permute-start.2 = (bf16[2,1,128,384]{3,2,1,0:T(8,128)(2,1)S(1)}, bf16[2,1,128,384]{3,2,1,0:T(8,128)(2,1)S(1)}, u32[]{:S(2)}, u32[]{:S(2)}) collective-permute-start(bf16[2,1,128,384]{3,2,1,0:T(8,128)(2,1)S(1)} %slice.199), channel_id=1, source_target_pairs={{0,48},{48,96},{96,144},{144,192},{192,240},{240,288},{288,336},{3... | collective-permute-start | bytes 589832 | tf_op jit(solution)/shard_map/ppermute | solution.py:11
  9.2 5.1 %collective-permute-start = (bf16[2,1,128,384]{3,2,1,0:T(8,128)(2,1)S(1)}, bf16[2,1,128,384]{3,2,1,0:T(8,128)(2,1)S(1)}, u32[]{:S(2)}, u32[]{:S(2)}) collective-permute-start(bf16[2,1,128,384]{3,2,1,0:T(8,128)(2,1)S(1)} %slice.199), channel_id=1, source_target_pairs={{0,49},{1,50},{2,51},{3,52},{4,53},{5,54},{6,55},{7,56},{8,57},{9,... | collective-permute-start | bytes 589832 | tf_op jit(solution)/shard_map/ppermute | solution.py:22
  14.3 4.6 %collective-permute-start.1 = (bf16[3,1,128,384]{3,2,1,0:T(8,128)(2,1)}, bf16[3,1,128,384]{3,2,1,0:T(8,128)(2,1)S(1)}, u32[]{:S(2)}, u32[]{:S(2)}) collective-permute-start(bf16[3,1,128,384]{3,2,1,0:T(8,128)(2,1)} %param.3), channel_id=1, source_target_pairs={{0,1},{1,2},{2,3},{3,4},{4,5},{5,6},{6,7},{7,8},{8,9},{9,10},{10,1... | collective-permute-start | bytes 884744 | tf_op jit(solution)/shard_map/ppermute | solution.py:11
  19.0 3.9 %fusion.18 = (bf16[1,3,3,384,384]{4,3,2,1,0:T(8,128)(2,1)S(1)}, bf16[1,3,3,384,384]{4,3,2,1,0:T(8,128)(2,1)S(1)}, bf16[1,3,3,384,384]{4,3,2,1,0:T(8,128)(2,1)S(1)}) fusion(bf16[3,3,3,384,384]{4,3,2,1,0:T(8,128)(2,1)} %param.4), kind=kLoop, calls=%fused_computation.100 | loop fusion | bytes 15925248 | tf_op jit(solution)/shard_map/slice | solution.py:104
  22.9 0.0 collective-permute-done.3
  23.0 0.0 collective-permute-done.2
  23.1 0.1 fusion.21
  23.3 0.1 fusion.22
  23.4 0.6 fusion.5
  24.0 0.1 fusion.20
  24.0 1.1 fusion.19
  25.7 1.5 %fusion.23 = f32[384,384]{1,0:T(8,128)S(1)} fusion(bf16[384,3456]{1,0:T(8,128)(2,1)S(1)} %constant_dynamic-update-slice_fusion.6, bf16[3456,384]{1,0:T(8,128)(2,1)S(1)} %bitcast.116), kind=kOutput, calls=%fused_computation.105 | convolution fusion | flops 1019215872 | bytes 5898240 | tf_op jit(solution)/shard_map/dot_general | solution.py:102
  28.1 1.5 %convolution_add_fusion.1 = f32[384,384]{1,0:T(8,128)S(1)} fusion(f32[384,384]{1,0:T(8,128)S(1)} %fusion.23, bf16[384,3456]{1,0:T(8,128)(2,1)S(1)} %constant_dynamic-update-slice_fusion.15, bf16[3456,384]{1,0:T(8,128)(2,1)S(1)} %bitcast.115), kind=kOutput, calls=%fused_computation.9 | convolution fusion | flops 1019363328 | bytes 6488064 | tf_op jit(solution)/shard_map/dot_general | solution.py:102
  29.7 1.5 %convolution_add_fusion = f32[384,384]{1,0:T(8,128)S(1)} fusion(f32[384,384]{1,0:T(8,128)S(1)} %convolution_add_fusion.1, bf16[384,3456]{1,0:T(8,128)(2,1)S(1)} %constant_dynamic-update-slice_fusion.24, bf16[3456,384]{1,0:T(8,128)(2,1)S(1)} %bitcast.114), kind=kOutput, calls=%fused_computation.8 | convolution fusion | flops 1019363328 | bytes 6488064 | tf_op jit(solution)/shard_map/dot_general | solution.py:102
  31.3 0.5 fusion.9
  32.2 25.2 %all_to_all.10 = bf16[16,3,10,384]{3,1,2,0:T(4,128)(2,1)S(1)} all-to-all(bf16[16,3,10,384]{3,1,2,0:T(4,128)(2,1)S(1)} %constant_dynamic-update-slice_fusion.33), channel_id=1, replica_groups=mesh['group'=16,'frame'=48] {'group'}, dimensions={0} | all-to-all | bytes 737280 | tf_op jit(solution)/shard_map/all_to_all | solution.py:112
  57.4 0.9 copy.11
  58.3 21.3 %all-to-all-start.1 = ((bf16[48,10,384]{2,1,0:T(8,128)(2,1)}), bf16[48,10,384]{2,1,0:T(8,128)(2,1)S(1)}, u32[]{:S(2)}, u32[]{:S(2)}) async-start(bf16[48,10,384]{2,1,0:T(8,128)(2,1)} %bitcast.119), calls=%async_computation.1 | async-start | bytes 1179648 | tf_op jit(solution)/shard_map/all_to_all | solution.py:114
  79.6 1.9 %multiply_convert_fusion = bf16[3,1,128,384]{3,2,1,0:T(8,128)(2,1)} fusion(f32[3,1,128,384]{3,2,1,0:T(8,128)} %bitcast.118), kind=kLoop, calls=%fused_computation.17 | loop fusion | flops 737280 | bytes 884736 | tf_op jit(solution)/shard_map/convert_element_type | solution.py:108
  81.6 25.0 %all-to-all-done.1 = bf16[48,10,384]{2,1,0:T(8,128)(2,1)S(1)} async-done(((bf16[48,10,384]{2,1,0:T(8,128)(2,1)}), bf16[48,10,384]{2,1,0:T(8,128)(2,1)S(1)}, u32[]{:S(2)}, u32[]{:S(2)}) %all-to-all-start.1) | async-done | bytes 368672 | tf_op jit(solution)/shard_map/all_to_all | solution.py:114
  106.6 0.1 fusion.11
  106.7 0.1 fusion.12
  106.9 0.1 slice_dynamic-update-slice_fusion.1
  107.1 0.1 slice_dynamic-update-slice_fusion
  107.2 0.1 fusion.14
  107.4 0.1 fusion.15
  107.6 2.3 %fusion.6 = bf16[1,48,8,384]{3,2,1,0:T(8,128)(2,1)} fusion(bf16[48,8,3456]{2,1,0:T(8,128)(2,1)S(1)} %fusion.15, bf16[3456,384,1]{1,0,2:T(8,128)(2,1)S(1)} %bitcast.113), kind=kOutput, calls=%fused_computation.11 | convolution fusion | flops 1019363328 | bytes 5603328 | tf_op jit(solution)/shard_map/dot_general | solution.py:120
  (59 shorter events, 2.0 us)
Async XLA Ops:
  0.6 106.9 %copy-start = (bf16[3,3,384,384]{3,2,1,0:T(8,128)(2,1)S(1)}, bf16[3,3,384,384]{3,2,1,0:T(8,128)(2,1)}, u32[]{:S(2)}) copy-start(bf16[3,3,384,384]{3,2,1,0:T(8,128)(2,1)} %param.5) | copy-start | bytes 7962628
  0.6 22.7 %collective-permute-start.4 = (bf16[3,1,128,384]{3,2,1,0:T(8,128)(2,1)}, bf16[3,1,128,384]{3,2,1,0:T(8,128)(2,1)S(1)}, u32[]{:S(2)}, u32[]{:S(2)}) collective-permute-start(bf16[3,1,128,384]{3,2,1,0:T(8,128)(2,1)} %param.3), channel_id=1, source_target_pairs={{1,0},{2,1},{3,2},{4,3},{5,4},{6,5},{7,6},{8,7},{9,8},{10,9},{11,1... | collective-permute-start | bytes 884744 | tf_op jit(solution)/shard_map/ppermute | solution.py:11
  3.2 19.9 %copy-start.2 = (bf16[3,1,128,384]{3,2,1,0:T(8,128)(2,1)S(1)}, bf16[3,1,128,384]{3,2,1,0:T(8,128)(2,1)}, u32[]{:S(2)}) copy-start(bf16[3,1,128,384]{3,2,1,0:T(8,128)(2,1)} %param.3) | copy-start | bytes 884740
  3.2 19.8 %collective-permute-start.3 = (bf16[2,1,128,384]{3,2,1,0:T(8,128)(2,1)S(1)}, bf16[2,1,128,384]{3,2,1,0:T(8,128)(2,1)S(1)}, u32[]{:S(2)}, u32[]{:S(2)}) collective-permute-start(bf16[2,1,128,384]{3,2,1,0:T(8,128)(2,1)S(1)} %slice.199), channel_id=1, source_target_pairs={{1,48},{2,49},{3,50},{4,51},{5,52},{6,53},{7,54},{8,55},{9,56},{10... | collective-permute-start | bytes 589832 | tf_op jit(solution)/shard_map/ppermute | solution.py:22
  4.6 18.4 %collective-permute-start.2 = (bf16[2,1,128,384]{3,2,1,0:T(8,128)(2,1)S(1)}, bf16[2,1,128,384]{3,2,1,0:T(8,128)(2,1)S(1)}, u32[]{:S(2)}, u32[]{:S(2)}) collective-permute-start(bf16[2,1,128,384]{3,2,1,0:T(8,128)(2,1)S(1)} %slice.199), channel_id=1, source_target_pairs={{0,48},{48,96},{96,144},{144,192},{192,240},{240,288},{288,336},{3... | collective-permute-start | bytes 589832 | tf_op jit(solution)/shard_map/ppermute | solution.py:11
  9.2 13.9 %collective-permute-start = (bf16[2,1,128,384]{3,2,1,0:T(8,128)(2,1)S(1)}, bf16[2,1,128,384]{3,2,1,0:T(8,128)(2,1)S(1)}, u32[]{:S(2)}, u32[]{:S(2)}) collective-permute-start(bf16[2,1,128,384]{3,2,1,0:T(8,128)(2,1)S(1)} %slice.199), channel_id=1, source_target_pairs={{0,49},{1,50},{2,51},{3,52},{4,53},{5,54},{6,55},{7,56},{8,57},{9,... | collective-permute-start | bytes 589832 | tf_op jit(solution)/shard_map/ppermute | solution.py:22
  14.3 8.8 %collective-permute-start.1 = (bf16[3,1,128,384]{3,2,1,0:T(8,128)(2,1)}, bf16[3,1,128,384]{3,2,1,0:T(8,128)(2,1)S(1)}, u32[]{:S(2)}, u32[]{:S(2)}) collective-permute-start(bf16[3,1,128,384]{3,2,1,0:T(8,128)(2,1)} %param.3), channel_id=1, source_target_pairs={{0,1},{1,2},{2,3},{3,4},{4,5},{5,6},{6,7},{7,8},{8,9},{9,10},{10,1... | collective-permute-start | bytes 884744 | tf_op jit(solution)/shard_map/ppermute | solution.py:11
  31.3 1.0 copy-start.1
  58.3 48.2 %all-to-all-start.1 = ((bf16[48,10,384]{2,1,0:T(8,128)(2,1)}), bf16[48,10,384]{2,1,0:T(8,128)(2,1)S(1)}, u32[]{:S(2)}, u32[]{:S(2)}) async-start(bf16[48,10,384]{2,1,0:T(8,128)(2,1)} %bitcast.119), calls=%async_computation.1 | async-start | bytes 1179648 | tf_op jit(solution)/shard_map/all_to_all | solution.py:114

commit v13 on v11

--- a/solution.py
+++ b/solution.py
@@ -93,9 +93,13 @@
         ],
         1,
     )
-    padded = jnp.pad(rows, ((0, 0), (0, 0), (1, 1), (0, 0)))
+    shifts = [
+        jnp.pad(rows[:, :, : width - 1], ((0, 0), (0, 0), (1, 0), (0, 0))),
+        rows,
+        jnp.pad(rows[:, :, 1:], ((0, 0), (0, 0), (0, 1), (0, 0))),
+    ]
     lhs = jnp.concatenate(
-        [padded[a : a + length, b, c : c + width] for a in range(3) for b in range(3) for c in range(3)], axis=-1
+        [shifts[c][a : a + length, b] for a in range(3) for b in range(3) for c in range(3)], axis=-1
     )
     conv = jnp.dot(
         lhs.reshape(length * width, 27 * channels),

time: 109 us -> 110 us (level)
  local copies, waits for them, and re-layouts: 6.16 us -> 7.9 us
where the time goes in v13:
time: 110 us
  blocking collectives  71.4 us (65%)
  starting transfers between devices  17.1 us (16%)
  local copies, waits for them, and re-layouts  7.9 us (7%)
  matrix products  6.6 us (6%)
  waiting for transfers between devices  4.19 us (4%)
  other arithmetic  1.27 us (1%)
    all_to_all x1, blocking collectives, shards(): rows_all = lax.all_to_all(pieces, 'frame', 0, 0, tiled=True)  46.5 us
    all_to_all x1, blocking collectives, shards(): pieces = lax.all_to_all(pieces, 'group', 0, 0, tiled=False)  24.9 us
    ppermute x3, starting transfers between devices, shifted(): lax.ppermute(value, axis, [(source, source + steps) for source in range(f...  9.41 us
    ppermute x2, starting transfers between devices, diagonal(): return lax.ppermute(value, ('group', 'frame'), pairs)  7.7 us
    unnamed x59, local copies, waits for them, and re-layouts  5.41 us
    dot_general x1, matrix products, shards(): jnp.dot(lhs.reshape(length * width, 27 * channels), kernel3.reshape(27 *...  4.34 us
    ppermute x3, waiting for transfers between devices, shifted(): lax.ppermute(value, axis, [(source, source + steps) for source in range(f...  4.18 us
    dot_general x1, matrix products, shards(): jnp.dot(lhs.reshape(rows * (span - 2), 9 * channels), kernel2.reshape(9 *...  2.26 us
  transfers between devices with their start and end apart: 5, of which 2 were waited for; matrix products, arithmetic and copies ran while one was open for 0% of the time, Pallas kernels for 0%

profile of v13, /device:TPU:1, one launch (start us, length us, event | category | flops | bytes accessed | tf_op | source)
XLA Modules:
  0.0 109.6 jit_solution(14746719799081156566)
XLA Ops:
  0.6 1.1 %slice.227 = bf16[2,1,128,384]{3,2,0,1:T(8,128)(2,1)S(1)} slice(bf16[3,1,128,384]{3,2,0,1:T(8,128)(2,1)} %bitcast.151), slice={[1:3], [0:1], [0:128], [0:384]} | slice | bytes 393216 | tf_op jit(solution)/shard_map/slice | solution.py:86
  1.7 6.4 %collective-permute-start = (bf16[2,1,128,384]{3,2,0,1:T(8,128)(2,1)S(1)}, bf16[2,1,128,384]{3,2,0,1:T(8,128)(2,1)S(1)}, u32[]{:S(2)}, u32[]{:S(2)}) collective-permute-start(bf16[2,1,128,384]{3,2,0,1:T(8,128)(2,1)S(1)} %slice.227), channel_id=1, source_target_pairs={{0,49},{1,50},{2,51},{3,52},{4,53},{5,54},{6,55},{7,56},{8,57},{9,... | collective-permute-start | bytes 589832 | tf_op jit(solution)/shard_map/ppermute | solution.py:22
  8.2 1.3 %collective-permute-start.3 = (bf16[2,1,128,384]{3,2,0,1:T(8,128)(2,1)S(1)}, bf16[2,1,128,384]{3,2,0,1:T(8,128)(2,1)S(1)}, u32[]{:S(2)}, u32[]{:S(2)}) collective-permute-start(bf16[2,1,128,384]{3,2,0,1:T(8,128)(2,1)S(1)} %slice.227), channel_id=1, source_target_pairs={{1,48},{2,49},{3,50},{4,51},{5,52},{6,53},{7,54},{8,55},{9,56},{10... | collective-permute-start | bytes 589832 | tf_op jit(solution)/shard_map/ppermute | solution.py:22
  9.5 1.3 %collective-permute-start.4 = (bf16[3,1,128,384]{3,2,0,1:T(8,128)(2,1)}, bf16[3,1,128,384]{3,2,0,1:T(8,128)(2,1)S(1)}, u32[]{:S(2)}, u32[]{:S(2)}) collective-permute-start(bf16[3,1,128,384]{3,2,0,1:T(8,128)(2,1)} %bitcast.152), channel_id=1, source_target_pairs={{1,0},{2,1},{3,2},{4,3},{5,4},{6,5},{7,6},{8,7},{9,8},{10,9},{11,1... | collective-permute-start | bytes 884744 | tf_op jit(solution)/shard_map/ppermute | solution.py:11
  10.8 1.9 %collective-permute-start.2 = (bf16[2,1,128,384]{3,2,0,1:T(8,128)(2,1)S(1)}, bf16[2,1,128,384]{3,2,0,1:T(8,128)(2,1)S(1)}, u32[]{:S(2)}, u32[]{:S(2)}) collective-permute-start(bf16[2,1,128,384]{3,2,0,1:T(8,128)(2,1)S(1)} %slice.227), channel_id=1, source_target_pairs={{0,48},{48,96},{96,144},{144,192},{192,240},{240,288},{288,336},{3... | collective-permute-start | bytes 589832 | tf_op jit(solution)/shard_map/ppermute | solution.py:11
  12.7 6.2 %collective-permute-start.1 = (bf16[3,1,128,384]{3,2,0,1:T(8,128)(2,1)}, bf16[3,1,128,384]{3,2,0,1:T(8,128)(2,1)S(1)}, u32[]{:S(2)}, u32[]{:S(2)}) collective-permute-start(bf16[3,1,128,384]{3,2,0,1:T(8,128)(2,1)} %bitcast.153), channel_id=1, source_target_pairs={{0,1},{1,2},{2,3},{3,4},{4,5},{5,6},{6,7},{7,8},{8,9},{9,10},{10,1... | collective-permute-start | bytes 884744 | tf_op jit(solution)/shard_map/ppermute | solution.py:11
  19.0 2.8 %collective-permute-done.4 = bf16[3,1,128,384]{3,2,0,1:T(8,128)(2,1)S(1)} collective-permute-done((bf16[3,1,128,384]{3,2,0,1:T(8,128)(2,1)}, bf16[3,1,128,384]{3,2,0,1:T(8,128)(2,1)S(1)}, u32[]{:S(2)}, u32[]{:S(2)}) %collective-permute-start.4) | collective-permute-done | bytes 294944 | tf_op jit(solution)/shard_map/ppermute | solution.py:11
  21.9 1.3 %collective-permute-done.1 = bf16[3,1,128,384]{3,2,0,1:T(8,128)(2,1)S(1)} collective-permute-done((bf16[3,1,128,384]{3,2,0,1:T(8,128)(2,1)}, bf16[3,1,128,384]{3,2,0,1:T(8,128)(2,1)S(1)}, u32[]{:S(2)}, u32[]{:S(2)}) %collective-permute-start.1) | collective-permute-done | bytes 294944 | tf_op jit(solution)/shard_map/ppermute | solution.py:11
  23.3 1.2 %pad_maximum_fusion = bf16[5,3,128,384]{3,2,0,1:T(8,128)(2,1)S(1)} fusion(bf16[5,1,128,384]{3,2,0,1:T(8,128)(2,1)S(1)} %constant_dynamic-update-slice_fusion.2, bf16[3,1,128,384]{3,2,0,1:T(8,128)(2,1)} %bitcast.154, bf16[2,1,128,384]{3,2,0,1:T(8,128)(2,1)S(1)} %collective-permute-done.2, bf16[5,1,128,384]{3,2,0,1:T(8,128)(2,1)S(1)} %constant_dynamic-update-slice_fusion), kind=kLoop, calls=%fused_computation | loop fusion | flops 2211840 | bytes 2949120 | tf_op jit(solution)/shard_map/concatenate | solution.py:88
  24.5 0.8 fusion.18
  25.5 0.1 bitcast_dynamic-update-slice_fusion.18
  25.7 0.1 bitcast_dynamic-update-slice_fusion.16
  25.9 0.1 bitcast_dynamic-update-slice_fusion.14
  26.1 0.1 bitcast_dynamic-update-slice_fusion.12
  26.4 0.1 bitcast_dynamic-update-slice_fusion.10
  26.6 0.1 bitcast_dynamic-update-slice_fusion.8
  26.8 0.1 bitcast_dynamic-update-slice_fusion.5
  27.0 0.1 bitcast_dynamic-update-slice_fusion.2
  27.3 1.3 %slice-done = s8[4194304]{0:T(1024)(128)(4,1)S(1)} async-done(((s8[7962624]{0:T(1024)(128)(4,1)}), s8[4194304]{0:T(1024)(128)(4,1)S(1)}, s32[]{:S(2)}) %slice-start) | async-done | bytes 4194328
  28.5 1.3 %slice-done.1 = s8[3768320]{0:T(1024)(128)(4,1)S(1)} async-done(((s8[7962624]{0:T(1024)(128)(4,1)}), s8[3768320]{0:T(1024)(128)(4,1)S(1)}, s32[]{:S(2)}) %slice-start.1) | async-done | bytes 3768344
  29.8 4.3 %multiply_convert_fusion = bf16[3,128,384]{2,1,0:T(8,128)(2,1)S(1)} fusion(bf16[3,128,10368]{2,1,0:T(8,128)(2,1)S(1)} %bitcast_dynamic-update-slice_fusion, bf16[10368,384,1]{1,0,2:T(8,128)(2,1)S(1)} %bitcast.161), kind=kOutput, calls=%fused_computation.3 | convolution fusion | flops 3058384896 | bytes 16220160 | tf_op jit(solution)/shard_map/dot_general | solution.py:104
  34.6 0.2 copy.14
  34.8 24.9 %all_to_all.10 = bf16[16,3,10,384]{3,1,2,0:T(4,128)(2,1)S(1)} all-to-all(bf16[16,3,10,384]{3,1,2,0:T(4,128)(2,1)S(1)} %copy.14), channel_id=1, replica_groups=mesh['group'=16,'frame'=48] {'group'}, dimensions={0} | all-to-all | bytes 737280 | tf_op jit(solution)/shard_map/all_to_all | solution.py:113
  59.7 0.1 copy.15
  59.8 46.5 %all_to_all.11 = bf16[48,10,384]{2,1,0:T(8,128)(2,1)S(1)} all-to-all(bf16[48,10,384]{2,1,0:T(8,128)(2,1)S(1)} %bitcast.158), channel_id=1, replica_groups=mesh['group'=16,'frame'=48] {'frame'}, dimensions={0} | all-to-all | bytes 737280 | tf_op jit(solution)/shard_map/all_to_all | solution.py:115
  106.3 0.1 fusion.2
  106.5 0.1 fusion.3
  106.7 0.1 slice_dynamic-update-slice_fusion.1
  106.8 0.1 slice_dynamic-update-slice_fusion
  107.0 0.1 fusion.5
  107.2 0.1 fusion.6
  107.3 2.3 %fusion = bf16[1,48,8,384]{3,2,1,0:T(8,128)(2,1)} fusion(bf16[48,8,3456]{2,1,0:T(8,128)(2,1)S(1)} %fusion.6, bf16[3456,384,1]{1,0,2:T(8,128)(2,1)S(1)} %bitcast.150), kind=kOutput, calls=%fused_computation.2 | convolution fusion | flops 1019363328 | bytes 5603328 | tf_op jit(solution)/shard_map/dot_general | solution.py:121
  (54 shorter events, 1.6 us)
Async XLA Ops:
  0.6 106.7 %copy-start = (bf16[3,3,384,384]{3,2,1,0:T(8,128)(2,1)S(1)}, bf16[3,3,384,384]{3,2,1,0:T(8,128)(2,1)}, u32[]{:S(2)}) copy-start(bf16[3,3,384,384]{3,2,1,0:T(8,128)(2,1)} %param.5) | copy-start | bytes 7962628
  1.7 17.2 %collective-permute-start = (bf16[2,1,128,384]{3,2,0,1:T(8,128)(2,1)S(1)}, bf16[2,1,128,384]{3,2,0,1:T(8,128)(2,1)S(1)}, u32[]{:S(2)}, u32[]{:S(2)}) collective-permute-start(bf16[2,1,128,384]{3,2,0,1:T(8,128)(2,1)S(1)} %slice.227), channel_id=1, source_target_pairs={{0,49},{1,50},{2,51},{3,52},{4,53},{5,54},{6,55},{7,56},{8,57},{9,... | collective-permute-start | bytes 589832 | tf_op jit(solution)/shard_map/ppermute | solution.py:22
  8.2 10.8 %collective-permute-start.3 = (bf16[2,1,128,384]{3,2,0,1:T(8,128)(2,1)S(1)}, bf16[2,1,128,384]{3,2,0,1:T(8,128)(2,1)S(1)}, u32[]{:S(2)}, u32[]{:S(2)}) collective-permute-start(bf16[2,1,128,384]{3,2,0,1:T(8,128)(2,1)S(1)} %slice.227), channel_id=1, source_target_pairs={{1,48},{2,49},{3,50},{4,51},{5,52},{6,53},{7,54},{8,55},{9,56},{10... | collective-permute-start | bytes 589832 | tf_op jit(solution)/shard_map/ppermute | solution.py:22
  9.5 12.4 %collective-permute-start.4 = (bf16[3,1,128,384]{3,2,0,1:T(8,128)(2,1)}, bf16[3,1,128,384]{3,2,0,1:T(8,128)(2,1)S(1)}, u32[]{:S(2)}, u32[]{:S(2)}) collective-permute-start(bf16[3,1,128,384]{3,2,0,1:T(8,128)(2,1)} %bitcast.152), channel_id=1, source_target_pairs={{1,0},{2,1},{3,2},{4,3},{5,4},{6,5},{7,6},{8,7},{9,8},{10,9},{11,1... | collective-permute-start | bytes 884744 | tf_op jit(solution)/shard_map/ppermute | solution.py:11
  10.8 12.5 %collective-permute-start.2 = (bf16[2,1,128,384]{3,2,0,1:T(8,128)(2,1)S(1)}, bf16[2,1,128,384]{3,2,0,1:T(8,128)(2,1)S(1)}, u32[]{:S(2)}, u32[]{:S(2)}) collective-permute-start(bf16[2,1,128,384]{3,2,0,1:T(8,128)(2,1)S(1)} %slice.227), channel_id=1, source_target_pairs={{0,48},{48,96},{96,144},{144,192},{192,240},{240,288},{288,336},{3... | collective-permute-start | bytes 589832 | tf_op jit(solution)/shard_map/ppermute | solution.py:11
  12.7 10.5 %collective-permute-start.1 = (bf16[3,1,128,384]{3,2,0,1:T(8,128)(2,1)}, bf16[3,1,128,384]{3,2,0,1:T(8,128)(2,1)S(1)}, u32[]{:S(2)}, u32[]{:S(2)}) collective-permute-start(bf16[3,1,128,384]{3,2,0,1:T(8,128)(2,1)} %bitcast.153), channel_id=1, source_target_pairs={{0,1},{1,2},{2,3},{3,4},{4,5},{5,6},{6,7},{7,8},{8,9},{9,10},{10,1... | collective-permute-start | bytes 884744 | tf_op jit(solution)/shard_map/ppermute | solution.py:11
  19.0 6.6 %copy-start.1 = (bf16[3,1,128,384]{3,2,1,0:T(8,128)(2,1)S(1)}, bf16[3,1,128,384]{3,2,1,0:T(8,128)(2,1)}, u32[]{:S(2)}) copy-start(bf16[3,1,128,384]{3,2,1,0:T(8,128)(2,1)} %param.3) | copy-start | bytes 884740
  26.4 2.2 %slice-start = ((s8[7962624]{0:T(1024)(128)(4,1)}), s8[4194304]{0:T(1024)(128)(4,1)S(1)}, s32[]{:S(2)}) async-start(s8[7962624]{0:T(1024)(128)(4,1)} %bitcast.159), calls=%async_computation.2 | async-start | bytes 8388608
  26.8 3.0 %slice-start.1 = ((s8[7962624]{0:T(1024)(128)(4,1)}), s8[3768320]{0:T(1024)(128)(4,1)S(1)}, s32[]{:S(2)}) async-start(s8[7962624]{0:T(1024)(128)(4,1)} %bitcast.159), calls=%async_computation.3 | async-start | bytes 7536640
  34.2 75.4 %copy-start.2 = (bf16[3,128,384]{2,1,0:T(8,128)(2,1)}, bf16[3,128,384]{2,1,0:T(8,128)(2,1)S(1)}, u32[]{:S(2)}) copy-start(bf16[3,128,384]{2,1,0:T(8,128)(2,1)S(1)} %multiply_convert_fusion) | copy-start | bytes 884740

commit v14 on v11

--- a/solution.py
+++ b/solution.py
@@ -110,9 +110,13 @@
     pieces = pieces.reshape(groups * length, block + 2, channels)
     rows_all = lax.all_to_all(pieces, "frame", 0, 0, tiled=True)
     rows, span = rows_all.shape[:2]
-    padded = jnp.pad(rows_all, ((1, 1), (0, 0), (0, 0)))
+    shifts = [
+        jnp.pad(rows_all[: rows - 1], ((1, 0), (0, 0), (0, 0))),
+        rows_all,
+        jnp.pad(rows_all[1:], ((0, 1), (0, 0), (0, 0))),
+    ]
     lhs = jnp.concatenate(
-        [padded[b : b + rows, c : c + span - 2] for b in range(3) for c in range(3)], axis=-1
+        [shifts[b][:, c : c + span - 2] for b in range(3) for c in range(3)], axis=-1
     )
     critic = jnp.dot(
         lhs.reshape(rows * (span - 2), 9 * channels),

time: 109 us -> 109 us (level)
  no operation moved by 1% of the time
where the time goes in v14:
time: 109 us; the launch traced here: 108 us
  blocking collectives  71.4 us (66%)
  starting transfers between devices  17.1 us (16%)
  matrix products  6.6 us (6%)
  local copies, waits for them, and re-layouts  6.24 us (6%)
  waiting for transfers between devices  4.2 us (4%)
  other arithmetic  1.6 us (1%)
  between operations  1.1 us (1%)
    all_to_all x1, blocking collectives, shards(): rows_all = lax.all_to_all(pieces, 'frame', 0, 0, tiled=True)  46.5 us
    all_to_all x1, blocking collectives, shards(): pieces = lax.all_to_all(pieces, 'group', 0, 0, tiled=False)  24.9 us
    ppermute x3, starting transfers between devices, shifted(): lax.ppermute(value, axis, [(source, source + steps) for source in range(f...  9.41 us
    ppermute x2, starting transfers between devices, diagonal(): return lax.ppermute(value, ('group', 'frame'), pairs)  7.7 us
    unnamed x59, local copies, waits for them, and re-layouts  4.4 us
    dot_general x1, matrix products, shards(): jnp.dot(lhs.reshape(length * width, 27 * channels), kernel3.reshape(27 *...  4.34 us
    ppermute x3, waiting for transfers between devices, shifted(): lax.ppermute(value, axis, [(source, source + steps) for source in range(f...  4.19 us
    dot_general x1, matrix products, shards(): jnp.dot(lhs.reshape(rows * (span - 2), 9 * channels), kernel2.reshape(9 *...  2.26 us
  transfers between devices with their start and end apart: 5, of which 2 were waited for; matrix products, arithmetic and copies ran while one was open for 0% of the time, Pallas kernels for 0%

profile of v14, /device:TPU:1, one launch (start us, length us, event | category | flops | bytes accessed | tf_op | source)
XLA Modules:
  0.0 108.3 jit_solution(695058380773328345)
XLA Ops:
  0.7 1.1 %slice.245 = bf16[2,1,128,384]{3,2,0,1:T(8,128)(2,1)S(1)} slice(bf16[3,1,128,384]{3,2,0,1:T(8,128)(2,1)} %bitcast.187), slice={[1:3], [0:1], [0:128], [0:384]} | slice | bytes 393216 | tf_op jit(solution)/shard_map/slice | solution.py:86
  1.8 6.4 %collective-permute-start = (bf16[2,1,128,384]{3,2,0,1:T(8,128)(2,1)S(1)}, bf16[2,1,128,384]{3,2,0,1:T(8,128)(2,1)S(1)}, u32[]{:S(2)}, u32[]{:S(2)}) collective-permute-start(bf16[2,1,128,384]{3,2,0,1:T(8,128)(2,1)S(1)} %slice.245), channel_id=1, source_target_pairs={{0,49},{1,50},{2,51},{3,52},{4,53},{5,54},{6,55},{7,56},{8,57},{9,... | collective-permute-start | bytes 589832 | tf_op jit(solution)/shard_map/ppermute | solution.py:22
  8.2 1.3 %collective-permute-start.3 = (bf16[2,1,128,384]{3,2,0,1:T(8,128)(2,1)S(1)}, bf16[2,1,128,384]{3,2,0,1:T(8,128)(2,1)S(1)}, u32[]{:S(2)}, u32[]{:S(2)}) collective-permute-start(bf16[2,1,128,384]{3,2,0,1:T(8,128)(2,1)S(1)} %slice.245), channel_id=1, source_target_pairs={{1,48},{2,49},{3,50},{4,51},{5,52},{6,53},{7,54},{8,55},{9,56},{10... | collective-permute-start | bytes 589832 | tf_op jit(solution)/shard_map/ppermute | solution.py:22
  9.5 1.3 %collective-permute-start.4 = (bf16[3,1,128,384]{3,2,0,1:T(8,128)(2,1)}, bf16[3,1,128,384]{3,2,0,1:T(8,128)(2,1)S(1)}, u32[]{:S(2)}, u32[]{:S(2)}) collective-permute-start(bf16[3,1,128,384]{3,2,0,1:T(8,128)(2,1)} %bitcast.188), channel_id=1, source_target_pairs={{1,0},{2,1},{3,2},{4,3},{5,4},{6,5},{7,6},{8,7},{9,8},{10,9},{11,1... | collective-permute-start | bytes 884744 | tf_op jit(solution)/shard_map/ppermute | solution.py:11
  10.8 1.9 %collective-permute-start.2 = (bf16[2,1,128,384]{3,2,0,1:T(8,128)(2,1)S(1)}, bf16[2,1,128,384]{3,2,0,1:T(8,128)(2,1)S(1)}, u32[]{:S(2)}, u32[]{:S(2)}) collective-permute-start(bf16[2,1,128,384]{3,2,0,1:T(8,128)(2,1)S(1)} %slice.245), channel_id=1, source_target_pairs={{0,48},{48,96},{96,144},{144,192},{192,240},{240,288},{288,336},{3... | collective-permute-start | bytes 589832 | tf_op jit(solution)/shard_map/ppermute | solution.py:11
  12.7 6.2 %collective-permute-start.1 = (bf16[3,1,128,384]{3,2,0,1:T(8,128)(2,1)}, bf16[3,1,128,384]{3,2,0,1:T(8,128)(2,1)S(1)}, u32[]{:S(2)}, u32[]{:S(2)}) collective-permute-start(bf16[3,1,128,384]{3,2,0,1:T(8,128)(2,1)} %bitcast.189), channel_id=1, source_target_pairs={{0,1},{1,2},{2,3},{3,4},{4,5},{5,6},{6,7},{7,8},{8,9},{9,10},{10,1... | collective-permute-start | bytes 884744 | tf_op jit(solution)/shard_map/ppermute | solution.py:11
  19.0 2.9 %collective-permute-done.4 = bf16[3,1,128,384]{3,2,0,1:T(8,128)(2,1)S(1)} collective-permute-done((bf16[3,1,128,384]{3,2,0,1:T(8,128)(2,1)}, bf16[3,1,128,384]{3,2,0,1:T(8,128)(2,1)S(1)}, u32[]{:S(2)}, u32[]{:S(2)}) %collective-permute-start.4) | collective-permute-done | bytes 294944 | tf_op jit(solution)/shard_map/ppermute | solution.py:11
  21.9 1.3 %collective-permute-done.1 = bf16[3,1,128,384]{3,2,0,1:T(8,128)(2,1)S(1)} collective-permute-done((bf16[3,1,128,384]{3,2,0,1:T(8,128)(2,1)}, bf16[3,1,128,384]{3,2,0,1:T(8,128)(2,1)S(1)}, u32[]{:S(2)}, u32[]{:S(2)}) %collective-permute-start.1) | collective-permute-done | bytes 294944 | tf_op jit(solution)/shard_map/ppermute | solution.py:11
  23.3 1.5 %select_maximum_fusion = bf16[5,3,130,384]{3,2,0,1:T(8,128)(2,1)S(1)} fusion(bf16[5,1,128,384]{3,2,0,1:T(8,128)(2,1)S(1)} %constant_dynamic-update-slice_fusion.2, bf16[5,1,128,384]{3,2,0,1:T(8,128)(2,1)S(1)} %constant_dynamic-update-slice_fusion, bf16[3,1,128,384]{3,2,0,1:T(8,128)(2,1)} %bitcast.190, bf16[2,1,128,384]{3,2,0,1:T(8,128)(2,1)S(1)} %collective-permute-done.2), kind=kLoop, calls=%fused_computation.3 | loop fusion | flops 11232000 | bytes 2972160 | tf_op jit(solution)/shard_map/concatenate | solution.py:88
  24.9 0.1 fusion.35
  25.1 0.1 fusion.33
  25.4 0.1 fusion.30
  25.6 0.1 fusion.27
  25.8 0.1 fusion.23
  26.0 0.1 fusion.20
  26.3 0.1 fusion.18
  26.5 0.1 fusion.16
  26.7 0.1 fusion.14
  26.8 0.2 slice-done
  27.0 1.4 %slice-done.1 = s8[3768320]{0:T(1024)(128)(4,1)S(1)} async-done(((s8[7962624]{0:T(1024)(128)(4,1)}), s8[3768320]{0:T(1024)(128)(4,1)S(1)}, s32[]{:S(2)}) %slice-start.1) | async-done | bytes 3768344
  28.4 4.3 %multiply_convert_fusion = bf16[3,128,384]{2,1,0:T(8,128)(2,1)S(1)} fusion(bf16[3,128,10368]{2,1,0:T(8,128)(2,1)S(1)} %fusion.14, bf16[10368,384,1]{1,0,2:T(8,128)(2,1)S(1)} %bitcast.197), kind=kOutput, calls=%fused_computation.10 | convolution fusion | flops 3058384896 | bytes 16220160 | tf_op jit(solution)/shard_map/dot_general | solution.py:100
  33.2 0.2 copy.14
  33.4 24.9 %all_to_all.10 = bf16[16,3,10,384]{3,1,2,0:T(4,128)(2,1)S(1)} all-to-all(bf16[16,3,10,384]{3,1,2,0:T(4,128)(2,1)S(1)} %copy.14), channel_id=1, replica_groups=mesh['group'=16,'frame'=48] {'group'}, dimensions={0} | all-to-all | bytes 737280 | tf_op jit(solution)/shard_map/all_to_all | solution.py:109
  58.4 46.5 %all_to_all.11 = bf16[48,10,384]{2,1,0:T(8,128)(2,1)S(1)} all-to-all(bf16[48,10,384]{2,1,0:T(8,128)(2,1)S(1)} %bitcast.194), channel_id=1, replica_groups=mesh['group'=16,'frame'=48] {'frame'}, dimensions={0} | all-to-all | bytes 737280 | tf_op jit(solution)/shard_map/all_to_all | solution.py:111
  104.9 0.1 fusion.40
  105.0 0.1 fusion.6
  105.2 0.1 fusion.7
  105.4 0.1 slice_dynamic-update-slice_fusion.1
  105.5 0.1 slice_dynamic-update-slice_fusion
  105.7 0.1 fusion.9
  105.9 0.1 fusion.10
  106.0 2.3 %fusion.4 = bf16[1,48,8,384]{3,2,1,0:T(8,128)(2,1)} fusion(bf16[48,8,3456]{2,1,0:T(8,128)(2,1)S(1)} %fusion.10, bf16[3456,384,1]{1,0,2:T(8,128)(2,1)S(1)} %bitcast.186), kind=kOutput, calls=%fused_computation.9 | convolution fusion | flops 1019363328 | bytes 5603328 | tf_op jit(solution)/shard_map/dot_general | solution.py:121
  (54 shorter events, 1.6 us)
Async XLA Ops:
  0.6 105.4 %copy-start = (bf16[3,3,384,384]{3,2,1,0:T(8,128)(2,1)S(1)}, bf16[3,3,384,384]{3,2,1,0:T(8,128)(2,1)}, u32[]{:S(2)}) copy-start(bf16[3,3,384,384]{3,2,1,0:T(8,128)(2,1)} %param.5) | copy-start | bytes 7962628
  0.6 24.4 %copy-start.1 = (bf16[3,1,128,384]{3,2,1,0:T(8,128)(2,1)S(1)}, bf16[3,1,128,384]{3,2,1,0:T(8,128)(2,1)}, u32[]{:S(2)}) copy-start(bf16[3,1,128,384]{3,2,1,0:T(8,128)(2,1)} %param.3) | copy-start | bytes 884740
  1.8 17.2 %collective-permute-start = (bf16[2,1,128,384]{3,2,0,1:T(8,128)(2,1)S(1)}, bf16[2,1,128,384]{3,2,0,1:T(8,128)(2,1)S(1)}, u32[]{:S(2)}, u32[]{:S(2)}) collective-permute-start(bf16[2,1,128,384]{3,2,0,1:T(8,128)(2,1)S(1)} %slice.245), channel_id=1, source_target_pairs={{0,49},{1,50},{2,51},{3,52},{4,53},{5,54},{6,55},{7,56},{8,57},{9,... | collective-permute-start | bytes 589832 | tf_op jit(solution)/shard_map/ppermute | solution.py:22
  8.2 10.8 %collective-permute-start.3 = (bf16[2,1,128,384]{3,2,0,1:T(8,128)(2,1)S(1)}, bf16[2,1,128,384]{3,2,0,1:T(8,128)(2,1)S(1)}, u32[]{:S(2)}, u32[]{:S(2)}) collective-permute-start(bf16[2,1,128,384]{3,2,0,1:T(8,128)(2,1)S(1)} %slice.245), channel_id=1, source_target_pairs={{1,48},{2,49},{3,50},{4,51},{5,52},{6,53},{7,54},{8,55},{9,56},{10... | collective-permute-start | bytes 589832 | tf_op jit(solution)/shard_map/ppermute | solution.py:22
  9.5 12.4 %collective-permute-start.4 = (bf16[3,1,128,384]{3,2,0,1:T(8,128)(2,1)}, bf16[3,1,128,384]{3,2,0,1:T(8,128)(2,1)S(1)}, u32[]{:S(2)}, u32[]{:S(2)}) collective-permute-start(bf16[3,1,128,384]{3,2,0,1:T(8,128)(2,1)} %bitcast.188), channel_id=1, source_target_pairs={{1,0},{2,1},{3,2},{4,3},{5,4},{6,5},{7,6},{8,7},{9,8},{10,9},{11,1... | collective-permute-start | bytes 884744 | tf_op jit(solution)/shard_map/ppermute | solution.py:11
  10.8 12.5 %collective-permute-start.2 = (bf16[2,1,128,384]{3,2,0,1:T(8,128)(2,1)S(1)}, bf16[2,1,128,384]{3,2,0,1:T(8,128)(2,1)S(1)}, u32[]{:S(2)}, u32[]{:S(2)}) collective-permute-start(bf16[2,1,128,384]{3,2,0,1:T(8,128)(2,1)S(1)} %slice.245), channel_id=1, source_target_pairs={{0,48},{48,96},{96,144},{144,192},{192,240},{240,288},{288,336},{3... | collective-permute-start | bytes 589832 | tf_op jit(solution)/shard_map/ppermute | solution.py:11
  12.7 10.5 %collective-permute-start.1 = (bf16[3,1,128,384]{3,2,0,1:T(8,128)(2,1)}, bf16[3,1,128,384]{3,2,0,1:T(8,128)(2,1)S(1)}, u32[]{:S(2)}, u32[]{:S(2)}) collective-permute-start(bf16[3,1,128,384]{3,2,0,1:T(8,128)(2,1)} %bitcast.189), channel_id=1, source_target_pairs={{0,1},{1,2},{2,3},{3,4},{4,5},{5,6},{6,7},{7,8},{8,9},{9,10},{10,1... | collective-permute-start | bytes 884744 | tf_op jit(solution)/shard_map/ppermute | solution.py:11
  24.8 2.2 %slice-start = ((s8[7962624]{0:T(1024)(128)(4,1)}), s8[4194304]{0:T(1024)(128)(4,1)S(1)}, s32[]{:S(2)}) async-start(s8[7962624]{0:T(1024)(128)(4,1)} %bitcast.195), calls=%async_computation.2 | async-start | bytes 8388608
  25.7 2.7 %slice-start.1 = ((s8[7962624]{0:T(1024)(128)(4,1)}), s8[3768320]{0:T(1024)(128)(4,1)S(1)}, s32[]{:S(2)}) async-start(s8[7962624]{0:T(1024)(128)(4,1)} %bitcast.195), calls=%async_computation.3 | async-start | bytes 7536640
  32.8 75.5 %copy-start.2 = (bf16[3,128,384]{2,1,0:T(8,128)(2,1)}, bf16[3,128,384]{2,1,0:T(8,128)(2,1)S(1)}, u32[]{:S(2)}) copy-start(bf16[3,128,384]{2,1,0:T(8,128)(2,1)S(1)} %multiply_convert_fusion) | copy-start | bytes 884740

commit v15 on v14

--- a/solution.py
+++ b/solution.py
@@ -80,11 +80,11 @@
 def shards(video, kernel3, kernel2):
     length, _, width, channels = video.shape
     groups = lax.axis_size("group")
-    cached = shifted(video[length - 2 :], "group", 1)
+    cached = shifted(video, "group", 1)[length - 2 :]
     above = shifted(video, "frame", 1)
     below = shifted(video, "frame", -1)
-    cached_above = diagonal(video[length - 2 :], 1, 1)
-    cached_below = diagonal(video[length - 2 :], 1, -1)
+    cached_above = diagonal(video, 1, 1)[length - 2 :]
+    cached_below = diagonal(video, 1, -1)[length - 2 :]
     rows = jnp.concatenate(
         [
             jnp.concatenate([cached_above, above], 0),

time: 109 us -> 111 us (1.018)
  waiting for transfers between devices: 4.2 us -> 6.52 us
  other arithmetic: 1.6 us -> 3.53 us
  local copies, waits for them, and re-layouts: 6.24 us -> 4.39 us
    ppermute x3, waiting for transfers between devices: 4.19 us -> 6.51 us  [shifted(): lax.ppermute(value, axis, [(source, source + steps) for source in range(f...]
    all_to_all x1, blocking collectives: 24.9 us -> 23.1 us  [shards(): pieces = lax.all_to_all(pieces, 'group', 0, 0, tiled=False)]
    all_to_all x1, blocking collectives: 46.5 us -> 48 us  [shards(): rows_all = lax.all_to_all(pieces, 'frame', 0, 0, tiled=True)]
    unnamed x3 -> x7, other arithmetic: 0.1 us -> 1.34 us
    unnamed x59 -> x53, local copies, waits for them, and re-layouts: 4.4 us -> 3.68 us
where the time goes in v15:
time: 111 us; the launch traced here: 110 us
  blocking collectives  71.1 us (64%)
  starting transfers between devices  17.2 us (15%)
  matrix products  6.6 us (6%)
  waiting for transfers between devices  6.52 us (6%)
  local copies, waits for them, and re-layouts  4.39 us (4%)
  other arithmetic  3.53 us (3%)
    all_to_all x1, blocking collectives, shards(): rows_all = lax.all_to_all(pieces, 'frame', 0, 0, tiled=True)  48 us
    all_to_all x1, blocking collectives, shards(): pieces = lax.all_to_all(pieces, 'group', 0, 0, tiled=False)  23.1 us
    ppermute x3, starting transfers between devices, shifted(): lax.ppermute(value, axis, [(source, source + steps) for source in range(f...  10.5 us
    ppermute x2, starting transfers between devices, diagonal(): return lax.ppermute(value, ('group', 'frame'), pairs)  6.69 us
    ppermute x3, waiting for transfers between devices, shifted(): lax.ppermute(value, axis, [(source, source + steps) for source in range(f...  6.51 us
    dot_general x1, matrix products, shards(): jnp.dot(lhs.reshape(length * width, 27 * channels), kernel3.reshape(27 *...  4.34 us
    unnamed x53, local copies, waits for them, and re-layouts  3.68 us
    dot_general x1, matrix products, shards(): jnp.dot(lhs.reshape(rows * (span - 2), 9 * channels), kernel2.reshape(9 *...  2.26 us
  transfers between devices with their start and end apart: 5, of which 2 were waited for; matrix products, arithmetic and copies ran while one was open for 0% of the time, Pallas kernels for 0%

profile of v15, /device:TPU:1, one launch (start us, length us, event | category | flops | bytes accessed | tf_op | source)
XLA Modules:
  0.0 110.4 jit_solution(3741448696388253752)
XLA Ops:
  0.7 1.6 %collective-permute-start.3 = (bf16[3,1,128,384]{3,2,0,1:T(8,128)(2,1)}, bf16[3,1,128,384]{3,2,0,1:T(8,128)(2,1)S(1)}, u32[]{:S(2)}, u32[]{:S(2)}) collective-permute-start(bf16[3,1,128,384]{3,2,0,1:T(8,128)(2,1)} %bitcast.189), channel_id=1, source_target_pairs={{1,48},{2,49},{3,50},{4,51},{5,52},{6,53},{7,54},{8,55},{9,56},{10... | collective-permute-start | bytes 884744 | tf_op jit(solution)/shard_map/ppermute | solution.py:22
  2.2 4.6 %collective-permute-start.2 = (bf16[3,1,128,384]{3,2,0,1:T(8,128)(2,1)}, bf16[3,1,128,384]{3,2,0,1:T(8,128)(2,1)S(1)}, u32[]{:S(2)}, u32[]{:S(2)}) collective-permute-start(bf16[3,1,128,384]{3,2,0,1:T(8,128)(2,1)} %bitcast.190), channel_id=1, source_target_pairs={{0,48},{48,96},{96,144},{144,192},{192,240},{240,288},{288,336},{3... | collective-permute-start | bytes 884744 | tf_op jit(solution)/shard_map/ppermute | solution.py:11
  6.8 5.1 %collective-permute-start = (bf16[3,1,128,384]{3,2,0,1:T(8,128)(2,1)}, bf16[3,1,128,384]{3,2,0,1:T(8,128)(2,1)S(1)}, u32[]{:S(2)}, u32[]{:S(2)}) collective-permute-start(bf16[3,1,128,384]{3,2,0,1:T(8,128)(2,1)} %bitcast.191), channel_id=1, source_target_pairs={{0,49},{1,50},{2,51},{3,52},{4,53},{5,54},{6,55},{7,56},{8,57},{9,... | collective-permute-start | bytes 884744 | tf_op jit(solution)/shard_map/ppermute | solution.py:22
  12.0 1.3 %collective-permute-start.4 = (bf16[3,1,128,384]{3,2,0,1:T(8,128)(2,1)}, bf16[3,1,128,384]{3,2,0,1:T(8,128)(2,1)S(1)}, u32[]{:S(2)}, u32[]{:S(2)}) collective-permute-start(bf16[3,1,128,384]{3,2,0,1:T(8,128)(2,1)} %bitcast.192), channel_id=1, source_target_pairs={{1,0},{2,1},{3,2},{4,3},{5,4},{6,5},{7,6},{8,7},{9,8},{10,9},{11,1... | collective-permute-start | bytes 884744 | tf_op jit(solution)/shard_map/ppermute | solution.py:11
  13.3 4.6 %collective-permute-start.1 = (bf16[3,1,128,384]{3,2,0,1:T(8,128)(2,1)}, bf16[3,1,128,384]{3,2,0,1:T(8,128)(2,1)S(1)}, u32[]{:S(2)}, u32[]{:S(2)}) collective-permute-start(bf16[3,1,128,384]{3,2,0,1:T(8,128)(2,1)} %bitcast.193), channel_id=1, source_target_pairs={{0,1},{1,2},{2,3},{3,4},{4,5},{5,6},{6,7},{7,8},{8,9},{9,10},{10,1... | collective-permute-start | bytes 884744 | tf_op jit(solution)/shard_map/ppermute | solution.py:11
  18.0 3.0 %collective-permute-done.4 = bf16[3,1,128,384]{3,2,0,1:T(8,128)(2,1)S(1)} collective-permute-done((bf16[3,1,128,384]{3,2,0,1:T(8,128)(2,1)}, bf16[3,1,128,384]{3,2,0,1:T(8,128)(2,1)S(1)}, u32[]{:S(2)}, u32[]{:S(2)}) %collective-permute-start.4) | collective-permute-done | bytes 294944 | tf_op jit(solution)/shard_map/ppermute | solution.py:11
  21.0 3.5 %collective-permute-done.1 = bf16[3,1,128,384]{3,2,0,1:T(8,128)(2,1)S(1)} collective-permute-done((bf16[3,1,128,384]{3,2,0,1:T(8,128)(2,1)}, bf16[3,1,128,384]{3,2,0,1:T(8,128)(2,1)S(1)}, u32[]{:S(2)}, u32[]{:S(2)}) %collective-permute-start.1) | collective-permute-done | bytes 294944 | tf_op jit(solution)/shard_map/ppermute | solution.py:11
  24.5 2.2 %fusion.1 = bf16[5,3,130,384]{3,2,0,1:T(8,128)(2,1)S(1)} fusion(bf16[3,1,128,384]{3,2,0,1:T(8,128)(2,1)S(1)} %collective-permute-done.4, bf16[2,1,128,384]{3,2,0,1:T(8,128)(2,1)S(1)} %slice.253, bf16[3,1,128,384]{3,2,0,1:T(8,128)(2,1)} %bitcast.194, bf16[2,1,128,384]{3,2,0,1:T(8,128)(2,1)S(1)} %slice.252, ...), kind=kLoop, calls=%fused_computation.4 | loop fusion | flops 15724800 | bytes 2972160 | tf_op jit(solution)/shard_map/concatenate | solution.py:88
  26.8 0.1 fusion.44
  27.0 1.1 fusion.18
  28.1 0.1 fusion.42
  28.3 0.1 fusion.40
  28.5 0.1 fusion.36
  28.8 0.1 fusion.32
  29.0 0.1 fusion.28
  29.2 0.1 fusion.26
  29.4 0.1 fusion.24
  29.7 0.1 fusion.22
  29.8 1.1 %slice-done.1 = s8[3768320]{0:T(1024)(128)(4,1)S(1)} async-done(((s8[7962624]{0:T(1024)(128)(4,1)}), s8[3768320]{0:T(1024)(128)(4,1)S(1)}, s32[]{:S(2)}) %slice-start.1) | async-done | bytes 3768344
  30.9 4.3 %multiply_convert_fusion = bf16[3,128,384]{2,1,0:T(8,128)(2,1)S(1)} fusion(bf16[3,128,10368]{2,1,0:T(8,128)(2,1)S(1)} %fusion.22, bf16[10368,384,1]{1,0,2:T(8,128)(2,1)S(1)} %bitcast.201), kind=kOutput, calls=%fused_computation.12 | convolution fusion | flops 3058384896 | bytes 16220160 | tf_op jit(solution)/shard_map/dot_general | solution.py:100
  35.7 0.2 copy.18
  35.9 23.1 %all_to_all.10 = bf16[16,3,10,384]{3,1,2,0:T(4,128)(2,1)S(1)} all-to-all(bf16[16,3,10,384]{3,1,2,0:T(4,128)(2,1)S(1)} %copy.18), channel_id=1, replica_groups=mesh['group'=16,'frame'=48] {'group'}, dimensions={0} | all-to-all | bytes 737280 | tf_op jit(solution)/shard_map/all_to_all | solution.py:109
  59.0 0.1 copy.19
  59.1 48.0 %all_to_all.11 = bf16[48,10,384]{2,1,0:T(8,128)(2,1)S(1)} all-to-all(bf16[48,10,384]{2,1,0:T(8,128)(2,1)S(1)} %bitcast.198), channel_id=1, replica_groups=mesh['group'=16,'frame'=48] {'frame'}, dimensions={0} | all-to-all | bytes 737280 | tf_op jit(solution)/shard_map/all_to_all | solution.py:111
  107.1 0.1 fusion.48
  107.2 0.1 fusion.8
  107.4 0.1 fusion.9
  107.6 0.1 slice_dynamic-update-slice_fusion.1
  107.7 0.1 slice_dynamic-update-slice_fusion
  107.9 0.1 fusion.11
  108.0 0.1 fusion.12
  108.2 2.3 %fusion.6 = bf16[1,48,8,384]{3,2,1,0:T(8,128)(2,1)} fusion(bf16[48,8,3456]{2,1,0:T(8,128)(2,1)S(1)} %fusion.12, bf16[3456,384,1]{1,0,2:T(8,128)(2,1)S(1)} %bitcast.188), kind=kOutput, calls=%fused_computation.11 | convolution fusion | flops 1019363328 | bytes 5603328 | tf_op jit(solution)/shard_map/dot_general | solution.py:121
  (52 shorter events, 1.4 us)
Async XLA Ops:
  0.6 107.5 %copy-start = (bf16[3,3,384,384]{3,2,1,0:T(8,128)(2,1)S(1)}, bf16[3,3,384,384]{3,2,1,0:T(8,128)(2,1)}, u32[]{:S(2)}) copy-start(bf16[3,3,384,384]{3,2,1,0:T(8,128)(2,1)} %param.5) | copy-start | bytes 7962628
  0.6 28.1 %copy-start.1 = (bf16[3,1,128,384]{3,2,1,0:T(8,128)(2,1)S(1)}, bf16[3,1,128,384]{3,2,1,0:T(8,128)(2,1)}, u32[]{:S(2)}) copy-start(bf16[3,1,128,384]{3,2,1,0:T(8,128)(2,1)} %param.3) | copy-start | bytes 884740
  0.7 17.3 %collective-permute-start.3 = (bf16[3,1,128,384]{3,2,0,1:T(8,128)(2,1)}, bf16[3,1,128,384]{3,2,0,1:T(8,128)(2,1)S(1)}, u32[]{:S(2)}, u32[]{:S(2)}) collective-permute-start(bf16[3,1,128,384]{3,2,0,1:T(8,128)(2,1)} %bitcast.189), channel_id=1, source_target_pairs={{1,48},{2,49},{3,50},{4,51},{5,52},{6,53},{7,54},{8,55},{9,56},{10... | collective-permute-start | bytes 884744 | tf_op jit(solution)/shard_map/ppermute | solution.py:22
  2.2 15.7 %collective-permute-start.2 = (bf16[3,1,128,384]{3,2,0,1:T(8,128)(2,1)}, bf16[3,1,128,384]{3,2,0,1:T(8,128)(2,1)S(1)}, u32[]{:S(2)}, u32[]{:S(2)}) collective-permute-start(bf16[3,1,128,384]{3,2,0,1:T(8,128)(2,1)} %bitcast.190), channel_id=1, source_target_pairs={{0,48},{48,96},{96,144},{144,192},{192,240},{240,288},{288,336},{3... | collective-permute-start | bytes 884744 | tf_op jit(solution)/shard_map/ppermute | solution.py:11
  6.8 11.2 %collective-permute-start = (bf16[3,1,128,384]{3,2,0,1:T(8,128)(2,1)}, bf16[3,1,128,384]{3,2,0,1:T(8,128)(2,1)S(1)}, u32[]{:S(2)}, u32[]{:S(2)}) collective-permute-start(bf16[3,1,128,384]{3,2,0,1:T(8,128)(2,1)} %bitcast.191), channel_id=1, source_target_pairs={{0,49},{1,50},{2,51},{3,52},{4,53},{5,54},{6,55},{7,56},{8,57},{9,... | collective-permute-start | bytes 884744 | tf_op jit(solution)/shard_map/ppermute | solution.py:22
  12.0 9.1 %collective-permute-start.4 = (bf16[3,1,128,384]{3,2,0,1:T(8,128)(2,1)}, bf16[3,1,128,384]{3,2,0,1:T(8,128)(2,1)S(1)}, u32[]{:S(2)}, u32[]{:S(2)}) collective-permute-start(bf16[3,1,128,384]{3,2,0,1:T(8,128)(2,1)} %bitcast.192), channel_id=1, source_target_pairs={{1,0},{2,1},{3,2},{4,3},{5,4},{6,5},{7,6},{8,7},{9,8},{10,9},{11,1... | collective-permute-start | bytes 884744 | tf_op jit(solution)/shard_map/ppermute | solution.py:11
  13.3 11.3 %collective-permute-start.1 = (bf16[3,1,128,384]{3,2,0,1:T(8,128)(2,1)}, bf16[3,1,128,384]{3,2,0,1:T(8,128)(2,1)S(1)}, u32[]{:S(2)}, u32[]{:S(2)}) collective-permute-start(bf16[3,1,128,384]{3,2,0,1:T(8,128)(2,1)} %bitcast.193), channel_id=1, source_target_pairs={{0,1},{1,2},{2,3},{3,4},{4,5},{5,6},{6,7},{7,8},{8,9},{9,10},{10,1... | collective-permute-start | bytes 884744 | tf_op jit(solution)/shard_map/ppermute | solution.py:11
  26.8 2.9 %slice-start = ((s8[7962624]{0:T(1024)(128)(4,1)}), s8[4194304]{0:T(1024)(128)(4,1)S(1)}, s32[]{:S(2)}) async-start(s8[7962624]{0:T(1024)(128)(4,1)} %bitcast.199), calls=%async_computation.2 | async-start | bytes 8388608
  28.8 2.1 %slice-start.1 = ((s8[7962624]{0:T(1024)(128)(4,1)}), s8[3768320]{0:T(1024)(128)(4,1)S(1)}, s32[]{:S(2)}) async-start(s8[7962624]{0:T(1024)(128)(4,1)} %bitcast.199), calls=%async_computation.3 | async-start | bytes 7536640
  35.3 75.2 %copy-start.2 = (bf16[3,128,384]{2,1,0:T(8,128)(2,1)}, bf16[3,128,384]{2,1,0:T(8,128)(2,1)S(1)}, u32[]{:S(2)}) copy-start(bf16[3,128,384]{2,1,0:T(8,128)(2,1)S(1)} %multiply_convert_fusion) | copy-start | bytes 884740

commit v16 on v14

--- a/solution.py
+++ b/solution.py
@@ -93,9 +93,13 @@
         ],
         1,
     )
-    padded = jnp.pad(rows, ((0, 0), (0, 0), (1, 1), (0, 0)))
+    shifts = [
+        jnp.pad(rows[:, :, : width - 1], ((0, 0), (0, 0), (1, 0), (0, 0))),
+        rows,
+        jnp.pad(rows[:, :, 1:], ((0, 0), (0, 0), (0, 1), (0, 0))),
+    ]
     lhs = jnp.concatenate(
-        [padded[a : a + length, b, c : c + width] for a in range(3) for b in range(3) for c in range(3)], axis=-1
+        [shifts[c][a : a + length, b] for a in range(3) for b in range(3) for c in range(3)], axis=-1
     )
     conv = jnp.dot(
         lhs.reshape(length * width, 27 * channels),

time: 109 us -> 110 us (level)
  local copies, waits for them, and re-layouts: 6.24 us -> 7.99 us
where the time goes in v16:
time: 110 us
  blocking collectives  71.4 us (65%)
  starting transfers between devices  17.1 us (16%)
  local copies, waits for them, and re-layouts  7.99 us (7%)
  matrix products  6.6 us (6%)
  waiting for transfers between devices  4.19 us (4%)
  other arithmetic  1.27 us (1%)
  between operations  1.1 us (1%)
    all_to_all x1, blocking collectives, shards(): rows_all = lax.all_to_all(pieces, 'frame', 0, 0, tiled=True)  46.5 us
    all_to_all x1, blocking collectives, shards(): pieces = lax.all_to_all(pieces, 'group', 0, 0, tiled=False)  24.9 us
    ppermute x3, starting transfers between devices, shifted(): lax.ppermute(value, axis, [(source, source + steps) for source in range(f...  9.41 us
    ppermute x2, starting transfers between devices, diagonal(): return lax.ppermute(value, ('group', 'frame'), pairs)  7.7 us
    unnamed x59, local copies, waits for them, and re-layouts  5.4 us
    dot_general x1, matrix products, shards(): jnp.dot(lhs.reshape(length * width, 27 * channels), kernel3.reshape(27 *...  4.34 us
    ppermute x3, waiting for transfers between devices, shifted(): lax.ppermute(value, axis, [(source, source + steps) for source in range(f...  4.18 us
    dot_general x1, matrix products, shards(): jnp.dot(lhs.reshape(rows * (span - 2), 9 * channels), kernel2.reshape(9 *...  2.26 us
  transfers between devices with their start and end apart: 5, of which 2 were waited for; matrix products, arithmetic and copies ran while one was open for 0% of the time, Pallas kernels for 0%

profile of v16, /device:TPU:1, one launch (start us, length us, event | category | flops | bytes accessed | tf_op | source)
XLA Modules:
  0.0 109.7 jit_solution(934133403481403912)
XLA Ops:
  0.6 1.1 %slice.232 = bf16[2,1,128,384]{3,2,0,1:T(8,128)(2,1)S(1)} slice(bf16[3,1,128,384]{3,2,0,1:T(8,128)(2,1)} %bitcast.151), slice={[1:3], [0:1], [0:128], [0:384]} | slice | bytes 393216 | tf_op jit(solution)/shard_map/slice | solution.py:86
  1.7 6.4 %collective-permute-start = (bf16[2,1,128,384]{3,2,0,1:T(8,128)(2,1)S(1)}, bf16[2,1,128,384]{3,2,0,1:T(8,128)(2,1)S(1)}, u32[]{:S(2)}, u32[]{:S(2)}) collective-permute-start(bf16[2,1,128,384]{3,2,0,1:T(8,128)(2,1)S(1)} %slice.232), channel_id=1, source_target_pairs={{0,49},{1,50},{2,51},{3,52},{4,53},{5,54},{6,55},{7,56},{8,57},{9,... | collective-permute-start | bytes 589832 | tf_op jit(solution)/shard_map/ppermute | solution.py:22
  8.2 1.3 %collective-permute-start.3 = (bf16[2,1,128,384]{3,2,0,1:T(8,128)(2,1)S(1)}, bf16[2,1,128,384]{3,2,0,1:T(8,128)(2,1)S(1)}, u32[]{:S(2)}, u32[]{:S(2)}) collective-permute-start(bf16[2,1,128,384]{3,2,0,1:T(8,128)(2,1)S(1)} %slice.232), channel_id=1, source_target_pairs={{1,48},{2,49},{3,50},{4,51},{5,52},{6,53},{7,54},{8,55},{9,56},{10... | collective-permute-start | bytes 589832 | tf_op jit(solution)/shard_map/ppermute | solution.py:22
  9.5 1.3 %collective-permute-start.4 = (bf16[3,1,128,384]{3,2,0,1:T(8,128)(2,1)}, bf16[3,1,128,384]{3,2,0,1:T(8,128)(2,1)S(1)}, u32[]{:S(2)}, u32[]{:S(2)}) collective-permute-start(bf16[3,1,128,384]{3,2,0,1:T(8,128)(2,1)} %bitcast.152), channel_id=1, source_target_pairs={{1,0},{2,1},{3,2},{4,3},{5,4},{6,5},{7,6},{8,7},{9,8},{10,9},{11,1... | collective-permute-start | bytes 884744 | tf_op jit(solution)/shard_map/ppermute | solution.py:11
  10.8 1.9 %collective-permute-start.2 = (bf16[2,1,128,384]{3,2,0,1:T(8,128)(2,1)S(1)}, bf16[2,1,128,384]{3,2,0,1:T(8,128)(2,1)S(1)}, u32[]{:S(2)}, u32[]{:S(2)}) collective-permute-start(bf16[2,1,128,384]{3,2,0,1:T(8,128)(2,1)S(1)} %slice.232), channel_id=1, source_target_pairs={{0,48},{48,96},{96,144},{144,192},{192,240},{240,288},{288,336},{3... | collective-permute-start | bytes 589832 | tf_op jit(solution)/shard_map/ppermute | solution.py:11
  12.7 6.2 %collective-permute-start.1 = (bf16[3,1,128,384]{3,2,0,1:T(8,128)(2,1)}, bf16[3,1,128,384]{3,2,0,1:T(8,128)(2,1)S(1)}, u32[]{:S(2)}, u32[]{:S(2)}) collective-permute-start(bf16[3,1,128,384]{3,2,0,1:T(8,128)(2,1)} %bitcast.153), channel_id=1, source_target_pairs={{0,1},{1,2},{2,3},{3,4},{4,5},{5,6},{6,7},{7,8},{8,9},{9,10},{10,1... | collective-permute-start | bytes 884744 | tf_op jit(solution)/shard_map/ppermute | solution.py:11
  19.0 2.8 %collective-permute-done.4 = bf16[3,1,128,384]{3,2,0,1:T(8,128)(2,1)S(1)} collective-permute-done((bf16[3,1,128,384]{3,2,0,1:T(8,128)(2,1)}, bf16[3,1,128,384]{3,2,0,1:T(8,128)(2,1)S(1)}, u32[]{:S(2)}, u32[]{:S(2)}) %collective-permute-start.4) | collective-permute-done | bytes 294944 | tf_op jit(solution)/shard_map/ppermute | solution.py:11
  21.9 1.3 %collective-permute-done.1 = bf16[3,1,128,384]{3,2,0,1:T(8,128)(2,1)S(1)} collective-permute-done((bf16[3,1,128,384]{3,2,0,1:T(8,128)(2,1)}, bf16[3,1,128,384]{3,2,0,1:T(8,128)(2,1)S(1)}, u32[]{:S(2)}, u32[]{:S(2)}) %collective-permute-start.1) | collective-permute-done | bytes 294944 | tf_op jit(solution)/shard_map/ppermute | solution.py:11
  23.3 1.2 %pad_maximum_fusion = bf16[5,3,128,384]{3,2,0,1:T(8,128)(2,1)S(1)} fusion(bf16[5,1,128,384]{3,2,0,1:T(8,128)(2,1)S(1)} %constant_dynamic-update-slice_fusion.2, bf16[3,1,128,384]{3,2,0,1:T(8,128)(2,1)} %bitcast.154, bf16[2,1,128,384]{3,2,0,1:T(8,128)(2,1)S(1)} %collective-permute-done.2, bf16[5,1,128,384]{3,2,0,1:T(8,128)(2,1)S(1)} %constant_dynamic-update-slice_fusion), kind=kLoop, calls=%fused_computation | loop fusion | flops 2211840 | bytes 2949120 | tf_op jit(solution)/shard_map/concatenate | solution.py:88
  24.5 0.8 fusion.18
  25.5 0.1 bitcast_dynamic-update-slice_fusion.18
  25.7 0.1 bitcast_dynamic-update-slice_fusion.16
  25.9 0.1 bitcast_dynamic-update-slice_fusion.14
  26.1 0.1 bitcast_dynamic-update-slice_fusion.12
  26.4 0.1 bitcast_dynamic-update-slice_fusion.10
  26.6 0.1 bitcast_dynamic-update-slice_fusion.8
  26.8 0.1 bitcast_dynamic-update-slice_fusion.5
  27.0 0.1 bitcast_dynamic-update-slice_fusion.2
  27.3 1.3 %slice-done = s8[4194304]{0:T(1024)(128)(4,1)S(1)} async-done(((s8[7962624]{0:T(1024)(128)(4,1)}), s8[4194304]{0:T(1024)(128)(4,1)S(1)}, s32[]{:S(2)}) %slice-start) | async-done | bytes 4194328
  28.5 1.3 %slice-done.1 = s8[3768320]{0:T(1024)(128)(4,1)S(1)} async-done(((s8[7962624]{0:T(1024)(128)(4,1)}), s8[3768320]{0:T(1024)(128)(4,1)S(1)}, s32[]{:S(2)}) %slice-start.1) | async-done | bytes 3768344
  29.8 4.3 %multiply_convert_fusion = bf16[3,128,384]{2,1,0:T(8,128)(2,1)S(1)} fusion(bf16[3,128,10368]{2,1,0:T(8,128)(2,1)S(1)} %bitcast_dynamic-update-slice_fusion, bf16[10368,384,1]{1,0,2:T(8,128)(2,1)S(1)} %bitcast.161), kind=kOutput, calls=%fused_computation.3 | convolution fusion | flops 3058384896 | bytes 16220160 | tf_op jit(solution)/shard_map/dot_general | solution.py:104
  34.6 0.2 copy.14
  34.8 24.9 %all_to_all.10 = bf16[16,3,10,384]{3,1,2,0:T(4,128)(2,1)S(1)} all-to-all(bf16[16,3,10,384]{3,1,2,0:T(4,128)(2,1)S(1)} %copy.14), channel_id=1, replica_groups=mesh['group'=16,'frame'=48] {'group'}, dimensions={0} | all-to-all | bytes 737280 | tf_op jit(solution)/shard_map/all_to_all | solution.py:113
  59.8 46.5 %all_to_all.11 = bf16[48,10,384]{2,1,0:T(8,128)(2,1)S(1)} all-to-all(bf16[48,10,384]{2,1,0:T(8,128)(2,1)S(1)} %bitcast.158), channel_id=1, replica_groups=mesh['group'=16,'frame'=48] {'frame'}, dimensions={0} | all-to-all | bytes 737280 | tf_op jit(solution)/shard_map/all_to_all | solution.py:115
  106.3 0.1 fusion.19
  106.4 0.1 fusion.2
  106.6 0.1 fusion.3
  106.8 0.1 slice_dynamic-update-slice_fusion.1
  106.9 0.1 slice_dynamic-update-slice_fusion
  107.1 0.1 fusion.5
  107.3 0.1 fusion.6
  107.4 2.3 %fusion = bf16[1,48,8,384]{3,2,1,0:T(8,128)(2,1)} fusion(bf16[48,8,3456]{2,1,0:T(8,128)(2,1)S(1)} %fusion.6, bf16[3456,384,1]{1,0,2:T(8,128)(2,1)S(1)} %bitcast.150), kind=kOutput, calls=%fused_computation.2 | convolution fusion | flops 1019363328 | bytes 5603328 | tf_op jit(solution)/shard_map/dot_general | solution.py:125
  (55 shorter events, 1.7 us)
Async XLA Ops:
  0.6 106.8 %copy-start = (bf16[3,3,384,384]{3,2,1,0:T(8,128)(2,1)S(1)}, bf16[3,3,384,384]{3,2,1,0:T(8,128)(2,1)}, u32[]{:S(2)}) copy-start(bf16[3,3,384,384]{3,2,1,0:T(8,128)(2,1)} %param.5) | copy-start | bytes 7962628
  1.7 17.2 %collective-permute-start = (bf16[2,1,128,384]{3,2,0,1:T(8,128)(2,1)S(1)}, bf16[2,1,128,384]{3,2,0,1:T(8,128)(2,1)S(1)}, u32[]{:S(2)}, u32[]{:S(2)}) collective-permute-start(bf16[2,1,128,384]{3,2,0,1:T(8,128)(2,1)S(1)} %slice.232), channel_id=1, source_target_pairs={{0,49},{1,50},{2,51},{3,52},{4,53},{5,54},{6,55},{7,56},{8,57},{9,... | collective-permute-start | bytes 589832 | tf_op jit(solution)/shard_map/ppermute | solution.py:22
  8.2 10.8 %collective-permute-start.3 = (bf16[2,1,128,384]{3,2,0,1:T(8,128)(2,1)S(1)}, bf16[2,1,128,384]{3,2,0,1:T(8,128)(2,1)S(1)}, u32[]{:S(2)}, u32[]{:S(2)}) collective-permute-start(bf16[2,1,128,384]{3,2,0,1:T(8,128)(2,1)S(1)} %slice.232), channel_id=1, source_target_pairs={{1,48},{2,49},{3,50},{4,51},{5,52},{6,53},{7,54},{8,55},{9,56},{10... | collective-permute-start | bytes 589832 | tf_op jit(solution)/shard_map/ppermute | solution.py:22
  9.5 12.4 %collective-permute-start.4 = (bf16[3,1,128,384]{3,2,0,1:T(8,128)(2,1)}, bf16[3,1,128,384]{3,2,0,1:T(8,128)(2,1)S(1)}, u32[]{:S(2)}, u32[]{:S(2)}) collective-permute-start(bf16[3,1,128,384]{3,2,0,1:T(8,128)(2,1)} %bitcast.152), channel_id=1, source_target_pairs={{1,0},{2,1},{3,2},{4,3},{5,4},{6,5},{7,6},{8,7},{9,8},{10,9},{11,1... | collective-permute-start | bytes 884744 | tf_op jit(solution)/shard_map/ppermute | solution.py:11
  10.8 12.5 %collective-permute-start.2 = (bf16[2,1,128,384]{3,2,0,1:T(8,128)(2,1)S(1)}, bf16[2,1,128,384]{3,2,0,1:T(8,128)(2,1)S(1)}, u32[]{:S(2)}, u32[]{:S(2)}) collective-permute-start(bf16[2,1,128,384]{3,2,0,1:T(8,128)(2,1)S(1)} %slice.232), channel_id=1, source_target_pairs={{0,48},{48,96},{96,144},{144,192},{192,240},{240,288},{288,336},{3... | collective-permute-start | bytes 589832 | tf_op jit(solution)/shard_map/ppermute | solution.py:11
  12.7 10.5 %collective-permute-start.1 = (bf16[3,1,128,384]{3,2,0,1:T(8,128)(2,1)}, bf16[3,1,128,384]{3,2,0,1:T(8,128)(2,1)S(1)}, u32[]{:S(2)}, u32[]{:S(2)}) collective-permute-start(bf16[3,1,128,384]{3,2,0,1:T(8,128)(2,1)} %bitcast.153), channel_id=1, source_target_pairs={{0,1},{1,2},{2,3},{3,4},{4,5},{5,6},{6,7},{7,8},{8,9},{9,10},{10,1... | collective-permute-start | bytes 884744 | tf_op jit(solution)/shard_map/ppermute | solution.py:11
  19.0 6.6 %copy-start.1 = (bf16[3,1,128,384]{3,2,1,0:T(8,128)(2,1)S(1)}, bf16[3,1,128,384]{3,2,1,0:T(8,128)(2,1)}, u32[]{:S(2)}) copy-start(bf16[3,1,128,384]{3,2,1,0:T(8,128)(2,1)} %param.3) | copy-start | bytes 884740
  26.4 2.2 %slice-start = ((s8[7962624]{0:T(1024)(128)(4,1)}), s8[4194304]{0:T(1024)(128)(4,1)S(1)}, s32[]{:S(2)}) async-start(s8[7962624]{0:T(1024)(128)(4,1)} %bitcast.159), calls=%async_computation.2 | async-start | bytes 8388608
  26.8 3.0 %slice-start.1 = ((s8[7962624]{0:T(1024)(128)(4,1)}), s8[3768320]{0:T(1024)(128)(4,1)S(1)}, s32[]{:S(2)}) async-start(s8[7962624]{0:T(1024)(128)(4,1)} %bitcast.159), calls=%async_computation.3 | async-start | bytes 7536640
  34.2 75.5 %copy-start.2 = (bf16[3,128,384]{2,1,0:T(8,128)(2,1)}, bf16[3,128,384]{2,1,0:T(8,128)(2,1)S(1)}, u32[]{:S(2)}) copy-start(bf16[3,128,384]{2,1,0:T(8,128)(2,1)S(1)} %multiply_convert_fusion) | copy-start | bytes 884740
